TPU v7x, 512 devices: a whole 4x4x16 slice. The times are simulated.
512 devices in a mesh: half: 2 (over core), cls: 64 (over z, x), vol: 4 (over y).
Axes of the slice: x: 4, y: 4, z: 16, core: 2. Of those that a mesh axis runs over, the one named last changes fastest.
Arguments:
- images: bfloat16 [16384, 16384], P(('half', 'cls'), 'vol')
- groups: int32 [16384, 1], P(('half', 'cls')), may hold values from 0 to 63; in each aligned block of 128 rows (0 to 127, 128 to 255, ...) at most 4 rows name the same one
- references: bfloat16 [2048, 16384], P('cls', 'vol'), may hold values from -0.046875 to 0.046875
- interp_index: int32 [2048, 16384], P('cls', 'vol'), may hold values from 0 to 2047
- shell_index: int32 [4, 262144], P('vol', ('half', 'cls')), may hold values from 0 to 127
Outputs:
- volume: float32 [4, 262144], P('vol', ('half', 'cls'))
- shell_fsc: float32 [128], replicated
Inputs may be any that keep to these rules, and one draw needn't show every extreme that they name: `groups`: within each aligned block of 128 particles no group appears more than 4 times, a bound that some block reaches.
All inputs are finite; a program needn't handle non-finite values.
Results may differ from a plain program's by a relative error of at most 0.00041.
Values may be sent and summed in bfloat16 or wider, within the bound.
No kernel may reach another device: no remote copies, remote signals or barrier semaphores. Data moves between devices by JAX's collectives and lax.ppermute only.
A program may use at most 64 MiB of HBM per device.

v0:
```python
import jax
import jax.numpy as jnp
from jax import lax
from jax.sharding import PartitionSpec as P

IMG = 128
SHIFTS = 5
NSHELL = 128
PLANES = 4
VBOX = 256
VOXS = 262144


EPS_W = 1e-05
EPS_F = 1e-06


def partner(shard, axis, apart):
    return lax.ppermute(shard, axis, [(i, i ^ 1 << apart) for i in range(lax.axis_size(axis))])


def shards(images, groups, references, interp_index, shell_index):
    n_cls = lax.axis_size("cls")
    n_vol = lax.axis_size("vol")
    n_half = lax.axis_size("half")
    part_count, pix_quarter = images.shape
    class_count = references.shape[0]
    capacity = max(2 * part_count // n_cls, 4)
    slot_count = n_cls * capacity
    owner_ids = groups[:, 0]
    matches = (owner_ids[:, None] == jnp.arange(n_cls, dtype=jnp.int32)[None, :]).astype(jnp.int32)
    order_in = jnp.sum(jnp.cumsum(matches, axis=0) * matches, axis=1) - 1
    slot_ids = owner_ids * capacity + order_in
    slot_hits = slot_ids[None, :] == jnp.arange(slot_count, dtype=jnp.int32)[:, None]
    source_ids = jnp.sum(
        jnp.where(slot_hits, jnp.arange(part_count, dtype=jnp.int32)[None, :], 0), axis=1
    )
    filled = jnp.any(slot_hits, axis=1)
    outgoing = jnp.where(
        filled[:, None], jnp.take(images, source_ids, axis=0), jnp.zeros((), jnp.bfloat16)
    )
    arrived = lax.all_to_all(
        outgoing.reshape(n_cls, capacity, pix_quarter),
        "cls",
        split_axis=0,
        concat_axis=0,
        tiled=True,
    )
    arrived = arrived.reshape(slot_count, pix_quarter)
    quarter_rows = pix_quarter // IMG
    shaped_refs = references.reshape(class_count, quarter_rows, IMG)
    rolled_refs = jnp.concatenate(
        [
            jnp.roll(shaped_refs, -(shift_id - SHIFTS // 2), axis=2).reshape(
                class_count, pix_quarter
            )
            for shift_id in range(SHIFTS)
        ],
        axis=0,
    )
    partial_scores = lax.dot_general(
        arrived, rolled_refs, (((1,), (1,)), ((), ())), preferred_element_type=jnp.float32
    )
    partial_scores = partial_scores.reshape(slot_count, SHIFTS, class_count)
    scores = lax.psum(partial_scores, "vol")
    squares = scores * scores
    mean_square = jnp.mean(squares, axis=(1, 2), keepdims=True)
    weights = (squares / (mean_square + EPS_W)).astype(jnp.bfloat16)
    weighted = lax.dot_general(
        weights.reshape(slot_count, SHIFTS * class_count),
        arrived,
        (((0,), (0,)), ((), ())),
        preferred_element_type=jnp.float32,
    )
    weighted = weighted.reshape(SHIFTS, class_count, quarter_rows, IMG)
    aligned = jnp.roll(weighted[0], -(SHIFTS // 2), axis=2)
    for shift_id in range(1, SHIFTS):
        aligned = aligned + jnp.roll(weighted[shift_id], shift_id - SHIFTS // 2, axis=2)
    column_ids = jnp.arange(pix_quarter, dtype=jnp.int32) % IMG
    placed = interp_index + 2 * VBOX * PLANES * column_ids[None, :]
    slab_part = jax.ops.segment_sum(aligned.reshape(-1), placed.reshape(-1), num_segments=VOXS)
    piece_len = VOXS // (n_half * n_cls)
    slab_part = jnp.transpose(slab_part.reshape(n_half, n_cls, piece_len), (1, 0, 2)).reshape(-1)
    block_len = VOXS // n_cls
    slab_full = lax.psum(slab_part, "cls")
    own_block = lax.dynamic_slice_in_dim(slab_full, lax.axis_index("cls") * block_len, block_len)
    half_id = lax.axis_index("half")
    own_piece = lax.dynamic_slice_in_dim(own_block, half_id * piece_len, piece_len)
    other_piece = lax.dynamic_slice_in_dim(own_block, (1 - half_id) * piece_len, piece_len)
    mirror_piece = partner(other_piece, "half", 0)
    first = jnp.where(half_id == 0, own_piece, mirror_piece)
    second = jnp.where(half_id == 0, mirror_piece, own_piece)
    shell_hot = (shell_index[0][:, None] == jnp.arange(NSHELL, dtype=jnp.int32)[None, :]).astype(
        jnp.float32
    )
    stats = jnp.stack([first * first, second * second, first * second])
    shell_terms = jnp.dot(stats, shell_hot, precision=lax.Precision.HIGHEST)
    shell_sums = lax.psum(shell_terms, ("half", "cls", "vol"))
    shell_fsc = shell_sums[2] / (jnp.sqrt(shell_sums[0]) * jnp.sqrt(shell_sums[1]) + EPS_F)
    mean_sq = (jnp.sum(shell_sums[0]) + jnp.sum(shell_sums[1]) + 2.0 * jnp.sum(shell_sums[2])) / (
        4.0 * n_vol * VOXS
    )
    filter_vox = jnp.dot(shell_hot, shell_fsc, precision=lax.Precision.HIGHEST)
    volume = filter_vox * (0.5 * (first + second)) / jnp.sqrt(mean_sq + EPS_F)
    return (volume[None, :], shell_fsc)


def solution(mesh):
    placed = (
        P(("half", "cls"), "vol"),
        P(("half", "cls"), None),
        P("cls", "vol"),
        P("cls", "vol"),
        P("vol", ("half", "cls")),
    )
    return jax.shard_map(
        shards,
        mesh=mesh,
        in_specs=placed,
        out_specs=(P("vol", ("half", "cls")), P()),
        check_vma=False,
    )
```

profile of v0, /device:TPU:6, one launch (start us, length us, event | category | flops | bytes accessed | tf_op | source)
XLA Modules:
  0.0 1275.6 jit_solution(14044876211775641448)
XLA Ops:
  7.2 0.8 fusion.7
  8.0 0.2 reduce_window_sum.11
  8.2 0.8 select_reduce_fusion.1
  9.0 0.7 add_add_fusion.1
  9.7 0.1 select_reduce_fusion
  9.8 0.1 fusion.6
  9.9 0.1 reduce_sum.60
  10.1 1.8 gather_fusion
  11.9 2.2 gather.7
  14.2 0.1 broadcast_in_dim.51
  14.3 3.7 select_select_fusion
  18.0 18.7 %all-to-all-start = ((bf16[64,4,4096]{2,1,0:T(4,128)(2,1)}), bf16[64,4,4096]{2,1,0:T(4,128)(2,1)S(1)}, u32[]{:S(2)}, u32[]{:S(2)}) async-start(bf16[64,4,4096]{2,1,0:T(4,128)(2,1)} %select_select_fusion), calls=%async_computation | async-start | bytes 4194304 | tf_op jit(solution)/shard_map/all_to_all | solution.py:42
  36.8 0.0 all-reduce.3.cloned.1.call-start
  36.9 0.1 fusion.21
  37.0 0.1 fusion.22
  37.2 0.3 pad_maximum_fusion.2
  37.5 0.1 fusion.23
  37.6 0.1 fusion.24
  37.8 0.3 pad_maximum_fusion.3
  38.1 0.8 bitcast_dynamic-update-slice_fusion.3
  38.9 0.8 bitcast_dynamic-update-slice_fusion.2
  39.7 0.7 constant_dynamic-update-slice_fusion
  40.4 0.8 bitcast_dynamic-update-slice_fusion.1
  41.2 0.8 bitcast_dynamic-update-slice_fusion
  42.0 94.9 %all-to-all-done = bf16[64,4,4096]{2,1,0:T(4,128)(2,1)S(1)} async-done(((bf16[64,4,4096]{2,1,0:T(4,128)(2,1)}), bf16[64,4,4096]{2,1,0:T(4,128)(2,1)S(1)}, u32[]{:S(2)}, u32[]{:S(2)}) %all-to-all-start) | async-done | bytes 2097184 | tf_op jit(solution)/shard_map/all_to_all | solution.py:42
  136.9 2.1 reshape.142
  139.0 3.5 fusion.25
  142.4 0.0 all-reduce.3.cloned.1.call-update
  142.5 0.0 all-reduce.5.cloned.1.call-start
  142.5 1.1 add_bitcast_fusion
  143.6 0.9 copy.9
  144.5 2.1 reshape.116
  146.6 44.8 %all-reduce.3.cloned.1.call-done = f32[256,5,32]{0,2,1:T(8,128)} async-done(((f32[256,5,32]{0,2,1:T(8,128)}), f32[256,5,32]{0,2,1:T(8,128)}) %all-reduce.3.cloned.1.call-update) | async-done | bytes 163856 | tf_op jit(solution)/shard_map/psum | solution.py:65
  191.4 1.0 multiply_reduce_fusion
  192.3 0.9 divide_convert_fusion
  193.3 2.1 fusion.26
  195.4 0.2 slice_bitcast_fusion.2
  195.6 0.1 copy.15
  195.7 0.2 slice.131
  195.9 0.1 copy.16
  196.0 0.2 slice.134
  196.2 0.1 copy.18
  196.3 0.2 slice.138
  196.5 0.1 copy.19
  196.6 0.2 slice.141
  196.8 0.1 copy.17
  196.9 0.2 pad_maximum_fusion
  197.2 0.2 pad_maximum_fusion.1
  197.4 0.3 maximum_add_fusion
  197.7 0.1 add_add_fusion
  197.8 683.3 %scatter_custom_fusion = f32[262144]{0:T(1024)S(1)} fusion(s32[131072]{0:T(1024)} %bitcast.88, f32[131072]{0:T(1024)S(1)} %add_add_fusion, f32[]{:T(128)} %constant.70.clone.1), kind=kCustom, calls=%fused_computation.17 | custom fusion | flops 131072 | bytes 1049088 | tf_op jit(solution)/shard_map/scatter-add | solution.py:81
  881.1 0.2 reshape.123
  881.3 0.8 copy.26
  882.1 1.1 copy.20
  883.2 275.0 %all-reduce.5.cloned.1.call-done = f32[262144]{0:T(1024)} async-done(((f32[262144]{0:T(1024)}), f32[262144]{0:T(1024)}) %all-reduce.5.cloned.1.call-update) | async-done | bytes 1048592 | tf_op jit(solution)/shard_map/psum | solution.py:85
  1158.2 0.8 dynamic_slice.14
  1159.0 1.9 collective-permute-start
  1160.9 1.1 collective-permute-done
  1162.1 0.8 fusion.20
  1162.9 0.6 fusion.1
  1163.4 101.3 %psum.23 = f32[3,128]{1,0:T(4,128)S(1)} all-reduce(f32[3,128]{1,0:T(4,128)S(1)} %fusion.1), channel_id=1, replica_groups=mesh['half'=2,'cls'=64,'vol'=4] {'half','cls','vol'}, use_global_device_ids=true, to_apply=%region_8.9 | all-reduce | flops 384 | bytes 3072 | tf_op jit(solution)/shard_map/psum | solution.py:98
  1264.8 0.7 slice_reduce_fusion.2
  1267.4 0.7 fusion
  1268.1 0.6 multiply_divide_fusion
  (16 shorter events, 0.1 us)
Async XLA Ops:
  7.2 2.9 copy-start
  18.0 18.8 %copy-start.1 = (bf16[32,4096]{1,0:T(8,128)(2,1)S(1)}, bf16[32,4096]{1,0:T(8,128)(2,1)}, u32[]{:S(2)}) copy-start(bf16[32,4096]{1,0:T(8,128)(2,1)} %param.7) | copy-start | bytes 786436
  18.0 118.9 %all-to-all-start = ((bf16[64,4,4096]{2,1,0:T(4,128)(2,1)}), bf16[64,4,4096]{2,1,0:T(4,128)(2,1)S(1)}, u32[]{:S(2)}, u32[]{:S(2)}) async-start(bf16[64,4,4096]{2,1,0:T(4,128)(2,1)} %select_select_fusion), calls=%async_computation | async-start | bytes 4194304 | tf_op jit(solution)/shard_map/all_to_all | solution.py:42
  36.8 154.6 %all-reduce.3.cloned.1.call-start = ((), (), s32[]{:S(2)}) async-start(), calls=%async_computation.1 | async-start | bytes 327680 | tf_op jit(solution)/shard_map/psum | solution.py:65
  142.5 1015.8 %all-reduce.5.cloned.1.call-start = ((), (), s32[]{:S(2)}) async-start(), calls=%async_computation.2 | async-start | bytes 2097152 | tf_op jit(solution)/shard_map/psum | solution.py:85
  882.1 280.8 %copy-start.3 = (s32[1,2048]{1,0:T(1,128)S(1)}, s32[1,2048]{1,0:T(1,128)}, u32[]{:S(2)}) copy-start(s32[1,2048]{1,0:T(1,128)} %param.9) | copy-start | bytes 24580
  1159.0 3.1 collective-permute-start
  1265.5 3.3 copy-start.2
Sparse Core Ops, SparseCore 0:
  142.6 48.7 all-reduce.2
  883.4 274.8 all-reduce.4
where the time goes:
time: 1280 us
  other arithmetic  696 us (54%)
  waiting for transfers between devices  416 us (32%)
  blocking collectives  101 us (8%)
  starting transfers between devices  20.7 us (2%)
  local copies, waits for them, and re-layouts  18.2 us (1%)
  between operations  16.3 us (1%)
    scatter-add x1, other arithmetic, shards(): jax.ops.segment_sum(aligned.reshape(-1), placed.reshape(-1), num_segments...  683 us
    psum x1, waiting for transfers between devices, shards(): slab_full = lax.psum(slab_part, 'cls')  275 us
    psum x1, blocking collectives, shards(): shell_sums = lax.psum(shell_terms, ('half', 'cls', 'vol'))  101 us
    all_to_all x1, waiting for transfers between devices, shards(): lax.all_to_all(outgoing.reshape(n_cls, capacity, pix_quarter), 'cls', spl...  94.9 us
    psum x1, waiting for transfers between devices, shards(): scores = lax.psum(partial_scores, 'vol')  44.8 us
  transfers between devices with their start and end apart: 4, of which 4 were waited for; matrix products, arithmetic and copies ran while one was open for 1% of the time, Pallas kernels for 0%

commit v1 on v0

--- a/solution.py
+++ b/solution.py
@@ -1,6 +1,10 @@
+import functools
+
 import jax
 import jax.numpy as jnp
 from jax import lax
+from jax.experimental import pallas as pl
+from jax.experimental.pallas import tpu as pltpu
 from jax.sharding import PartitionSpec as P
 
 IMG = 128
@@ -14,9 +18,56 @@
 EPS_W = 1e-05
 EPS_F = 1e-06
 
+LO = 128
+Q_BLOCK = 16
+
 
 def partner(shard, axis, apart):
     return lax.ppermute(shard, axis, [(i, i ^ 1 << apart) for i in range(lax.axis_size(axis))])
+
+
+def _project_kernel(val_ref, idx_ref, out_ref):
+    n = val_ref.shape[1]
+    hi_count = out_ref.shape[1]
+    lo_iota = lax.broadcasted_iota(jnp.int32, (LO, n), 0)
+    hi_iota = lax.broadcasted_iota(jnp.int32, (hi_count, n), 0)
+
+    def body(q, carry):
+        v = val_ref[pl.ds(q, 1), :]
+        idx = idx_ref[pl.ds(q, 1), :]
+        lo = jnp.bitwise_and(idx, LO - 1)
+        hi = jnp.right_shift(idx, 7)
+        rt = jnp.where(lo == lo_iota, 1.0, 0.0).astype(jnp.bfloat16)
+        vh = v.astype(jnp.bfloat16)
+        vl = (v - vh.astype(jnp.float32)).astype(jnp.bfloat16)
+        mask = hi == hi_iota
+        zero = jnp.zeros((), jnp.bfloat16)
+        lt = jnp.concatenate([jnp.where(mask, vh, zero), jnp.where(mask, vl, zero)], axis=0)
+        o = lax.dot_general(lt, rt, (((1,), (1,)), ((), ())), preferred_element_type=jnp.float32)
+        out_ref[q] = o[:hi_count] + o[hi_count:]
+        return carry
+
+    lax.fori_loop(0, val_ref.shape[0], body, 0)
+
+
+def project(val_t, idx_t, bins):
+    q_count, n = val_t.shape
+    hi_count = bins // LO
+    return pl.pallas_call(
+        _project_kernel,
+        out_shape=jax.ShapeDtypeStruct((q_count, hi_count, LO), jnp.float32),
+        grid=(q_count // Q_BLOCK,),
+        in_specs=[
+            pl.BlockSpec((Q_BLOCK, n), lambda i: (i, 0)),
+            pl.BlockSpec((Q_BLOCK, n), lambda i: (i, 0)),
+        ],
+        out_specs=pl.BlockSpec((Q_BLOCK, hi_count, LO), lambda i: (i, 0, 0)),
+        cost_estimate=pl.CostEstimate(
+            flops=2 * q_count * 2 * hi_count * LO * n,
+            bytes_accessed=q_count * n * 8 + q_count * bins * 4,
+            transcendentals=0,
+        ),
+    )(val_t, idx_t)
 
 
 def shards(images, groups, references, interp_index, shell_index):
@@ -48,6 +99,10 @@
     )
     arrived = arrived.reshape(slot_count, pix_quarter)
     quarter_rows = pix_quarter // IMG
+    bins = VOXS // IMG
+    piece_rows = IMG // n_half
+    idx_t = interp_index.reshape(class_count * quarter_rows, IMG).T
+    idx_t = idx_t.reshape(n_half, piece_rows, -1).transpose(1, 0, 2).reshape(IMG, -1)
     shaped_refs = references.reshape(class_count, quarter_rows, IMG)
     rolled_refs = jnp.concatenate(
         [
@@ -76,17 +131,16 @@
     aligned = jnp.roll(weighted[0], -(SHIFTS // 2), axis=2)
     for shift_id in range(1, SHIFTS):
         aligned = aligned + jnp.roll(weighted[shift_id], shift_id - SHIFTS // 2, axis=2)
-    column_ids = jnp.arange(pix_quarter, dtype=jnp.int32) % IMG
-    placed = interp_index + 2 * VBOX * PLANES * column_ids[None, :]
-    slab_part = jax.ops.segment_sum(aligned.reshape(-1), placed.reshape(-1), num_segments=VOXS)
+    val_t = aligned.reshape(class_count * quarter_rows, IMG).T
+    val_t = val_t.reshape(n_half, piece_rows, -1).transpose(1, 0, 2).reshape(IMG, -1)
+    slab_part = project(val_t, idx_t, bins)
     piece_len = VOXS // (n_half * n_cls)
-    slab_part = jnp.transpose(slab_part.reshape(n_half, n_cls, piece_len), (1, 0, 2)).reshape(-1)
-    block_len = VOXS // n_cls
-    slab_full = lax.psum(slab_part, "cls")
-    own_block = lax.dynamic_slice_in_dim(slab_full, lax.axis_index("cls") * block_len, block_len)
+    slab_part = slab_part.reshape(n_cls, n_half * piece_len)
+    own_block = lax.psum_scatter(slab_part, "cls", scatter_dimension=0, tiled=True)
+    own_block = own_block.reshape(n_half, piece_len)
     half_id = lax.axis_index("half")
-    own_piece = lax.dynamic_slice_in_dim(own_block, half_id * piece_len, piece_len)
-    other_piece = lax.dynamic_slice_in_dim(own_block, (1 - half_id) * piece_len, piece_len)
+    own_piece = jnp.where(half_id == 0, own_block[0], own_block[1])
+    other_piece = jnp.where(half_id == 0, own_block[1], own_block[0])
     mirror_piece = partner(other_piece, "half", 0)
     first = jnp.where(half_id == 0, own_piece, mirror_piece)
     second = jnp.where(half_id == 0, mirror_piece, own_piece)

time: 1280 us -> 634 us (0.50)
  other arithmetic: 696 us -> 15 us
  Pallas kernels: 0 us -> 27.8 us
  local copies, waits for them, and re-layouts: 18.2 us -> 35.3 us
    scatter-add x1 -> x0, other arithmetic: 683 us -> none  [shards(): jax.ops.segment_sum(aligned.reshape(-1), placed.reshape(-1), num_segments...]
    psum x1 -> x0, waiting for transfers between devices: 275 us -> none  [shards(): slab_full = lax.psum(slab_part, 'cls')]
    unnamed x2 -> x3, waiting for transfers between devices: 0.03 us -> 274 us
    pallas_call x0 -> x1, Pallas kernels: none -> 27.8 us  [project(): pl.pallas_call(_project_kernel, out_shape=jax.ShapeDtypeStruct((q_count,...]
  transfers between devices with their start and end apart: 4 -> 4, of which waited for: 4 -> 4; matrix products, arithmetic and copies ran while one was open for 1% -> 3% of each run, Pallas kernels for 0% -> 0%
where the time goes in v1:
time: 634 us; the launch traced here: 631 us
  waiting for transfers between devices  408 us (64%)
  blocking collectives  101 us (16%)
  local copies, waits for them, and re-layouts  35.3 us (6%)
  Pallas kernels  27.8 us (4%)
  starting transfers between devices  20.7 us (3%)
  between operations  16.2 us (3%)
  other arithmetic  15 us (2%)
  matrix products  6.86 us (1%)
    unnamed x3, waiting for transfers between devices  274 us
    psum x1, blocking collectives, shards(): shell_sums = lax.psum(shell_terms, ('half', 'cls', 'vol'))  101 us
    all_to_all x1, waiting for transfers between devices, shards(): lax.all_to_all(outgoing.reshape(n_cls, capacity, pix_quarter), 'cls', spl...  94.9 us
    psum x1, waiting for transfers between devices, shards(): scores = lax.psum(partial_scores, 'vol')  38.3 us
    pallas_call x1, Pallas kernels, project(): pl.pallas_call(_project_kernel, out_shape=jax.ShapeDtypeStruct((q_count,...  27.8 us
    all_to_all x1, starting transfers between devices, shards(): lax.all_to_all(outgoing.reshape(n_cls, capacity, pix_quarter), 'cls', spl...  18.7 us
  transfers between devices with their start and end apart: 4, of which 4 were waited for; matrix products, arithmetic and copies ran while one was open for 3% of the time, Pallas kernels for 0%

profile of v1, /device:TPU:6, one launch (start us, length us, event | category | flops | bytes accessed | tf_op | source)
XLA Modules:
  0.0 631.4 jit_solution(12281063352032240056)
XLA Ops:
  7.2 0.8 fusion.9
  8.0 0.2 reduce_window_sum.11
  8.2 0.8 select_reduce_fusion.1
  9.0 0.7 add_add_fusion
  9.7 0.1 select_reduce_fusion
  9.8 0.1 fusion.8
  9.9 0.1 reduce_sum.60
  10.1 1.8 gather_fusion
  11.9 2.2 gather.7
  14.2 0.1 broadcast_in_dim.46
  14.3 3.7 select_select_fusion
  18.0 18.7 %all-to-all-start = ((bf16[64,4,4096]{2,1,0:T(4,128)(2,1)}), bf16[64,4,4096]{2,1,0:T(4,128)(2,1)S(1)}, u32[]{:S(2)}, u32[]{:S(2)}) async-start(bf16[64,4,4096]{2,1,0:T(4,128)(2,1)} %select_select_fusion), calls=%async_computation | async-start | bytes 4194304 | tf_op jit(solution)/shard_map/all_to_all | solution.py:93
  36.8 0.0 all-reduce.4.cloned.1.call-start
  36.9 0.1 fusion.19
  37.0 0.1 fusion.20
  37.2 0.3 pad_maximum_fusion
  37.5 0.1 fusion.21
  37.6 0.1 fusion.22
  37.8 0.3 pad_maximum_fusion.1
  38.1 0.8 bitcast_dynamic-update-slice_fusion.3
  38.9 0.8 bitcast_dynamic-update-slice_fusion.2
  39.7 0.7 constant_dynamic-update-slice_fusion
  40.4 0.8 bitcast_dynamic-update-slice_fusion.1
  41.2 0.8 bitcast_dynamic-update-slice_fusion
  42.0 94.9 %all-to-all-done = bf16[64,4,4096]{2,1,0:T(4,128)(2,1)S(1)} async-done(((bf16[64,4,4096]{2,1,0:T(4,128)(2,1)}), bf16[64,4,4096]{2,1,0:T(4,128)(2,1)S(1)}, u32[]{:S(2)}, u32[]{:S(2)}) %all-to-all-start) | async-done | bytes 2097184 | tf_op jit(solution)/shard_map/all_to_all | solution.py:93
  136.9 2.1 reshape.150
  139.0 3.5 fusion.23
  142.4 0.0 all-reduce.4.cloned.1.call-update
  142.5 0.0 all-reduce.6.cloned.1.call-start
  142.5 1.9 reshape.138
  144.5 2.0 copy.34
  146.5 2.3 copy.35
  148.7 2.2 reshape.140.idx_ref
  150.9 2.1 reshape.129
  153.0 38.3 %all-reduce.4.cloned.1.call-done = f32[256,5,32]{0,2,1:T(8,128)} async-done(((f32[256,5,32]{0,2,1:T(8,128)}), f32[256,5,32]{0,2,1:T(8,128)}) %all-reduce.4.cloned.1.call-update) | async-done | bytes 163856 | tf_op jit(solution)/shard_map/psum | solution.py:120
  191.3 1.0 multiply_reduce_fusion
  192.3 0.9 divide_convert_fusion
  193.2 2.1 fusion.24
  195.4 1.0 slice_bitcast_fusion
  196.4 0.1 copy.43
  196.5 1.0 slice.150
  197.5 0.1 copy.44
  197.6 1.0 slice.153
  198.6 0.1 copy.41
  198.7 1.0 slice.143
  199.7 0.1 copy.42
  199.8 1.0 slice.146
  200.8 1.9 squeeze.15
  202.7 3.1 fusion.5
  205.8 1.2 copy.32
  207.0 0.4 copy.33
  207.5 1.2 reshape.137.val_ref
  208.6 27.8 %shard_map.68 = f32[128,16,128]{2,1,0:T(8,128)} custom-call(f32[128,1024]{1,0:T(8,128)} %reshape.137.val_ref, s32[128,1024]{1,0:T(8,128)} %reshape.140.idx_ref), custom_call_target="tpu_custom_call" | custom-call | flops 1073741824 | bytes 2097152 | tf_op jit(solution)/shard_map/pallas_call | solution.py:56
  236.4 2.5 reshape.141
  238.9 1.3 dynamic-slice
  240.2 273.7 %all-reduce.6.cloned.1.call-done = f32[64,4096]{1,0:T(8,128)} async-done(((f32[64,4096]{1,0:T(8,128)}), f32[64,4096]{1,0:T(8,128)}) %all-reduce.6.cloned.1.call-update) | async-done | bytes 1048592
  513.9 1.6 broadcast_select_fusion
  515.5 1.9 collective-permute-start
  517.5 1.1 collective-permute-done
  518.6 0.6 fusion.1
  519.2 101.3 %psum.15 = f32[3,128]{1,0:T(4,128)S(1)} all-reduce(f32[3,128]{1,0:T(4,128)S(1)} %fusion.1), channel_id=1, replica_groups=mesh['half'=2,'cls'=64,'vol'=4] {'half','cls','vol'}, use_global_device_ids=true, to_apply=%region_7.8 | all-reduce | flops 384 | bytes 3072 | tf_op jit(solution)/shard_map/psum | solution.py:152
  620.5 0.7 slice_reduce_fusion.2
  623.2 0.7 fusion
  623.9 0.6 multiply_divide_fusion
  (16 shorter events, 0.1 us)
Async XLA Ops:
  7.2 2.9 copy-start
  18.0 18.8 %copy-start.1 = (bf16[32,4096]{1,0:T(8,128)(2,1)S(1)}, bf16[32,4096]{1,0:T(8,128)(2,1)}, u32[]{:S(2)}) copy-start(bf16[32,4096]{1,0:T(8,128)(2,1)} %param.7) | copy-start | bytes 786436
  18.0 118.9 %all-to-all-start = ((bf16[64,4,4096]{2,1,0:T(4,128)(2,1)}), bf16[64,4,4096]{2,1,0:T(4,128)(2,1)S(1)}, u32[]{:S(2)}, u32[]{:S(2)}) async-start(bf16[64,4,4096]{2,1,0:T(4,128)(2,1)} %select_select_fusion), calls=%async_computation | async-start | bytes 4194304 | tf_op jit(solution)/shard_map/all_to_all | solution.py:93
  36.8 154.6 %all-reduce.4.cloned.1.call-start = ((), (), s32[]{:S(2)}) async-start(), calls=%async_computation.1 | async-start | bytes 327680 | tf_op jit(solution)/shard_map/psum | solution.py:120
  142.5 371.4 %all-reduce.6.cloned.1.call-start = ((), (), s32[]{:S(2)}) async-start(), calls=%async_computation.2 | async-start | bytes 2097152
  236.4 282.2 %copy-start.3 = (s32[1,2048]{1,0:T(1,128)S(1)}, s32[1,2048]{1,0:T(1,128)}, u32[]{:S(2)}) copy-start(s32[1,2048]{1,0:T(1,128)} %param.9) | copy-start | bytes 24580
  515.5 3.1 collective-permute-start
  621.2 3.3 copy-start.2
Sparse Core Ops, SparseCore 0:
  142.6 48.7 all-reduce.3
  239.1 274.8 all-reduce.5

commit v2 on v1

--- a/solution.py
+++ b/solution.py
@@ -24,6 +24,34 @@
 
 def partner(shard, axis, apart):
     return lax.ppermute(shard, axis, [(i, i ^ 1 << apart) for i in range(lax.axis_size(axis))])
+
+
+def butterfly_sum(x, axis):
+    for bit in range(lax.axis_size(axis).bit_length() - 1):
+        x = x + partner(x, axis, bit)
+    return x
+
+
+def halving_order(bits):
+    if bits == 6:
+        return [0, 2, 1, 3, 4, 5]
+    return list(range(bits))
+
+
+def reduce_scatter(x, axis):
+    n = lax.axis_size(axis)
+    bits = n.bit_length() - 1
+    me = lax.axis_index(axis)
+    remaining = list(range(bits - 1, -1, -1))
+    data = x.reshape([2] * bits + [x.shape[1]])
+    for bit in halving_order(bits):
+        ax = remaining.index(bit)
+        mine = jnp.right_shift(me, bit) & 1
+        keep = lax.dynamic_index_in_dim(data, mine, axis=ax, keepdims=False)
+        send = lax.dynamic_index_in_dim(data, 1 - mine, axis=ax, keepdims=False)
+        data = keep + partner(send, axis, bit)
+        remaining.remove(bit)
+    return data
 
 
 def _project_kernel(val_ref, idx_ref, out_ref):
@@ -117,7 +145,7 @@
         arrived, rolled_refs, (((1,), (1,)), ((), ())), preferred_element_type=jnp.float32
     )
     partial_scores = partial_scores.reshape(slot_count, SHIFTS, class_count)
-    scores = lax.psum(partial_scores, "vol")
+    scores = butterfly_sum(partial_scores, "vol")
     squares = scores * scores
     mean_square = jnp.mean(squares, axis=(1, 2), keepdims=True)
     weights = (squares / (mean_square + EPS_W)).astype(jnp.bfloat16)
@@ -136,7 +164,7 @@
     slab_part = project(val_t, idx_t, bins)
     piece_len = VOXS // (n_half * n_cls)
     slab_part = slab_part.reshape(n_cls, n_half * piece_len)
-    own_block = lax.psum_scatter(slab_part, "cls", scatter_dimension=0, tiled=True)
+    own_block = reduce_scatter(slab_part, "cls")
     own_block = own_block.reshape(n_half, piece_len)
     half_id = lax.axis_index("half")
     own_piece = jnp.where(half_id == 0, own_block[0], own_block[1])
@@ -149,7 +177,7 @@
     )
     stats = jnp.stack([first * first, second * second, first * second])
     shell_terms = jnp.dot(stats, shell_hot, precision=lax.Precision.HIGHEST)
-    shell_sums = lax.psum(shell_terms, ("half", "cls", "vol"))
+    shell_sums = butterfly_sum(butterfly_sum(butterfly_sum(shell_terms, "half"), "vol"), "cls")
     shell_fsc = shell_sums[2] / (jnp.sqrt(shell_sums[0]) * jnp.sqrt(shell_sums[1]) + EPS_F)
     mean_sq = (jnp.sum(shell_sums[0]) + jnp.sum(shell_sums[1]) + 2.0 * jnp.sum(shell_sums[2])) / (
         4.0 * n_vol * VOXS

time: 634 us -> 340 us (0.54)
  waiting for transfers between devices: 408 us -> 187 us
  blocking collectives: 101 us -> 0 us
  starting transfers between devices: 20.7 us -> 66.6 us
  between operations: 16.2 us -> 3.09 us
    unnamed x3 -> x0, waiting for transfers between devices: 274 us -> none
    psum x1 -> x0, blocking collectives: 101 us -> none  [shards(): shell_sums = lax.psum(shell_terms, ('half', 'cls', 'vol'))]
    ppermute x1 -> x18, waiting for transfers between devices: 1.14 us -> 92.3 us  [partner(): lax.ppermute(shard, axis, [(i, i ^ 1 << apart) for i in range(lax.axis_si...]
    ppermute x1 -> x18, starting transfers between devices: 1.92 us -> 47.9 us  [partner(): lax.ppermute(shard, axis, [(i, i ^ 1 << apart) for i in range(lax.axis_si...]
    psum x1 -> x0, waiting for transfers between devices: 38.3 us -> none  [shards(): scores = lax.psum(partial_scores, 'vol')]
  transfers between devices with their start and end apart: 4 -> 19, of which waited for: 4 -> 18; matrix products, arithmetic and copies ran while one was open for 3% -> 5% of each run, Pallas kernels for 0% -> 0%
where the time goes in v2:
time: 340 us; the launch traced here: 339 us
  waiting for transfers between devices  187 us (55%)
  starting transfers between devices  66.6 us (20%)
  local copies, waits for them, and re-layouts  35.4 us (10%)
  Pallas kernels  27.8 us (8%)
  other arithmetic  12.5 us (4%)
  matrix products  6.18 us (2%)
    all_to_all x1, waiting for transfers between devices, shards(): lax.all_to_all(outgoing.reshape(n_cls, capacity, pix_quarter), 'cls', spl...  95 us
    ppermute x18, waiting for transfers between devices, partner(): lax.ppermute(shard, axis, [(i, i ^ 1 << apart) for i in range(lax.axis_si...  92.3 us
    ppermute x18, starting transfers between devices, partner(): lax.ppermute(shard, axis, [(i, i ^ 1 << apart) for i in range(lax.axis_si...  47.9 us
    pallas_call x1, Pallas kernels, project(): pl.pallas_call(_project_kernel, out_shape=jax.ShapeDtypeStruct((q_count,...  27.8 us
    all_to_all x1, starting transfers between devices, shards(): lax.all_to_all(outgoing.reshape(n_cls, capacity, pix_quarter), 'cls', spl...  18.7 us
  transfers between devices with their start and end apart: 19, of which 18 were waited for; matrix products, arithmetic and copies ran while one was open for 5% of the time, Pallas kernels for 0%

profile of v2, /device:TPU:6, one launch (start us, length us, event | category | flops | bytes accessed | tf_op | source)
XLA Modules:
  0.0 338.9 jit_solution(3458294228535546117)
XLA Ops:
  0.6 0.8 fusion.9
  1.6 0.8 select_reduce_fusion.1
  3.5 1.8 gather_fusion
  5.4 2.2 gather.7
  7.7 3.7 %select_select_fusion = bf16[64,4,4096]{2,1,0:T(4,128)(2,1)} fusion(bf16[64,4,4096]{2,1,0:T(4,128)(2,1)} %gather.7, pred[64,4]{1,0:T(8,128)(4,1)S(1)} %compare_and_fusion, pred[64,4]{1,0:T(8,128)(4,1)S(1)} %broadcast_in_dim.46), kind=kLoop, calls=%fused_computation.1 | loop fusion | flops 2097152 | bytes 4194816 | tf_op jit(solution)/shard_map/jit(_where)/select_n | solution.py:118
  11.4 18.7 %all-to-all-start = ((bf16[64,4,4096]{2,1,0:T(4,128)(2,1)}), bf16[64,4,4096]{2,1,0:T(4,128)(2,1)S(1)}, u32[]{:S(2)}, u32[]{:S(2)}) async-start(bf16[64,4,4096]{2,1,0:T(4,128)(2,1)} %select_select_fusion), calls=%async_computation | async-start | bytes 4194304 | tf_op jit(solution)/shard_map/all_to_all | solution.py:121
  31.4 0.8 bitcast_dynamic-update-slice_fusion.3
  33.7 0.8 bitcast_dynamic-update-slice_fusion.1
  35.3 95.0 %all-to-all-done = bf16[64,4,4096]{2,1,0:T(4,128)(2,1)S(1)} async-done(((bf16[64,4,4096]{2,1,0:T(4,128)(2,1)}), bf16[64,4,4096]{2,1,0:T(4,128)(2,1)S(1)}, u32[]{:S(2)}, u32[]{:S(2)}) %all-to-all-start) | async-done | bytes 2097184 | tf_op jit(solution)/shard_map/all_to_all | solution.py:121
  130.3 2.0 reshape.142
  132.3 2.8 fusion.24
  135.1 3.5 %collective-permute-start = (f32[256,5,32]{0,2,1:T(8,128)S(1)}, f32[256,5,32]{0,2,1:T(8,128)S(1)}, u32[]{:S(2)}, u32[]{:S(2)}) collective-permute-start(f32[256,5,32]{0,2,1:T(8,128)S(1)} %fusion.24), channel_id=1, source_target_pairs={{0,1},{1,0},{2,3},{3,2},{4,5},{5,4},{6,7},{7,6},{8,9},{9,8},{10,11... | collective-permute-start | bytes 491528 | tf_op jit(solution)/shard_map/ppermute | solution.py:26
  138.6 3.7 %collective-permute-done = f32[256,5,32]{0,2,1:T(8,128)S(1)} collective-permute-done((f32[256,5,32]{0,2,1:T(8,128)S(1)}, f32[256,5,32]{0,2,1:T(8,128)S(1)}, u32[]{:S(2)}, u32[]{:S(2)}) %collective-permute-start) | collective-permute-done | bytes 163872 | tf_op jit(solution)/shard_map/ppermute | solution.py:26
  142.4 5.3 %collective-permute-start.1 = (f32[256,5,32]{0,2,1:T(8,128)S(1)}, f32[256,5,32]{0,2,1:T(8,128)S(1)}, u32[]{:S(2)}, u32[]{:S(2)}) collective-permute-start(f32[256,5,32]{0,2,1:T(8,128)S(1)} %add.184), channel_id=1, source_target_pairs={{0,2},{1,3},{2,0},{3,1},{4,6},{5,7},{6,4},{7,5},{8,10},{9,11},{10,... | collective-permute-start | bytes 491528 | tf_op jit(solution)/shard_map/ppermute | solution.py:26
  147.7 1.9 reshape.131
  149.6 2.0 copy.28
  151.6 2.2 copy.29
  153.9 2.2 reshape.133.idx_ref
  156.1 2.0 reshape.122
  158.2 2.1 fusion.25
  160.3 1.0 slice_bitcast_fusion
  161.4 1.0 slice.150
  162.6 1.0 slice.153
  163.7 1.0 slice.143
  164.8 1.0 slice.146
  165.8 1.9 squeeze.73
  167.7 3.1 fusion.5
  170.8 1.2 copy.26
  172.4 1.2 reshape.130.val_ref
  173.6 27.8 %shard_map.68 = f32[128,16,128]{2,1,0:T(8,128)} custom-call(f32[128,1024]{1,0:T(8,128)} %reshape.130.val_ref, s32[128,1024]{1,0:T(8,128)} %reshape.133.idx_ref), custom_call_target="tpu_custom_call" | custom-call | flops 1073741824 | bytes 2097152 | tf_op jit(solution)/shard_map/pallas_call | solution.py:84
  201.4 1.8 reshape_reshape.3
  203.2 1.1 constant_dynamic-slice_fusion.8
  204.7 3.2 collective-permute-start.2
  208.0 9.7 %collective-permute-done.2 = f32[2,2,2,2,2,4096]{5,4,3,2,1,0:T(2,128)S(1)} collective-permute-done((f32[2,2,2,2,2,4096]{5,4,3,2,1,0:T(2,128)S(1)}, f32[2,2,2,2,2,4096]{5,4,3,2,1,0:T(2,128)S(1)}, u32[]{:S(2)}, u32[]{:S(2)}) %collective-permute-start.2) | collective-permute-done | bytes 524320 | tf_op jit(solution)/shard_map/ppermute | solution.py:26
  218.3 2.6 collective-permute-start.3
  221.0 5.6 %collective-permute-done.3 = f32[2,2,2,2,4096]{4,3,2,1,0:T(2,128)S(1)} collective-permute-done((f32[2,2,2,2,4096]{4,3,2,1,0:T(2,128)S(1)}, f32[2,2,2,2,4096]{4,3,2,1,0:T(2,128)S(1)}, u32[]{:S(2)}, u32[]{:S(2)}) %collective-permute-start.3) | collective-permute-done | bytes 262176 | tf_op jit(solution)/shard_map/ppermute | solution.py:26
  227.1 1.9 collective-permute-start.4
  229.1 6.4 %collective-permute-done.4 = f32[2,2,2,4096]{3,2,1,0:T(2,128)S(1)} collective-permute-done((f32[2,2,2,4096]{3,2,1,0:T(2,128)S(1)}, f32[2,2,2,4096]{3,2,1,0:T(2,128)S(1)}, u32[]{:S(2)}, u32[]{:S(2)}) %collective-permute-start.4) | collective-permute-done | bytes 131104 | tf_op jit(solution)/shard_map/ppermute | solution.py:26
  235.8 1.9 collective-permute-start.5
  237.8 5.8 %collective-permute-done.5 = f32[2,2,4096]{2,1,0:T(2,128)S(1)} collective-permute-done((f32[2,2,4096]{2,1,0:T(2,128)S(1)}, f32[2,2,4096]{2,1,0:T(2,128)S(1)}, u32[]{:S(2)}, u32[]{:S(2)}) %collective-permute-start.5) | collective-permute-done | bytes 65568 | tf_op jit(solution)/shard_map/ppermute | solution.py:26
  243.8 2.2 collective-permute-start.6
  246.0 7.5 %collective-permute-done.6 = f32[2,4096]{1,0:T(2,128)S(1)} collective-permute-done((f32[2,4096]{1,0:T(2,128)S(1)}, f32[2,4096]{1,0:T(2,128)S(1)}, u32[]{:S(2)}, u32[]{:S(2)}) %collective-permute-start.6) | collective-permute-done | bytes 32800 | tf_op jit(solution)/shard_map/ppermute | solution.py:26
  253.6 3.6 %collective-permute-start.7 = (f32[4096]{0:T(1024)S(1)}, f32[4096]{0:T(1024)S(1)}, u32[]{:S(2)}, u32[]{:S(2)}) collective-permute-start(f32[4096]{0:T(1024)S(1)} %bitcast.123), channel_id=1, source_target_pairs={{0,128},{4,132},{8,136},{12,140},{16,144},{20,148},{24,152},{28,15... | collective-permute-start | bytes 49160 | tf_op jit(solution)/shard_map/ppermute | solution.py:26
  257.2 10.8 %collective-permute-done.7 = f32[4096]{0:T(1024)S(1)} collective-permute-done((f32[4096]{0:T(1024)S(1)}, f32[4096]{0:T(1024)S(1)}, u32[]{:S(2)}, u32[]{:S(2)}) %collective-permute-start.7) | collective-permute-done | bytes 16416 | tf_op jit(solution)/shard_map/ppermute | solution.py:26
  267.9 1.9 collective-permute-start.8
  269.9 1.1 collective-permute-done.8
  271.6 2.1 collective-permute-start.9
  273.7 1.0 collective-permute-done.9
  274.7 2.6 collective-permute-start.10
  277.2 2.9 collective-permute-done.10
  280.1 2.4 collective-permute-start.11
  282.5 4.6 %collective-permute-done.11 = f32[3,128]{1,0:T(4,128)S(1)} collective-permute-done((f32[3,128]{1,0:T(4,128)S(1)}, f32[3,128]{1,0:T(4,128)S(1)}, u32[]{:S(2)}, u32[]{:S(2)}) %collective-permute-start.11) | collective-permute-done | bytes 1568 | tf_op jit(solution)/shard_map/ppermute | solution.py:26
  287.1 1.9 collective-permute-start.12
  289.0 3.6 %collective-permute-done.12 = f32[3,128]{1,0:T(4,128)S(1)} collective-permute-done((f32[3,128]{1,0:T(4,128)S(1)}, f32[3,128]{1,0:T(4,128)S(1)}, u32[]{:S(2)}, u32[]{:S(2)}) %collective-permute-start.12) | collective-permute-done | bytes 1568 | tf_op jit(solution)/shard_map/ppermute | solution.py:26
  292.6 3.0 collective-permute-start.13
  295.6 4.0 %collective-permute-done.13 = f32[3,128]{1,0:T(4,128)S(1)} collective-permute-done((f32[3,128]{1,0:T(4,128)S(1)}, f32[3,128]{1,0:T(4,128)S(1)}, u32[]{:S(2)}, u32[]{:S(2)}) %collective-permute-start.13) | collective-permute-done | bytes 1568 | tf_op jit(solution)/shard_map/ppermute | solution.py:26
  299.6 2.0 collective-permute-start.14
  301.6 3.5 %collective-permute-done.14 = f32[3,128]{1,0:T(4,128)S(1)} collective-permute-done((f32[3,128]{1,0:T(4,128)S(1)}, f32[3,128]{1,0:T(4,128)S(1)}, u32[]{:S(2)}, u32[]{:S(2)}) %collective-permute-start.14) | collective-permute-done | bytes 1568 | tf_op jit(solution)/shard_map/ppermute | solution.py:26
  305.0 1.9 collective-permute-start.15
  306.9 4.4 %collective-permute-done.15 = f32[3,128]{1,0:T(4,128)S(1)} collective-permute-done((f32[3,128]{1,0:T(4,128)S(1)}, f32[3,128]{1,0:T(4,128)S(1)}, u32[]{:S(2)}, u32[]{:S(2)}) %collective-permute-start.15) | collective-permute-done | bytes 1568 | tf_op jit(solution)/shard_map/ppermute | solution.py:26
  311.4 2.3 collective-permute-start.16
  313.7 7.1 %collective-permute-done.16 = f32[3,128]{1,0:T(4,128)S(1)} collective-permute-done((f32[3,128]{1,0:T(4,128)S(1)}, f32[3,128]{1,0:T(4,128)S(1)}, u32[]{:S(2)}, u32[]{:S(2)}) %collective-permute-start.16) | collective-permute-done | bytes 1568 | tf_op jit(solution)/shard_map/ppermute | solution.py:26
  320.8 3.6 %collective-permute-start.17 = (f32[3,128]{1,0:T(4,128)S(1)}, f32[3,128]{1,0:T(4,128)S(1)}, u32[]{:S(2)}, u32[]{:S(2)}) collective-permute-start(f32[3,128]{1,0:T(4,128)S(1)} %add.217), channel_id=1, source_target_pairs={{0,128},{4,132},{8,136},{12,140},{16,144},{20,148},{24,152},{28,15... | collective-permute-start | bytes 4616 | tf_op jit(solution)/shard_map/ppermute | solution.py:26
  324.4 10.6 %collective-permute-done.17 = f32[3,128]{1,0:T(4,128)S(1)} collective-permute-done((f32[3,128]{1,0:T(4,128)S(1)}, f32[3,128]{1,0:T(4,128)S(1)}, u32[]{:S(2)}, u32[]{:S(2)}) %collective-permute-start.17) | collective-permute-done | bytes 1568 | tf_op jit(solution)/shard_map/ppermute | solution.py:26
  (68 shorter events, 10.4 us)
Async XLA Ops:
  0.6 2.9 copy-start
  11.4 18.7 %copy-start.1 = (bf16[32,4096]{1,0:T(8,128)(2,1)S(1)}, bf16[32,4096]{1,0:T(8,128)(2,1)}, u32[]{:S(2)}) copy-start(bf16[32,4096]{1,0:T(8,128)(2,1)} %param.7) | copy-start | bytes 786436
  11.4 118.9 %all-to-all-start = ((bf16[64,4,4096]{2,1,0:T(4,128)(2,1)}), bf16[64,4,4096]{2,1,0:T(4,128)(2,1)S(1)}, u32[]{:S(2)}, u32[]{:S(2)}) async-start(bf16[64,4,4096]{2,1,0:T(4,128)(2,1)} %select_select_fusion), calls=%async_computation | async-start | bytes 4194304 | tf_op jit(solution)/shard_map/all_to_all | solution.py:121
  135.1 7.2 %collective-permute-start = (f32[256,5,32]{0,2,1:T(8,128)S(1)}, f32[256,5,32]{0,2,1:T(8,128)S(1)}, u32[]{:S(2)}, u32[]{:S(2)}) collective-permute-start(f32[256,5,32]{0,2,1:T(8,128)S(1)} %fusion.24), channel_id=1, source_target_pairs={{0,1},{1,0},{2,3},{3,2},{4,5},{5,4},{6,7},{7,6},{8,9},{9,8},{10,11... | collective-permute-start | bytes 491528 | tf_op jit(solution)/shard_map/ppermute | solution.py:26
  142.4 15.7 %collective-permute-start.1 = (f32[256,5,32]{0,2,1:T(8,128)S(1)}, f32[256,5,32]{0,2,1:T(8,128)S(1)}, u32[]{:S(2)}, u32[]{:S(2)}) collective-permute-start(f32[256,5,32]{0,2,1:T(8,128)S(1)} %add.184), channel_id=1, source_target_pairs={{0,2},{1,3},{2,0},{3,1},{4,6},{5,7},{6,4},{7,5},{8,10},{9,11},{10,... | collective-permute-start | bytes 491528 | tf_op jit(solution)/shard_map/ppermute | solution.py:26
  204.7 13.0 %collective-permute-start.2 = (f32[2,2,2,2,2,4096]{5,4,3,2,1,0:T(2,128)S(1)}, f32[2,2,2,2,2,4096]{5,4,3,2,1,0:T(2,128)S(1)}, u32[]{:S(2)}, u32[]{:S(2)}) collective-permute-start(f32[2,2,2,2,2,4096]{5,4,3,2,1,0:T(2,128)S(1)} %bitcast.117), channel_id=1, source_target_pairs={{0,4},{4,0},{8,12},{12,8},{16,20},{20,16},{24,28},{28,24},{32,36},... | collective-permute-start | bytes 1572872 | tf_op jit(solution)/shard_map/ppermute | solution.py:26
  218.3 52.7 %copy-start.3 = (s32[1,2048]{1,0:T(1,128)S(1)}, s32[1,2048]{1,0:T(1,128)}, u32[]{:S(2)}) copy-start(s32[1,2048]{1,0:T(1,128)} %param.9) | copy-start | bytes 24580
  218.3 8.3 %collective-permute-start.3 = (f32[2,2,2,2,4096]{4,3,2,1,0:T(2,128)S(1)}, f32[2,2,2,2,4096]{4,3,2,1,0:T(2,128)S(1)}, u32[]{:S(2)}, u32[]{:S(2)}) collective-permute-start(f32[2,2,2,2,4096]{4,3,2,1,0:T(2,128)S(1)} %dynamic-slice_bitcast_fusion), channel_id=1, source_target_pairs={{0,16},{4,20},{8,24},{12,28},{16,0},{20,4},{24,8},{28,12},{32,48},... | collective-permute-start | bytes 786440 | tf_op jit(solution)/shard_map/ppermute | solution.py:26
  227.1 8.4 %collective-permute-start.4 = (f32[2,2,2,4096]{3,2,1,0:T(2,128)S(1)}, f32[2,2,2,4096]{3,2,1,0:T(2,128)S(1)}, u32[]{:S(2)}, u32[]{:S(2)}) collective-permute-start(f32[2,2,2,4096]{3,2,1,0:T(2,128)S(1)} %bitcast.119), channel_id=1, source_target_pairs={{0,8},{4,12},{8,0},{12,4},{16,24},{20,28},{24,16},{28,20},{32,40},... | collective-permute-start | bytes 393224 | tf_op jit(solution)/shard_map/ppermute | solution.py:26
  235.8 7.8 %collective-permute-start.5 = (f32[2,2,4096]{2,1,0:T(2,128)S(1)}, f32[2,2,4096]{2,1,0:T(2,128)S(1)}, u32[]{:S(2)}, u32[]{:S(2)}) collective-permute-start(f32[2,2,4096]{2,1,0:T(2,128)S(1)} %bitcast.120), channel_id=1, source_target_pairs={{0,32},{4,36},{8,40},{12,44},{16,48},{20,52},{24,56},{28,60},{32,0... | collective-permute-start | bytes 196616 | tf_op jit(solution)/shard_map/ppermute | solution.py:26
  243.8 9.7 %collective-permute-start.6 = (f32[2,4096]{1,0:T(2,128)S(1)}, f32[2,4096]{1,0:T(2,128)S(1)}, u32[]{:S(2)}, u32[]{:S(2)}) collective-permute-start(f32[2,4096]{1,0:T(2,128)S(1)} %bitcast.122), channel_id=1, source_target_pairs={{0,64},{4,68},{8,72},{12,76},{16,80},{20,84},{24,88},{28,92},{32,9... | collective-permute-start | bytes 98312 | tf_op jit(solution)/shard_map/ppermute | solution.py:26
  253.6 14.3 %collective-permute-start.7 = (f32[4096]{0:T(1024)S(1)}, f32[4096]{0:T(1024)S(1)}, u32[]{:S(2)}, u32[]{:S(2)}) collective-permute-start(f32[4096]{0:T(1024)S(1)} %bitcast.123), channel_id=1, source_target_pairs={{0,128},{4,132},{8,136},{12,140},{16,144},{20,148},{24,152},{28,15... | collective-permute-start | bytes 49160 | tf_op jit(solution)/shard_map/ppermute | solution.py:26
  267.9 3.1 collective-permute-start.8
  271.6 3.1 collective-permute-start.9
  274.7 5.5 %collective-permute-start.10 = (f32[3,128]{1,0:T(4,128)S(1)}, f32[3,128]{1,0:T(4,128)S(1)}, u32[]{:S(2)}, u32[]{:S(2)}) collective-permute-start(f32[3,128]{1,0:T(4,128)S(1)} %add.210), channel_id=1, source_target_pairs={{0,1},{1,0},{2,3},{3,2},{4,5},{5,4},{6,7},{7,6},{8,9},{9,8},{10,11... | collective-permute-start | bytes 4616 | tf_op jit(solution)/shard_map/ppermute | solution.py:26
  280.1 7.0 %collective-permute-start.11 = (f32[3,128]{1,0:T(4,128)S(1)}, f32[3,128]{1,0:T(4,128)S(1)}, u32[]{:S(2)}, u32[]{:S(2)}) collective-permute-start(f32[3,128]{1,0:T(4,128)S(1)} %add.211), channel_id=1, source_target_pairs={{0,2},{1,3},{2,0},{3,1},{4,6},{5,7},{6,4},{7,5},{8,10},{9,11},{10,... | collective-permute-start | bytes 4616 | tf_op jit(solution)/shard_map/ppermute | solution.py:26
  287.1 5.5 %collective-permute-start.12 = (f32[3,128]{1,0:T(4,128)S(1)}, f32[3,128]{1,0:T(4,128)S(1)}, u32[]{:S(2)}, u32[]{:S(2)}) collective-permute-start(f32[3,128]{1,0:T(4,128)S(1)} %add.212), channel_id=1, source_target_pairs={{0,4},{4,0},{8,12},{12,8},{16,20},{20,16},{24,28},{28,24},{32,36},... | collective-permute-start | bytes 4616 | tf_op jit(solution)/shard_map/ppermute | solution.py:26
  292.6 7.0 %collective-permute-start.13 = (f32[3,128]{1,0:T(4,128)S(1)}, f32[3,128]{1,0:T(4,128)S(1)}, u32[]{:S(2)}, u32[]{:S(2)}) collective-permute-start(f32[3,128]{1,0:T(4,128)S(1)} %add.213), channel_id=1, source_target_pairs={{0,8},{4,12},{8,0},{12,4},{16,24},{20,28},{24,16},{28,20},{32,40},... | collective-permute-start | bytes 4616 | tf_op jit(solution)/shard_map/ppermute | solution.py:26
  299.6 5.5 %collective-permute-start.14 = (f32[3,128]{1,0:T(4,128)S(1)}, f32[3,128]{1,0:T(4,128)S(1)}, u32[]{:S(2)}, u32[]{:S(2)}) collective-permute-start(f32[3,128]{1,0:T(4,128)S(1)} %add.214), channel_id=1, source_target_pairs={{0,16},{4,20},{8,24},{12,28},{16,0},{20,4},{24,8},{28,12},{32,48},... | collective-permute-start | bytes 4616 | tf_op jit(solution)/shard_map/ppermute | solution.py:26
  305.0 6.4 %collective-permute-start.15 = (f32[3,128]{1,0:T(4,128)S(1)}, f32[3,128]{1,0:T(4,128)S(1)}, u32[]{:S(2)}, u32[]{:S(2)}) collective-permute-start(f32[3,128]{1,0:T(4,128)S(1)} %add.215), channel_id=1, source_target_pairs={{0,32},{4,36},{8,40},{12,44},{16,48},{20,52},{24,56},{28,60},{32,0... | collective-permute-start | bytes 4616 | tf_op jit(solution)/shard_map/ppermute | solution.py:26
  311.4 9.4 %collective-permute-start.16 = (f32[3,128]{1,0:T(4,128)S(1)}, f32[3,128]{1,0:T(4,128)S(1)}, u32[]{:S(2)}, u32[]{:S(2)}) collective-permute-start(f32[3,128]{1,0:T(4,128)S(1)} %add.216), channel_id=1, source_target_pairs={{0,64},{4,68},{8,72},{12,76},{16,80},{20,84},{24,88},{28,92},{32,9... | collective-permute-start | bytes 4616 | tf_op jit(solution)/shard_map/ppermute | solution.py:26
  320.8 14.2 %collective-permute-start.17 = (f32[3,128]{1,0:T(4,128)S(1)}, f32[3,128]{1,0:T(4,128)S(1)}, u32[]{:S(2)}, u32[]{:S(2)}) collective-permute-start(f32[3,128]{1,0:T(4,128)S(1)} %add.217), channel_id=1, source_target_pairs={{0,128},{4,132},{8,136},{12,140},{16,144},{20,148},{24,152},{28,15... | collective-permute-start | bytes 4616 | tf_op jit(solution)/shard_map/ppermute | solution.py:26
  335.6 3.3 copy-start.2

commit v3 on v1

--- a/solution.py
+++ b/solution.py
@@ -24,6 +24,52 @@
 
 def partner(shard, axis, apart):
     return lax.ppermute(shard, axis, [(i, i ^ 1 << apart) for i in range(lax.axis_size(axis))])
+
+
+def digits_of(n):
+    out, stride = [], 1
+    while n % 4 == 0 and n > 1:
+        out.append((stride, 4))
+        stride, n = stride * 4, n // 4
+    while n % 2 == 0 and n > 1:
+        out.append((stride, 2))
+        stride, n = stride * 2, n // 2
+    return out
+
+
+def shift_in_digit(x, axis, stride, radix, shift):
+    n = lax.axis_size(axis)
+    perm = []
+    for i in range(n):
+        d = (i // stride) % radix
+        perm.append((i, i + ((d + shift) % radix - d) * stride))
+    return lax.ppermute(x, axis, perm)
+
+
+def digit_sum(x, axis):
+    me = lax.axis_index(axis)
+    for stride, radix in digits_of(lax.axis_size(axis)):
+        d = (me // stride) % radix
+        got = jnp.stack([x] + [shift_in_digit(x, axis, stride, radix, s) for s in range(1, radix)])
+        total = lax.dynamic_index_in_dim(got, d % radix, keepdims=False)
+        for t in range(1, radix):
+            total = total + lax.dynamic_index_in_dim(got, (d - t) % radix, keepdims=False)
+        x = total
+    return x
+
+
+def reduce_scatter(x, axis):
+    me = lax.axis_index(axis)
+    data = x
+    for stride, radix in digits_of(lax.axis_size(axis)):
+        d = (me // stride) % radix
+        data = data.reshape(data.shape[0] // radix, radix, data.shape[1])
+        total = lax.dynamic_index_in_dim(data, d, axis=1, keepdims=False)
+        for s in range(1, radix):
+            send = lax.dynamic_index_in_dim(data, (d + s) % radix, axis=1, keepdims=False)
+            total = total + shift_in_digit(send, axis, stride, radix, s)
+        data = total
+    return data[0]
 
 
 def _project_kernel(val_ref, idx_ref, out_ref):
@@ -117,7 +163,7 @@
         arrived, rolled_refs, (((1,), (1,)), ((), ())), preferred_element_type=jnp.float32
     )
     partial_scores = partial_scores.reshape(slot_count, SHIFTS, class_count)
-    scores = lax.psum(partial_scores, "vol")
+    scores = digit_sum(partial_scores, "vol")
     squares = scores * scores
     mean_square = jnp.mean(squares, axis=(1, 2), keepdims=True)
     weights = (squares / (mean_square + EPS_W)).astype(jnp.bfloat16)
@@ -136,23 +182,31 @@
     slab_part = project(val_t, idx_t, bins)
     piece_len = VOXS // (n_half * n_cls)
     slab_part = slab_part.reshape(n_cls, n_half * piece_len)
-    own_block = lax.psum_scatter(slab_part, "cls", scatter_dimension=0, tiled=True)
-    own_block = own_block.reshape(n_half, piece_len)
+    own_block = reduce_scatter(slab_part, "cls")
     half_id = lax.axis_index("half")
-    own_piece = jnp.where(half_id == 0, own_block[0], own_block[1])
-    other_piece = jnp.where(half_id == 0, own_block[1], own_block[0])
-    mirror_piece = partner(other_piece, "half", 0)
-    first = jnp.where(half_id == 0, own_piece, mirror_piece)
-    second = jnp.where(half_id == 0, mirror_piece, own_piece)
-    shell_hot = (shell_index[0][:, None] == jnp.arange(NSHELL, dtype=jnp.int32)[None, :]).astype(
+    other_block = partner(own_block, "half", 0)
+    other_shell = partner(shell_index[0], "half", 0)
+    first_block = jnp.where(half_id == 0, own_block, other_block)
+    second_block = jnp.where(half_id == 0, other_block, own_block)
+    shell_block = jnp.where(
+        half_id == 0,
+        jnp.concatenate([shell_index[0], other_shell]),
+        jnp.concatenate([other_shell, shell_index[0]]),
+    )
+    block_hot = (shell_block[:, None] == jnp.arange(NSHELL, dtype=jnp.int32)[None, :]).astype(
         jnp.float32
     )
-    stats = jnp.stack([first * first, second * second, first * second])
-    shell_terms = jnp.dot(stats, shell_hot, precision=lax.Precision.HIGHEST)
-    shell_sums = lax.psum(shell_terms, ("half", "cls", "vol"))
+    stats = jnp.stack([first_block * first_block, second_block * second_block, first_block * second_block])
+    shell_terms = jnp.dot(stats, block_hot, precision=lax.Precision.HIGHEST)
+    shell_sums = digit_sum(digit_sum(shell_terms, "vol"), "cls")
     shell_fsc = shell_sums[2] / (jnp.sqrt(shell_sums[0]) * jnp.sqrt(shell_sums[1]) + EPS_F)
     mean_sq = (jnp.sum(shell_sums[0]) + jnp.sum(shell_sums[1]) + 2.0 * jnp.sum(shell_sums[2])) / (
         4.0 * n_vol * VOXS
+    )
+    first = lax.dynamic_index_in_dim(first_block.reshape(n_half, piece_len), half_id, keepdims=False)
+    second = lax.dynamic_index_in_dim(second_block.reshape(n_half, piece_len), half_id, keepdims=False)
+    shell_hot = (shell_index[0][:, None] == jnp.arange(NSHELL, dtype=jnp.int32)[None, :]).astype(
+        jnp.float32
     )
     filter_vox = jnp.dot(shell_hot, shell_fsc, precision=lax.Precision.HIGHEST)
     volume = filter_vox * (0.5 * (first + second)) / jnp.sqrt(mean_sq + EPS_F)

time: 634 us -> 316 us (0.50)
  waiting for transfers between devices: 408 us -> 129 us
  blocking collectives: 101 us -> 0 us
  starting transfers between devices: 20.7 us -> 109 us
  between operations: 16.2 us -> 3.86 us
    unnamed x3 -> x0, waiting for transfers between devices: 274 us -> none
    psum x1 -> x0, blocking collectives: 101 us -> none  [shards(): shell_sums = lax.psum(shell_terms, ('half', 'cls', 'vol'))]
    ppermute x0 -> x24, starting transfers between devices: none -> 86.1 us  [shift_in_digit(): return lax.ppermute(x, axis, perm)]
    psum x1 -> x0, waiting for transfers between devices: 38.3 us -> none  [shards(): scores = lax.psum(partial_scores, 'vol')]
    ppermute x0 -> x24, waiting for transfers between devices: none -> 33.1 us  [shift_in_digit(): return lax.ppermute(x, axis, perm)]
  transfers between devices with their start and end apart: 4 -> 27, of which waited for: 4 -> 14; matrix products, arithmetic and copies ran while one was open for 3% -> 4% of each run, Pallas kernels for 0% -> 0%
where the time goes in v3:
time: 316 us; the launch traced here: 314 us
  waiting for transfers between devices  129 us (41%)
  starting transfers between devices  109 us (34%)
  local copies, waits for them, and re-layouts  29.7 us (9%)
  Pallas kernels  27.8 us (9%)
  other arithmetic  10.5 us (3%)
  matrix products  4.37 us (1%)
  between operations  3.86 us (1%)
    all_to_all x1, waiting for transfers between devices, shards(): lax.all_to_all(outgoing.reshape(n_cls, capacity, pix_quarter), 'cls', spl...  94.9 us
    ppermute x24, starting transfers between devices, shift_in_digit(): return lax.ppermute(x, axis, perm)  86.1 us
    ppermute x24, waiting for transfers between devices, shift_in_digit(): return lax.ppermute(x, axis, perm)  33.1 us
    pallas_call x1, Pallas kernels, project(): pl.pallas_call(_project_kernel, out_shape=jax.ShapeDtypeStruct((q_count,...  27.8 us
    all_to_all x1, starting transfers between devices, shards(): lax.all_to_all(outgoing.reshape(n_cls, capacity, pix_quarter), 'cls', spl...  18.9 us
    unnamed x24, local copies, waits for them, and re-layouts  6.39 us
  transfers between devices with their start and end apart: 27, of which 14 were waited for; matrix products, arithmetic and copies ran while one was open for 4% of the time, Pallas kernels for 0%

profile of v3, /device:TPU:6, one launch (start us, length us, event | category | flops | bytes accessed | tf_op | source)
XLA Modules:
  0.0 314.1 jit_solution(9133094187938736102)
XLA Ops:
  0.6 0.8 fusion.18
  1.6 0.8 select_reduce_fusion.1
  3.5 1.8 gather_fusion
  5.4 2.2 gather.7
  7.7 3.7 %select_select_fusion = bf16[64,4,4096]{2,1,0:T(4,128)(2,1)} fusion(bf16[64,4,4096]{2,1,0:T(4,128)(2,1)} %gather.7, pred[64,4]{1,0:T(8,128)(4,1)S(1)} %compare_and_fusion, pred[64,4]{1,0:T(8,128)(4,1)S(1)} %broadcast_in_dim.48), kind=kLoop, calls=%fused_computation.2 | loop fusion | flops 2097152 | bytes 4194816 | tf_op jit(solution)/shard_map/jit(_where)/select_n | solution.py:136
  11.4 18.9 %all-to-all-start = ((bf16[64,4,4096]{2,1,0:T(4,128)(2,1)}), bf16[64,4,4096]{2,1,0:T(4,128)(2,1)}, u32[]{:S(2)}, u32[]{:S(2)}) async-start(bf16[64,4,4096]{2,1,0:T(4,128)(2,1)} %select_select_fusion), calls=%async_computation | async-start | bytes 4194304 | tf_op jit(solution)/shard_map/all_to_all | solution.py:139
  31.6 0.8 bitcast_dynamic-update-slice_fusion.3
  32.4 0.8 bitcast_dynamic-update-slice_fusion.2
  33.9 0.8 bitcast_dynamic-update-slice_fusion.1
  34.7 0.8 bitcast_dynamic-update-slice_fusion
  35.5 94.9 %all-to-all-done = bf16[64,4,4096]{2,1,0:T(4,128)(2,1)} async-done(((bf16[64,4,4096]{2,1,0:T(4,128)(2,1)}), bf16[64,4,4096]{2,1,0:T(4,128)(2,1)}, u32[]{:S(2)}, u32[]{:S(2)}) %all-to-all-start) | async-done | bytes 2097184 | tf_op jit(solution)/shard_map/all_to_all | solution.py:139
  130.4 2.5 reshape.201
  132.9 2.2 fusion.42
  135.1 4.9 %collective-permute-start.2 = (f32[256,5,32]{0,2,1:T(8,128)S(1)}, f32[256,5,32]{0,2,1:T(8,128)S(1)}, u32[]{:S(2)}, u32[]{:S(2)}) collective-permute-start(f32[256,5,32]{0,2,1:T(8,128)S(1)} %bitcast.147), channel_id=1, source_target_pairs={{0,3},{1,0},{2,1},{3,2},{4,7},{5,4},{6,5},{7,6},{8,11},{9,8},{10,9... | collective-permute-start | bytes 491528 | tf_op jit(solution)/shard_map/ppermute | solution.py:46
  140.0 2.5 collective-permute-start.1
  142.6 3.1 collective-permute-start
  145.8 1.9 reshape.210
  147.7 2.0 copy.28
  149.8 2.2 copy.29
  152.0 2.2 reshape.212.idx_ref
  154.2 1.0 pad_maximum_fusion
  155.9 1.2 slice_bitcast_fusion
  157.0 1.1 squeeze.99
  158.2 1.1 copy.43
  161.7 1.2 reshape.209.val_ref
  162.8 27.8 %shard_map.68 = f32[128,16,128]{2,1,0:T(8,128)} custom-call(f32[128,1024]{1,0:T(8,128)} %reshape.209.val_ref, s32[128,1024]{1,0:T(8,128)} %reshape.212.idx_ref), custom_call_target="tpu_custom_call" | custom-call | flops 1073741824 | bytes 2097152 | tf_op jit(solution)/shard_map/pallas_call | solution.py:102
  190.6 1.6 reshape_reshape.3
  192.2 1.1 constant_dynamic-slice_fusion.25
  193.5 2.8 collective-permute-start.5
  196.4 3.1 collective-permute-start.4
  199.7 4.0 %collective-permute-start.3 = (f32[16,4096]{1,0:T(8,128)S(1)}, f32[16,4096]{1,0:T(8,128)S(1)}, u32[]{:S(2)}, u32[]{:S(2)}) collective-permute-start(f32[16,4096]{1,0:T(8,128)S(1)} %bitcast.154), channel_id=1, source_target_pairs={{0,4},{4,8},{8,12},{12,0},{16,20},{20,24},{24,28},{28,16},{32,36},... | collective-permute-start | bytes 786440 | tf_op jit(solution)/shard_map/ppermute | solution.py:46
  203.7 4.6 %collective-permute-done.5 = f32[16,4096]{1,0:T(8,128)S(1)} collective-permute-done((f32[16,4096]{1,0:T(8,128)S(1)}, f32[16,4096]{1,0:T(8,128)S(1)}, u32[]{:S(2)}, u32[]{:S(2)}) %collective-permute-start.5) | collective-permute-done | bytes 262176 | tf_op jit(solution)/shard_map/ppermute | solution.py:46
  208.3 2.7 collective-permute-done.3
  211.5 2.8 collective-permute-start.8
  214.3 1.9 collective-permute-start.7
  216.3 3.1 collective-permute-start.6
  219.5 2.7 collective-permute-done.7
  222.2 2.2 collective-permute-done.6
  224.5 2.9 collective-permute-start.11
  227.4 9.0 %collective-permute-start.10 = (f32[1,4096]{1,0:T(1,128)S(1)}, f32[1,4096]{1,0:T(1,128)S(1)}, u32[]{:S(2)}, u32[]{:S(2)}) collective-permute-start(f32[1,4096]{1,0:T(1,128)S(1)} %get-tuple-element.34), channel_id=1, source_target_pairs={{0,128},{4,132},{8,136},{12,140},{16,144},{20,148},{24,152},{28,15... | collective-permute-start | bytes 49160 | tf_op jit(solution)/shard_map/ppermute | solution.py:46
  236.4 2.5 collective-permute-start.9
  238.9 1.9 collective-permute-start.13
  241.1 0.8 collective-permute-done.10
  241.9 4.0 %collective-permute-done.9 = f32[1,4096]{1,0:T(1,128)S(1)} collective-permute-done((f32[1,4096]{1,0:T(1,128)S(1)}, f32[1,4096]{1,0:T(1,128)S(1)}, u32[]{:S(2)}, u32[]{:S(2)}) %collective-permute-start.9) | collective-permute-done | bytes 16416 | tf_op jit(solution)/shard_map/ppermute | solution.py:46
  245.9 1.9 collective-permute-start.12
  247.9 1.1 collective-permute-done.12
  249.1 1.0 fusion
  250.0 4.2 %collective-permute-start.16 = (f32[3,128]{1,0:T(4,128)S(1)}, f32[3,128]{1,0:T(4,128)S(1)}, u32[]{:S(2)}, u32[]{:S(2)}) collective-permute-start(f32[3,128]{1,0:T(4,128)S(1)} %fusion), channel_id=1, source_target_pairs={{0,3},{1,0},{2,1},{3,2},{4,7},{5,4},{6,5},{7,6},{8,11},{9,8},{10,9... | collective-permute-start | bytes 4616 | tf_op jit(solution)/shard_map/ppermute | solution.py:46
  254.2 3.6 %collective-permute-start.15 = (f32[3,128]{1,0:T(4,128)S(1)}, f32[3,128]{1,0:T(4,128)S(1)}, u32[]{:S(2)}, u32[]{:S(2)}) collective-permute-start(f32[3,128]{1,0:T(4,128)S(1)} %fusion), channel_id=1, source_target_pairs={{0,2},{1,3},{2,0},{3,1},{4,6},{5,7},{6,4},{7,5},{8,10},{9,11},{10,... | collective-permute-start | bytes 4616 | tf_op jit(solution)/shard_map/ppermute | solution.py:46
  257.8 1.9 collective-permute-start.14
  259.8 1.4 collective-permute-done.15
  261.2 3.3 %collective-permute-done.14 = f32[3,128]{1,0:T(4,128)S(1)} collective-permute-done((f32[3,128]{1,0:T(4,128)S(1)}, f32[3,128]{1,0:T(4,128)S(1)}, u32[]{:S(2)}, u32[]{:S(2)}) %collective-permute-start.14) | collective-permute-done | bytes 1568 | tf_op jit(solution)/shard_map/ppermute | solution.py:46
  264.5 2.6 collective-permute-start.19
  267.2 5.3 %collective-permute-start.18 = (f32[3,128]{1,0:T(4,128)S(1)}, f32[3,128]{1,0:T(4,128)S(1)}, u32[]{:S(2)}, u32[]{:S(2)}) collective-permute-start(f32[3,128]{1,0:T(4,128)S(1)} %fusion.50), channel_id=1, source_target_pairs={{0,8},{4,12},{8,0},{12,4},{16,24},{20,28},{24,16},{28,20},{32,40},... | collective-permute-start | bytes 4616 | tf_op jit(solution)/shard_map/ppermute | solution.py:46
  272.5 1.9 collective-permute-start.17
  274.5 3.5 %collective-permute-done.17 = f32[3,128]{1,0:T(4,128)S(1)} collective-permute-done((f32[3,128]{1,0:T(4,128)S(1)}, f32[3,128]{1,0:T(4,128)S(1)}, u32[]{:S(2)}, u32[]{:S(2)}) %collective-permute-start.17) | collective-permute-done | bytes 1568 | tf_op jit(solution)/shard_map/ppermute | solution.py:46
  278.0 2.0 collective-permute-start.22
  280.0 1.9 collective-permute-start.21
  281.9 3.9 %collective-permute-start.20 = (f32[3,128]{1,0:T(4,128)S(1)}, f32[3,128]{1,0:T(4,128)S(1)}, u32[]{:S(2)}, u32[]{:S(2)}) collective-permute-start(f32[3,128]{1,0:T(4,128)S(1)} %fusion.49), channel_id=1, source_target_pairs={{0,16},{4,20},{8,24},{12,28},{16,32},{20,36},{24,40},{28,44},{32,4... | collective-permute-start | bytes 4616 | tf_op jit(solution)/shard_map/ppermute | solution.py:46
  286.4 3.3 %collective-permute-done.20 = f32[3,128]{1,0:T(4,128)S(1)} collective-permute-done((f32[3,128]{1,0:T(4,128)S(1)}, f32[3,128]{1,0:T(4,128)S(1)}, u32[]{:S(2)}, u32[]{:S(2)}) %collective-permute-start.20) | collective-permute-done | bytes 1568 | tf_op jit(solution)/shard_map/ppermute | solution.py:46
  289.7 6.2 %collective-permute-start.25 = (f32[3,128]{1,0:T(4,128)S(1)}, f32[3,128]{1,0:T(4,128)S(1)}, u32[]{:S(2)}, u32[]{:S(2)}) collective-permute-start(f32[3,128]{1,0:T(4,128)S(1)} %fusion.48), channel_id=1, source_target_pairs={{0,192},{4,196},{8,200},{12,204},{16,208},{20,212},{24,216},{28,22... | collective-permute-start | bytes 4616 | tf_op jit(solution)/shard_map/ppermute | solution.py:46
  295.9 4.8 %collective-permute-start.24 = (f32[3,128]{1,0:T(4,128)S(1)}, f32[3,128]{1,0:T(4,128)S(1)}, u32[]{:S(2)}, u32[]{:S(2)}) collective-permute-start(f32[3,128]{1,0:T(4,128)S(1)} %fusion.48), channel_id=1, source_target_pairs={{0,128},{4,132},{8,136},{12,140},{16,144},{20,148},{24,152},{28,15... | collective-permute-start | bytes 4616 | tf_op jit(solution)/shard_map/ppermute | solution.py:46
  300.8 5.3 %collective-permute-start.23 = (f32[3,128]{1,0:T(4,128)S(1)}, f32[3,128]{1,0:T(4,128)S(1)}, u32[]{:S(2)}, u32[]{:S(2)}) collective-permute-start(f32[3,128]{1,0:T(4,128)S(1)} %fusion.48), channel_id=1, source_target_pairs={{0,64},{4,68},{8,72},{12,76},{16,80},{20,84},{24,88},{28,92},{32,9... | collective-permute-start | bytes 4616 | tf_op jit(solution)/shard_map/ppermute | solution.py:46
  306.1 4.1 %collective-permute-done.24 = f32[3,128]{1,0:T(4,128)S(1)} collective-permute-done((f32[3,128]{1,0:T(4,128)S(1)}, f32[3,128]{1,0:T(4,128)S(1)}, u32[]{:S(2)}, u32[]{:S(2)}) %collective-permute-start.24) | collective-permute-done | bytes 1568 | tf_op jit(solution)/shard_map/ppermute | solution.py:46
  (85 shorter events, 10.2 us)
Async XLA Ops:
  0.6 2.9 copy-start
  11.4 18.9 %copy-start.1 = (bf16[32,4096]{1,0:T(8,128)(2,1)S(1)}, bf16[32,4096]{1,0:T(8,128)(2,1)}, u32[]{:S(2)}) copy-start(bf16[32,4096]{1,0:T(8,128)(2,1)} %param.7) | copy-start | bytes 786436
  11.4 119.0 %all-to-all-start = ((bf16[64,4,4096]{2,1,0:T(4,128)(2,1)}), bf16[64,4,4096]{2,1,0:T(4,128)(2,1)}, u32[]{:S(2)}, u32[]{:S(2)}) async-start(bf16[64,4,4096]{2,1,0:T(4,128)(2,1)} %select_select_fusion), calls=%async_computation | async-start | bytes 4194304 | tf_op jit(solution)/shard_map/all_to_all | solution.py:139
  135.1 19.1 %collective-permute-start.2 = (f32[256,5,32]{0,2,1:T(8,128)S(1)}, f32[256,5,32]{0,2,1:T(8,128)S(1)}, u32[]{:S(2)}, u32[]{:S(2)}) collective-permute-start(f32[256,5,32]{0,2,1:T(8,128)S(1)} %bitcast.147), channel_id=1, source_target_pairs={{0,3},{1,0},{2,1},{3,2},{4,7},{5,4},{6,5},{7,6},{8,11},{9,8},{10,9... | collective-permute-start | bytes 491528 | tf_op jit(solution)/shard_map/ppermute | solution.py:46
  140.0 14.2 %collective-permute-start.1 = (f32[256,5,32]{0,2,1:T(8,128)S(1)}, f32[256,5,32]{0,2,1:T(8,128)}, u32[]{:S(2)}, u32[]{:S(2)}) collective-permute-start(f32[256,5,32]{0,2,1:T(8,128)S(1)} %bitcast.148), channel_id=1, source_target_pairs={{0,2},{1,3},{2,0},{3,1},{4,6},{5,7},{6,4},{7,5},{8,10},{9,11},{10,... | collective-permute-start | bytes 491528 | tf_op jit(solution)/shard_map/ppermute | solution.py:46
  142.6 11.6 %collective-permute-start = (f32[256,5,32]{0,2,1:T(8,128)S(1)}, f32[256,5,32]{0,2,1:T(8,128)}, u32[]{:S(2)}, u32[]{:S(2)}) collective-permute-start(f32[256,5,32]{0,2,1:T(8,128)S(1)} %bitcast.149), channel_id=1, source_target_pairs={{0,1},{1,2},{2,3},{3,0},{4,5},{5,6},{6,7},{7,4},{8,9},{9,10},{10,1... | collective-permute-start | bytes 491528 | tf_op jit(solution)/shard_map/ppermute | solution.py:46
  193.5 14.8 %collective-permute-start.5 = (f32[16,4096]{1,0:T(8,128)S(1)}, f32[16,4096]{1,0:T(8,128)S(1)}, u32[]{:S(2)}, u32[]{:S(2)}) collective-permute-start(f32[16,4096]{1,0:T(8,128)S(1)} %bitcast.152), channel_id=1, source_target_pairs={{0,12},{4,0},{8,4},{12,8},{16,28},{20,16},{24,20},{28,24},{32,44},... | collective-permute-start | bytes 786440 | tf_op jit(solution)/shard_map/ppermute | solution.py:46
  196.4 42.4 %copy-start.2 = (s32[1,2048]{1,0:T(1,128)S(1)}, s32[1,2048]{1,0:T(1,128)}, u32[]{:S(2)}) copy-start(s32[1,2048]{1,0:T(1,128)} %param.9) | copy-start | bytes 24580
  196.4 11.9 %collective-permute-start.4 = (f32[16,4096]{1,0:T(8,128)S(1)}, f32[16,4096]{1,0:T(8,128)S(1)}, u32[]{:S(2)}, u32[]{:S(2)}) collective-permute-start(f32[16,4096]{1,0:T(8,128)S(1)} %bitcast.153), channel_id=1, source_target_pairs={{0,8},{4,12},{8,0},{12,4},{16,24},{20,28},{24,16},{28,20},{32,40},... | collective-permute-start | bytes 786440 | tf_op jit(solution)/shard_map/ppermute | solution.py:46
  199.7 11.3 %collective-permute-start.3 = (f32[16,4096]{1,0:T(8,128)S(1)}, f32[16,4096]{1,0:T(8,128)S(1)}, u32[]{:S(2)}, u32[]{:S(2)}) collective-permute-start(f32[16,4096]{1,0:T(8,128)S(1)} %bitcast.154), channel_id=1, source_target_pairs={{0,4},{4,8},{8,12},{12,0},{16,20},{20,24},{24,28},{28,16},{32,36},... | collective-permute-start | bytes 786440 | tf_op jit(solution)/shard_map/ppermute | solution.py:46
  211.5 8.0 %collective-permute-start.8 = (f32[4,4096]{1,0:T(4,128)S(1)}, f32[4,4096]{1,0:T(4,128)S(1)}, u32[]{:S(2)}, u32[]{:S(2)}) collective-permute-start(f32[4,4096]{1,0:T(4,128)S(1)} %bitcast.156), channel_id=1, source_target_pairs={{0,48},{4,52},{8,56},{12,60},{16,0},{20,4},{24,8},{28,12},{32,16},... | collective-permute-start | bytes 196616 | tf_op jit(solution)/shard_map/ppermute | solution.py:46
  214.3 7.8 %collective-permute-start.7 = (f32[4,4096]{1,0:T(4,128)S(1)}, f32[4,4096]{1,0:T(4,128)S(1)}, u32[]{:S(2)}, u32[]{:S(2)}) collective-permute-start(f32[4,4096]{1,0:T(4,128)S(1)} %bitcast.157), channel_id=1, source_target_pairs={{0,32},{4,36},{8,40},{12,44},{16,48},{20,52},{24,56},{28,60},{32,0... | collective-permute-start | bytes 196616 | tf_op jit(solution)/shard_map/ppermute | solution.py:46
  216.3 8.0 %collective-permute-start.6 = (f32[4,4096]{1,0:T(4,128)S(1)}, f32[4,4096]{1,0:T(4,128)S(1)}, u32[]{:S(2)}, u32[]{:S(2)}) collective-permute-start(f32[4,4096]{1,0:T(4,128)S(1)} %bitcast.158), channel_id=1, source_target_pairs={{0,16},{4,20},{8,24},{12,28},{16,32},{20,36},{24,40},{28,44},{32,4... | collective-permute-start | bytes 196616 | tf_op jit(solution)/shard_map/ppermute | solution.py:46
  224.5 16.6 %collective-permute-start.11 = (f32[1,4096]{1,0:T(1,128)S(1)}, f32[1,4096]{1,0:T(1,128)S(1)}, u32[]{:S(2)}, u32[]{:S(2)}) collective-permute-start(f32[1,4096]{1,0:T(1,128)S(1)} %get-tuple-element.33), channel_id=1, source_target_pairs={{0,192},{4,196},{8,200},{12,204},{16,208},{20,212},{24,216},{28,22... | collective-permute-start | bytes 49160 | tf_op jit(solution)/shard_map/ppermute | solution.py:46
  227.4 14.5 %collective-permute-start.10 = (f32[1,4096]{1,0:T(1,128)S(1)}, f32[1,4096]{1,0:T(1,128)S(1)}, u32[]{:S(2)}, u32[]{:S(2)}) collective-permute-start(f32[1,4096]{1,0:T(1,128)S(1)} %get-tuple-element.34), channel_id=1, source_target_pairs={{0,128},{4,132},{8,136},{12,140},{16,144},{20,148},{24,152},{28,15... | collective-permute-start | bytes 49160 | tf_op jit(solution)/shard_map/ppermute | solution.py:46
  236.4 9.5 %collective-permute-start.9 = (f32[1,4096]{1,0:T(1,128)S(1)}, f32[1,4096]{1,0:T(1,128)S(1)}, u32[]{:S(2)}, u32[]{:S(2)}) collective-permute-start(f32[1,4096]{1,0:T(1,128)S(1)} %get-tuple-element.32), channel_id=1, source_target_pairs={{0,64},{4,68},{8,72},{12,76},{16,80},{20,84},{24,88},{28,92},{32,9... | collective-permute-start | bytes 49160 | tf_op jit(solution)/shard_map/ppermute | solution.py:46
  238.9 9.0 %collective-permute-start.13 = (s32[2048]{0:T(1024)S(1)}, s32[2048]{0:T(1024)S(1)}, u32[]{:S(2)}, u32[]{:S(2)}) collective-permute-start(s32[2048]{0:T(1024)S(1)} %bitcast.167), channel_id=1, source_target_pairs={{0,256},{256,0},{1,257},{257,1},{2,258},{258,2},{3,259},{259,3},{4... | collective-permute-start | bytes 24584 | tf_op jit(solution)/shard_map/ppermute | solution.py:26
  245.9 3.1 collective-permute-start.12
  250.0 9.8 %collective-permute-start.16 = (f32[3,128]{1,0:T(4,128)S(1)}, f32[3,128]{1,0:T(4,128)S(1)}, u32[]{:S(2)}, u32[]{:S(2)}) collective-permute-start(f32[3,128]{1,0:T(4,128)S(1)} %fusion), channel_id=1, source_target_pairs={{0,3},{1,0},{2,1},{3,2},{4,7},{5,4},{6,5},{7,6},{8,11},{9,8},{10,9... | collective-permute-start | bytes 4616 | tf_op jit(solution)/shard_map/ppermute | solution.py:46
  254.2 7.0 %collective-permute-start.15 = (f32[3,128]{1,0:T(4,128)S(1)}, f32[3,128]{1,0:T(4,128)S(1)}, u32[]{:S(2)}, u32[]{:S(2)}) collective-permute-start(f32[3,128]{1,0:T(4,128)S(1)} %fusion), channel_id=1, source_target_pairs={{0,2},{1,3},{2,0},{3,1},{4,6},{5,7},{6,4},{7,5},{8,10},{9,11},{10,... | collective-permute-start | bytes 4616 | tf_op jit(solution)/shard_map/ppermute | solution.py:46
  257.8 6.7 %collective-permute-start.14 = (f32[3,128]{1,0:T(4,128)S(1)}, f32[3,128]{1,0:T(4,128)S(1)}, u32[]{:S(2)}, u32[]{:S(2)}) collective-permute-start(f32[3,128]{1,0:T(4,128)S(1)} %fusion), channel_id=1, source_target_pairs={{0,1},{1,2},{2,3},{3,0},{4,5},{5,6},{6,7},{7,4},{8,9},{9,10},{10,1... | collective-permute-start | bytes 4616 | tf_op jit(solution)/shard_map/ppermute | solution.py:46
  264.5 9.9 %collective-permute-start.19 = (f32[3,128]{1,0:T(4,128)S(1)}, f32[3,128]{1,0:T(4,128)S(1)}, u32[]{:S(2)}, u32[]{:S(2)}) collective-permute-start(f32[3,128]{1,0:T(4,128)S(1)} %fusion.50), channel_id=1, source_target_pairs={{0,12},{4,0},{8,4},{12,8},{16,28},{20,16},{24,20},{28,24},{32,44},... | collective-permute-start | bytes 4616 | tf_op jit(solution)/shard_map/ppermute | solution.py:46
  267.2 7.3 %collective-permute-start.18 = (f32[3,128]{1,0:T(4,128)S(1)}, f32[3,128]{1,0:T(4,128)S(1)}, u32[]{:S(2)}, u32[]{:S(2)}) collective-permute-start(f32[3,128]{1,0:T(4,128)S(1)} %fusion.50), channel_id=1, source_target_pairs={{0,8},{4,12},{8,0},{12,4},{16,24},{20,28},{24,16},{28,20},{32,40},... | collective-permute-start | bytes 4616 | tf_op jit(solution)/shard_map/ppermute | solution.py:46
  272.5 5.5 %collective-permute-start.17 = (f32[3,128]{1,0:T(4,128)S(1)}, f32[3,128]{1,0:T(4,128)S(1)}, u32[]{:S(2)}, u32[]{:S(2)}) collective-permute-start(f32[3,128]{1,0:T(4,128)S(1)} %fusion.50), channel_id=1, source_target_pairs={{0,4},{4,8},{8,12},{12,0},{16,20},{20,24},{24,28},{28,16},{32,36},... | collective-permute-start | bytes 4616 | tf_op jit(solution)/shard_map/ppermute | solution.py:46
  278.0 7.8 %collective-permute-start.22 = (f32[3,128]{1,0:T(4,128)S(1)}, f32[3,128]{1,0:T(4,128)S(1)}, u32[]{:S(2)}, u32[]{:S(2)}) collective-permute-start(f32[3,128]{1,0:T(4,128)S(1)} %fusion.49), channel_id=1, source_target_pairs={{0,48},{4,52},{8,56},{12,60},{16,0},{20,4},{24,8},{28,12},{32,16},... | collective-permute-start | bytes 4616 | tf_op jit(solution)/shard_map/ppermute | solution.py:46
  280.0 6.4 %collective-permute-start.21 = (f32[3,128]{1,0:T(4,128)S(1)}, f32[3,128]{1,0:T(4,128)S(1)}, u32[]{:S(2)}, u32[]{:S(2)}) collective-permute-start(f32[3,128]{1,0:T(4,128)S(1)} %fusion.49), channel_id=1, source_target_pairs={{0,32},{4,36},{8,40},{12,44},{16,48},{20,52},{24,56},{28,60},{32,0... | collective-permute-start | bytes 4616 | tf_op jit(solution)/shard_map/ppermute | solution.py:46
  281.9 7.8 %collective-permute-start.20 = (f32[3,128]{1,0:T(4,128)S(1)}, f32[3,128]{1,0:T(4,128)S(1)}, u32[]{:S(2)}, u32[]{:S(2)}) collective-permute-start(f32[3,128]{1,0:T(4,128)S(1)} %fusion.49), channel_id=1, source_target_pairs={{0,16},{4,20},{8,24},{12,28},{16,32},{20,36},{24,40},{28,44},{32,4... | collective-permute-start | bytes 4616 | tf_op jit(solution)/shard_map/ppermute | solution.py:46
  289.7 16.4 %collective-permute-start.25 = (f32[3,128]{1,0:T(4,128)S(1)}, f32[3,128]{1,0:T(4,128)S(1)}, u32[]{:S(2)}, u32[]{:S(2)}) collective-permute-start(f32[3,128]{1,0:T(4,128)S(1)} %fusion.48), channel_id=1, source_target_pairs={{0,192},{4,196},{8,200},{12,204},{16,208},{20,212},{24,216},{28,22... | collective-permute-start | bytes 4616 | tf_op jit(solution)/shard_map/ppermute | solution.py:46
  295.9 14.2 %collective-permute-start.24 = (f32[3,128]{1,0:T(4,128)S(1)}, f32[3,128]{1,0:T(4,128)S(1)}, u32[]{:S(2)}, u32[]{:S(2)}) collective-permute-start(f32[3,128]{1,0:T(4,128)S(1)} %fusion.48), channel_id=1, source_target_pairs={{0,128},{4,132},{8,136},{12,140},{16,144},{20,148},{24,152},{28,15... | collective-permute-start | bytes 4616 | tf_op jit(solution)/shard_map/ppermute | solution.py:46
  300.8 9.4 %collective-permute-start.23 = (f32[3,128]{1,0:T(4,128)S(1)}, f32[3,128]{1,0:T(4,128)S(1)}, u32[]{:S(2)}, u32[]{:S(2)}) collective-permute-start(f32[3,128]{1,0:T(4,128)S(1)} %fusion.48), channel_id=1, source_target_pairs={{0,64},{4,68},{8,72},{12,76},{16,80},{20,84},{24,88},{28,92},{32,9... | collective-permute-start | bytes 4616 | tf_op jit(solution)/shard_map/ppermute | solution.py:46
  310.8 3.3 %copy-start.3 = (f32[1,1,128]{2,1,0:T(1,128)}, f32[1,1,128]{2,1,0:T(1,128)S(1)}, u32[]{:S(2)}) copy-start(f32[1,1,128]{2,1,0:T(1,128)S(1)} %get-tuple-element.37) | copy-start | bytes 1540

commit v4 on v3

--- a/solution.py
+++ b/solution.py
@@ -19,7 +19,6 @@
 EPS_F = 1e-06
 
 LO = 128
-Q_BLOCK = 16
 
 
 def partner(shard, axis, apart):
@@ -44,6 +43,12 @@
         d = (i // stride) % radix
         perm.append((i, i + ((d + shift) % radix - d) * stride))
     return lax.ppermute(x, axis, perm)
+
+
+def butterfly_sum(x, axis):
+    for bit in range(lax.axis_size(axis).bit_length() - 1):
+        x = x + partner(x, axis, bit)
+    return x
 
 
 def digit_sum(x, axis):
@@ -63,24 +68,26 @@
     data = x
     for stride, radix in digits_of(lax.axis_size(axis)):
         d = (me // stride) % radix
-        data = data.reshape(data.shape[0] // radix, radix, data.shape[1])
-        total = lax.dynamic_index_in_dim(data, d, axis=1, keepdims=False)
+        data = data.reshape(data.shape[0], data.shape[1] // radix, radix, data.shape[2])
+        total = lax.dynamic_index_in_dim(data, d, axis=2, keepdims=False)
         for s in range(1, radix):
-            send = lax.dynamic_index_in_dim(data, (d + s) % radix, axis=1, keepdims=False)
+            send = lax.dynamic_index_in_dim(data, (d + s) % radix, axis=2, keepdims=False)
             total = total + shift_in_digit(send, axis, stride, radix, s)
         data = total
-    return data[0]
-
-
-def _project_kernel(val_ref, idx_ref, out_ref):
-    n = val_ref.shape[1]
+    return data[:, 0]
+
+
+def _project_kernel(val_ref, idx_ref, out_ref, vt_ref, it_ref):
+    n = val_ref.shape[0]
     hi_count = out_ref.shape[1]
+    vt_ref[...] = val_ref[...].T
+    it_ref[...] = idx_ref[...].T
     lo_iota = lax.broadcasted_iota(jnp.int32, (LO, n), 0)
     hi_iota = lax.broadcasted_iota(jnp.int32, (hi_count, n), 0)
 
     def body(q, carry):
-        v = val_ref[pl.ds(q, 1), :]
-        idx = idx_ref[pl.ds(q, 1), :]
+        v = vt_ref[pl.ds(q, 1), :]
+        idx = it_ref[pl.ds(q, 1), :]
         lo = jnp.bitwise_and(idx, LO - 1)
         hi = jnp.right_shift(idx, 7)
         rt = jnp.where(lo == lo_iota, 1.0, 0.0).astype(jnp.bfloat16)
@@ -93,27 +100,30 @@
         out_ref[q] = o[:hi_count] + o[hi_count:]
         return carry
 
-    lax.fori_loop(0, val_ref.shape[0], body, 0)
-
-
-def project(val_t, idx_t, bins):
-    q_count, n = val_t.shape
+    lax.fori_loop(0, IMG, body, 0)
+
+
+def project(val, idx, bins):
+    n, q_count = val.shape
     hi_count = bins // LO
     return pl.pallas_call(
         _project_kernel,
         out_shape=jax.ShapeDtypeStruct((q_count, hi_count, LO), jnp.float32),
-        grid=(q_count // Q_BLOCK,),
         in_specs=[
-            pl.BlockSpec((Q_BLOCK, n), lambda i: (i, 0)),
-            pl.BlockSpec((Q_BLOCK, n), lambda i: (i, 0)),
+            pl.BlockSpec(memory_space=pltpu.VMEM),
+            pl.BlockSpec(memory_space=pltpu.VMEM),
         ],
-        out_specs=pl.BlockSpec((Q_BLOCK, hi_count, LO), lambda i: (i, 0, 0)),
+        out_specs=pl.BlockSpec(memory_space=pltpu.VMEM),
+        scratch_shapes=[
+            pltpu.VMEM((q_count, n), jnp.float32),
+            pltpu.VMEM((q_count, n), jnp.int32),
+        ],
         cost_estimate=pl.CostEstimate(
             flops=2 * q_count * 2 * hi_count * LO * n,
             bytes_accessed=q_count * n * 8 + q_count * bins * 4,
             transcendentals=0,
         ),
-    )(val_t, idx_t)
+    )(val, idx)
 
 
 def shards(images, groups, references, interp_index, shell_index):
@@ -136,19 +146,9 @@
     outgoing = jnp.where(
         filled[:, None], jnp.take(images, source_ids, axis=0), jnp.zeros((), jnp.bfloat16)
     )
-    arrived = lax.all_to_all(
-        outgoing.reshape(n_cls, capacity, pix_quarter),
-        "cls",
-        split_axis=0,
-        concat_axis=0,
-        tiled=True,
-    )
-    arrived = arrived.reshape(slot_count, pix_quarter)
+    arrived = lax.all_to_all(outgoing, "cls", split_axis=0, concat_axis=0, tiled=True)
     quarter_rows = pix_quarter // IMG
     bins = VOXS // IMG
-    piece_rows = IMG // n_half
-    idx_t = interp_index.reshape(class_count * quarter_rows, IMG).T
-    idx_t = idx_t.reshape(n_half, piece_rows, -1).transpose(1, 0, 2).reshape(IMG, -1)
     shaped_refs = references.reshape(class_count, quarter_rows, IMG)
     rolled_refs = jnp.concatenate(
         [
@@ -177,12 +177,14 @@
     aligned = jnp.roll(weighted[0], -(SHIFTS // 2), axis=2)
     for shift_id in range(1, SHIFTS):
         aligned = aligned + jnp.roll(weighted[shift_id], shift_id - SHIFTS // 2, axis=2)
-    val_t = aligned.reshape(class_count * quarter_rows, IMG).T
-    val_t = val_t.reshape(n_half, piece_rows, -1).transpose(1, 0, 2).reshape(IMG, -1)
-    slab_part = project(val_t, idx_t, bins)
+    slab_part = project(
+        aligned.reshape(class_count * quarter_rows, IMG),
+        interp_index.reshape(class_count * quarter_rows, IMG),
+        bins,
+    )
     piece_len = VOXS // (n_half * n_cls)
-    slab_part = slab_part.reshape(n_cls, n_half * piece_len)
-    own_block = reduce_scatter(slab_part, "cls")
+    slab_part = slab_part.reshape(n_half, n_cls, piece_len)
+    own_block = reduce_scatter(slab_part, "cls").reshape(-1)
     half_id = lax.axis_index("half")
     other_block = partner(own_block, "half", 0)
     other_shell = partner(shell_index[0], "half", 0)
@@ -198,7 +200,7 @@
     )
     stats = jnp.stack([first_block * first_block, second_block * second_block, first_block * second_block])
     shell_terms = jnp.dot(stats, block_hot, precision=lax.Precision.HIGHEST)
-    shell_sums = digit_sum(digit_sum(shell_terms, "vol"), "cls")
+    shell_sums = butterfly_sum(butterfly_sum(shell_terms, "vol"), "cls")
     shell_fsc = shell_sums[2] / (jnp.sqrt(shell_sums[0]) * jnp.sqrt(shell_sums[1]) + EPS_F)
     mean_sq = (jnp.sum(shell_sums[0]) + jnp.sum(shell_sums[1]) + 2.0 * jnp.sum(shell_sums[2])) / (
         4.0 * n_vol * VOXS

time: 316 us -> 316 us (level)
  waiting for transfers between devices: 129 us -> 137 us
  starting transfers between devices: 109 us -> 103 us
  local copies, waits for them, and re-layouts: 29.7 us -> 24.1 us
    ppermute x24 -> x12, starting transfers between devices: 86.1 us -> 43.8 us  [shift_in_digit(): return lax.ppermute(x, axis, perm)]
    ppermute x2 -> x10, starting transfers between devices: 3.84 us -> 40 us  [partner(): lax.ppermute(shard, axis, [(i, i ^ 1 << apart) for i in range(lax.axis_si...]
    ppermute x2 -> x10, waiting for transfers between devices: 1.13 us -> 26.3 us  [partner(): lax.ppermute(shard, axis, [(i, i ^ 1 << apart) for i in range(lax.axis_si...]
    ppermute x24 -> x12, waiting for transfers between devices: 33.1 us -> 16 us  [shift_in_digit(): return lax.ppermute(x, axis, perm)]
    reshape x5 -> x2, local copies, waits for them, and re-layouts: 7.91 us -> 2.02 us  [the longest x1 1.95 us: shards(): interp_index.reshape(class_count * quarter_rows, IMG)]
    transpose x4 -> x0, local copies, waits for them, and re-layouts: 4.88 us -> none  [the longest x1 2.23 us: shards(): idx_t.reshape(n_half, piece_rows, -1).transpose(1, 0, 2).reshape(IMG, -1)]
  transfers between devices with their start and end apart: 27 -> 23, of which waited for: 14 -> 17; matrix products, arithmetic and copies ran while one was open for 4% -> 2% of each run, Pallas kernels for 0% -> 0%
where the time goes in v4:
time: 316 us; the launch traced here: 313 us
  waiting for transfers between devices  137 us (43%)
  starting transfers between devices  103 us (33%)
  Pallas kernels  28.9 us (9%)
  local copies, waits for them, and re-layouts  24.1 us (8%)
  other arithmetic  12.9 us (4%)
  matrix products  4.37 us (1%)
  between operations  3.44 us (1%)
    all_to_all x1, waiting for transfers between devices, shards(): lax.all_to_all(outgoing, 'cls', split_axis=0, concat_axis=0, tiled=True)  94.9 us
    ppermute x12, starting transfers between devices, shift_in_digit(): return lax.ppermute(x, axis, perm)  43.8 us
    ppermute x10, starting transfers between devices, partner(): lax.ppermute(shard, axis, [(i, i ^ 1 << apart) for i in range(lax.axis_si...  40 us
    pallas_call x1, Pallas kernels, project(): pl.pallas_call(_project_kernel, out_shape=jax.ShapeDtypeStruct((q_count,...  28.9 us
    ppermute x10, waiting for transfers between devices, partner(): lax.ppermute(shard, axis, [(i, i ^ 1 << apart) for i in range(lax.axis_si...  26.3 us
    all_to_all x1, starting transfers between devices, shards(): lax.all_to_all(outgoing, 'cls', split_axis=0, concat_axis=0, tiled=True)  18.9 us
    ppermute x12, waiting for transfers between devices, shift_in_digit(): return lax.ppermute(x, axis, perm)  16 us
  transfers between devices with their start and end apart: 23, of which 17 were waited for; matrix products, arithmetic and copies ran while one was open for 2% of the time, Pallas kernels for 0%

profile of v4, /device:TPU:6, one launch (start us, length us, event | category | flops | bytes accessed | tf_op | source)
XLA Modules:
  0.0 313.4 jit_solution(12390593023619620392)
XLA Ops:
  0.6 0.8 fusion.17
  1.6 0.8 select_reduce_fusion.1
  3.5 1.8 gather_fusion
  5.4 2.2 gather.7
  7.8 3.7 %select_select_fusion = bf16[64,4,4096]{2,1,0:T(4,128)(2,1)} fusion(bf16[64,4,4096]{2,1,0:T(4,128)(2,1)} %gather.7, pred[64,4]{1,0:T(8,128)(4,1)S(1)} %compare_and_fusion, pred[64,4]{1,0:T(8,128)(4,1)S(1)} %broadcast_in_dim.48), kind=kLoop, calls=%fused_computation.2 | loop fusion | flops 2097152 | bytes 4194816 | tf_op jit(solution)/shard_map/jit(_where)/select_n | solution.py:146
  11.5 18.9 %all-to-all-start = ((bf16[64,4,4096]{2,1,0:T(4,128)(2,1)}), bf16[64,4,4096]{2,1,0:T(4,128)(2,1)}, u32[]{:S(2)}, u32[]{:S(2)}) async-start(bf16[64,4,4096]{2,1,0:T(4,128)(2,1)} %select_select_fusion), calls=%async_computation | async-start | bytes 4194304 | tf_op jit(solution)/shard_map/all_to_all | solution.py:149
  31.6 0.8 bitcast_dynamic-update-slice_fusion.3
  32.4 0.8 bitcast_dynamic-update-slice_fusion.2
  33.9 0.8 bitcast_dynamic-update-slice_fusion.1
  34.7 0.8 bitcast_dynamic-update-slice_fusion
  35.5 94.9 %all-to-all-done = bf16[64,4,4096]{2,1,0:T(4,128)(2,1)} async-done(((bf16[64,4,4096]{2,1,0:T(4,128)(2,1)}), bf16[64,4,4096]{2,1,0:T(4,128)(2,1)}, u32[]{:S(2)}, u32[]{:S(2)}) %all-to-all-start) | async-done | bytes 2097184 | tf_op jit(solution)/shard_map/all_to_all | solution.py:149
  130.5 2.5 all_to_all.7
  133.0 2.2 fusion.27
  135.2 3.5 %collective-permute-start = (f32[256,5,32]{0,2,1:T(8,128)S(1)}, f32[256,5,32]{0,2,1:T(8,128)S(1)}, u32[]{:S(2)}, u32[]{:S(2)}) collective-permute-start(f32[256,5,32]{0,2,1:T(8,128)S(1)} %bitcast.115), channel_id=1, source_target_pairs={{0,1},{1,2},{2,3},{3,0},{4,5},{5,6},{6,7},{7,4},{8,9},{9,10},{10,1... | collective-permute-start | bytes 491528 | tf_op jit(solution)/shard_map/ppermute | solution.py:45
  138.7 4.8 %collective-permute-start.1 = (f32[256,5,32]{0,2,1:T(8,128)S(1)}, f32[256,5,32]{0,2,1:T(8,128)}, u32[]{:S(2)}, u32[]{:S(2)}) collective-permute-start(f32[256,5,32]{0,2,1:T(8,128)S(1)} %bitcast.116), channel_id=1, source_target_pairs={{0,2},{1,3},{2,0},{3,1},{4,6},{5,7},{6,4},{7,5},{8,10},{9,11},{10,... | collective-permute-start | bytes 491528 | tf_op jit(solution)/shard_map/ppermute | solution.py:45
  143.5 3.3 %collective-permute-start.2 = (f32[256,5,32]{0,2,1:T(8,128)S(1)}, f32[256,5,32]{0,2,1:T(8,128)}, u32[]{:S(2)}, u32[]{:S(2)}) collective-permute-start(f32[256,5,32]{0,2,1:T(8,128)S(1)} %bitcast.117), channel_id=1, source_target_pairs={{0,3},{1,0},{2,1},{3,2},{4,7},{5,4},{6,5},{7,6},{8,11},{9,8},{10,9... | collective-permute-start | bytes 491528 | tf_op jit(solution)/shard_map/ppermute | solution.py:45
  146.9 1.9 reshape.176.idx_ref
  148.9 1.9 collective-permute-done.2
  150.8 1.0 pad_maximum_fusion
  152.5 1.0 slice_bitcast_fusion
  153.6 1.0 slice.131
  154.7 1.0 slice.134
  155.8 1.0 slice.138
  156.9 1.0 slice.141
  157.9 1.9 squeeze.77
  159.8 3.1 fusion.5.val_ref
  162.9 28.9 %shard_map.68 = f32[128,16,128]{2,1,0:T(8,128)} custom-call(f32[1024,128]{1,0:T(8,128)} %fusion.5.val_ref, s32[1024,128]{1,0:T(8,128)} %reshape.176.idx_ref), custom_call_target="tpu_custom_call" | custom-call | flops 1073741824 | bytes 2097152 | tf_op jit(solution)/shard_map/pallas_call | solution.py:109
  191.8 1.6 reshape_reshape.3
  193.3 1.1 constant_dynamic-slice_fusion.9
  194.6 2.4 collective-permute-start.3
  197.1 4.3 %collective-permute-start.4 = (f32[2,16,2048]{2,1,0:T(8,128)S(1)}, f32[2,16,2048]{2,1,0:T(8,128)S(1)}, u32[]{:S(2)}, u32[]{:S(2)}) collective-permute-start(f32[2,16,2048]{2,1,0:T(8,128)S(1)} %bitcast.121), channel_id=1, source_target_pairs={{0,8},{4,12},{8,0},{12,4},{16,24},{20,28},{24,16},{28,20},{32,40},... | collective-permute-start | bytes 786440 | tf_op jit(solution)/shard_map/ppermute | solution.py:45
  201.5 2.1 collective-permute-start.5
  203.7 1.3 collective-permute-done.3
  205.0 4.6 %collective-permute-done.4 = f32[2,16,2048]{2,1,0:T(8,128)S(1)} collective-permute-done((f32[2,16,2048]{2,1,0:T(8,128)S(1)}, f32[2,16,2048]{2,1,0:T(8,128)S(1)}, u32[]{:S(2)}, u32[]{:S(2)}) %collective-permute-start.4) | collective-permute-done | bytes 262176 | tf_op jit(solution)/shard_map/ppermute | solution.py:45
  209.6 2.1 collective-permute-done.5
  212.2 2.9 collective-permute-start.6
  215.1 2.8 collective-permute-start.7
  218.0 3.8 %collective-permute-start.8 = (f32[2,4,2048]{2,1,0:T(4,128)S(1)}, f32[2,4,2048]{2,1,0:T(4,128)S(1)}, u32[]{:S(2)}, u32[]{:S(2)}) collective-permute-start(f32[2,4,2048]{2,1,0:T(4,128)S(1)} %bitcast.126), channel_id=1, source_target_pairs={{0,48},{4,52},{8,56},{12,60},{16,0},{20,4},{24,8},{28,12},{32,16},... | collective-permute-start | bytes 196616 | tf_op jit(solution)/shard_map/ppermute | solution.py:45
  221.9 0.9 collective-permute-done.7
  222.8 1.8 collective-permute-done.8
  224.7 4.1 %collective-permute-start.10 = (f32[2,1,2048]{2,1,0:T(1,128)S(1)}, f32[2,1,2048]{2,1,0:T(1,128)S(1)}, u32[]{:S(2)}, u32[]{:S(2)}) collective-permute-start(f32[2,1,2048]{2,1,0:T(1,128)S(1)} %get-tuple-element.34), channel_id=1, source_target_pairs={{0,128},{4,132},{8,136},{12,140},{16,144},{20,148},{24,152},{28,15... | collective-permute-start | bytes 49160 | tf_op jit(solution)/shard_map/ppermute | solution.py:45
  228.8 5.5 %collective-permute-start.11 = (f32[2,1,2048]{2,1,0:T(1,128)S(1)}, f32[2,1,2048]{2,1,0:T(1,128)S(1)}, u32[]{:S(2)}, u32[]{:S(2)}) collective-permute-start(f32[2,1,2048]{2,1,0:T(1,128)S(1)} %get-tuple-element.33), channel_id=1, source_target_pairs={{0,192},{4,196},{8,200},{12,204},{16,208},{20,212},{24,216},{28,22... | collective-permute-start | bytes 49160 | tf_op jit(solution)/shard_map/ppermute | solution.py:45
  234.3 4.2 %collective-permute-start.9 = (f32[2,1,2048]{2,1,0:T(1,128)S(1)}, f32[2,1,2048]{2,1,0:T(1,128)S(1)}, u32[]{:S(2)}, u32[]{:S(2)}) collective-permute-start(f32[2,1,2048]{2,1,0:T(1,128)S(1)} %get-tuple-element.32), channel_id=1, source_target_pairs={{0,64},{4,68},{8,72},{12,76},{16,80},{20,84},{24,88},{28,92},{32,9... | collective-permute-start | bytes 49160 | tf_op jit(solution)/shard_map/ppermute | solution.py:45
  238.6 1.9 collective-permute-start.13
  240.5 3.3 %collective-permute-done.9 = f32[2,1,2048]{2,1,0:T(1,128)S(1)} collective-permute-done((f32[2,1,2048]{2,1,0:T(1,128)S(1)}, f32[2,1,2048]{2,1,0:T(1,128)S(1)}, u32[]{:S(2)}, u32[]{:S(2)}) %collective-permute-start.9) | collective-permute-done | bytes 16416 | tf_op jit(solution)/shard_map/ppermute | solution.py:45
  243.9 1.9 collective-permute-start.12
  245.9 1.1 collective-permute-done.12
  247.0 1.0 fusion
  248.0 5.1 %collective-permute-start.14 = (f32[3,128]{1,0:T(4,128)S(1)}, f32[3,128]{1,0:T(4,128)S(1)}, u32[]{:S(2)}, u32[]{:S(2)}) collective-permute-start(f32[3,128]{1,0:T(4,128)S(1)} %fusion), channel_id=1, source_target_pairs={{0,1},{1,0},{2,3},{3,2},{4,5},{5,4},{6,7},{7,6},{8,9},{9,8},{10,11... | collective-permute-start | bytes 4616 | tf_op jit(solution)/shard_map/ppermute | solution.py:25
  253.1 1.5 collective-permute-done.14
  254.6 3.7 %collective-permute-start.15 = (f32[3,128]{1,0:T(4,128)S(1)}, f32[3,128]{1,0:T(4,128)S(1)}, u32[]{:S(2)}, u32[]{:S(2)}) collective-permute-start(f32[3,128]{1,0:T(4,128)S(1)} %add.358), channel_id=1, source_target_pairs={{0,2},{1,3},{2,0},{3,1},{4,6},{5,7},{6,4},{7,5},{8,10},{9,11},{10,... | collective-permute-start | bytes 4616 | tf_op jit(solution)/shard_map/ppermute | solution.py:25
  258.3 3.3 %collective-permute-done.15 = f32[3,128]{1,0:T(4,128)S(1)} collective-permute-done((f32[3,128]{1,0:T(4,128)S(1)}, f32[3,128]{1,0:T(4,128)S(1)}, u32[]{:S(2)}, u32[]{:S(2)}) %collective-permute-start.15) | collective-permute-done | bytes 1568 | tf_op jit(solution)/shard_map/ppermute | solution.py:25
  261.6 2.8 collective-permute-start.16
  264.4 2.7 collective-permute-done.16
  267.1 4.7 %collective-permute-start.17 = (f32[3,128]{1,0:T(4,128)S(1)}, f32[3,128]{1,0:T(4,128)S(1)}, u32[]{:S(2)}, u32[]{:S(2)}) collective-permute-start(f32[3,128]{1,0:T(4,128)S(1)} %add.360), channel_id=1, source_target_pairs={{0,8},{4,12},{8,0},{12,4},{16,24},{20,28},{24,16},{28,20},{32,40},... | collective-permute-start | bytes 4616 | tf_op jit(solution)/shard_map/ppermute | solution.py:25
  271.8 2.2 collective-permute-done.17
  274.0 3.5 %collective-permute-start.18 = (f32[3,128]{1,0:T(4,128)S(1)}, f32[3,128]{1,0:T(4,128)S(1)}, u32[]{:S(2)}, u32[]{:S(2)}) collective-permute-start(f32[3,128]{1,0:T(4,128)S(1)} %add.361), channel_id=1, source_target_pairs={{0,16},{4,20},{8,24},{12,28},{16,0},{20,4},{24,8},{28,12},{32,48},... | collective-permute-start | bytes 4616 | tf_op jit(solution)/shard_map/ppermute | solution.py:25
  277.5 2.0 collective-permute-done.18
  279.5 4.6 %collective-permute-start.19 = (f32[3,128]{1,0:T(4,128)S(1)}, f32[3,128]{1,0:T(4,128)S(1)}, u32[]{:S(2)}, u32[]{:S(2)}) collective-permute-start(f32[3,128]{1,0:T(4,128)S(1)} %add.362), channel_id=1, source_target_pairs={{0,32},{4,36},{8,40},{12,44},{16,48},{20,52},{24,56},{28,60},{32,0... | collective-permute-start | bytes 4616 | tf_op jit(solution)/shard_map/ppermute | solution.py:25
  284.1 1.8 collective-permute-done.19
  285.9 4.3 %collective-permute-start.20 = (f32[3,128]{1,0:T(4,128)S(1)}, f32[3,128]{1,0:T(4,128)S(1)}, u32[]{:S(2)}, u32[]{:S(2)}) collective-permute-start(f32[3,128]{1,0:T(4,128)S(1)} %add.363), channel_id=1, source_target_pairs={{0,64},{4,68},{8,72},{12,76},{16,80},{20,84},{24,88},{28,92},{32,9... | collective-permute-start | bytes 4616 | tf_op jit(solution)/shard_map/ppermute | solution.py:25
  290.2 5.0 %collective-permute-done.20 = f32[3,128]{1,0:T(4,128)S(1)} collective-permute-done((f32[3,128]{1,0:T(4,128)S(1)}, f32[3,128]{1,0:T(4,128)S(1)}, u32[]{:S(2)}, u32[]{:S(2)}) %collective-permute-start.20) | collective-permute-done | bytes 1568 | tf_op jit(solution)/shard_map/ppermute | solution.py:25
  295.3 7.4 %collective-permute-start.21 = (f32[3,128]{1,0:T(4,128)S(1)}, f32[3,128]{1,0:T(4,128)S(1)}, u32[]{:S(2)}, u32[]{:S(2)}) collective-permute-start(f32[3,128]{1,0:T(4,128)S(1)} %add.364), channel_id=1, source_target_pairs={{0,128},{4,132},{8,136},{12,140},{16,144},{20,148},{24,152},{28,15... | collective-permute-start | bytes 4616 | tf_op jit(solution)/shard_map/ppermute | solution.py:25
  302.7 6.7 %collective-permute-done.21 = f32[3,128]{1,0:T(4,128)S(1)} collective-permute-done((f32[3,128]{1,0:T(4,128)S(1)}, f32[3,128]{1,0:T(4,128)S(1)}, u32[]{:S(2)}, u32[]{:S(2)}) %collective-permute-start.21) | collective-permute-done | bytes 1568 | tf_op jit(solution)/shard_map/ppermute | solution.py:25
  (68 shorter events, 7.3 us)
Async XLA Ops:
  0.6 2.9 copy-start
  11.5 18.9 %copy-start.1 = (bf16[32,4096]{1,0:T(8,128)(2,1)S(1)}, bf16[32,4096]{1,0:T(8,128)(2,1)}, u32[]{:S(2)}) copy-start(bf16[32,4096]{1,0:T(8,128)(2,1)} %param.7) | copy-start | bytes 786436
  11.5 119.0 %all-to-all-start = ((bf16[64,4,4096]{2,1,0:T(4,128)(2,1)}), bf16[64,4,4096]{2,1,0:T(4,128)(2,1)}, u32[]{:S(2)}, u32[]{:S(2)}) async-start(bf16[64,4,4096]{2,1,0:T(4,128)(2,1)} %select_select_fusion), calls=%async_computation | async-start | bytes 4194304 | tf_op jit(solution)/shard_map/all_to_all | solution.py:149
  135.2 13.7 %collective-permute-start = (f32[256,5,32]{0,2,1:T(8,128)S(1)}, f32[256,5,32]{0,2,1:T(8,128)S(1)}, u32[]{:S(2)}, u32[]{:S(2)}) collective-permute-start(f32[256,5,32]{0,2,1:T(8,128)S(1)} %bitcast.115), channel_id=1, source_target_pairs={{0,1},{1,2},{2,3},{3,0},{4,5},{5,6},{6,7},{7,4},{8,9},{9,10},{10,1... | collective-permute-start | bytes 491528 | tf_op jit(solution)/shard_map/ppermute | solution.py:45
  138.7 10.2 %collective-permute-start.1 = (f32[256,5,32]{0,2,1:T(8,128)S(1)}, f32[256,5,32]{0,2,1:T(8,128)}, u32[]{:S(2)}, u32[]{:S(2)}) collective-permute-start(f32[256,5,32]{0,2,1:T(8,128)S(1)} %bitcast.116), channel_id=1, source_target_pairs={{0,2},{1,3},{2,0},{3,1},{4,6},{5,7},{6,4},{7,5},{8,10},{9,11},{10,... | collective-permute-start | bytes 491528 | tf_op jit(solution)/shard_map/ppermute | solution.py:45
  143.5 7.3 %collective-permute-start.2 = (f32[256,5,32]{0,2,1:T(8,128)S(1)}, f32[256,5,32]{0,2,1:T(8,128)}, u32[]{:S(2)}, u32[]{:S(2)}) collective-permute-start(f32[256,5,32]{0,2,1:T(8,128)S(1)} %bitcast.117), channel_id=1, source_target_pairs={{0,3},{1,0},{2,1},{3,2},{4,7},{5,4},{6,5},{7,6},{8,11},{9,8},{10,9... | collective-permute-start | bytes 491528 | tf_op jit(solution)/shard_map/ppermute | solution.py:45
  194.6 10.5 %collective-permute-start.3 = (f32[2,16,2048]{2,1,0:T(8,128)S(1)}, f32[2,16,2048]{2,1,0:T(8,128)S(1)}, u32[]{:S(2)}, u32[]{:S(2)}) collective-permute-start(f32[2,16,2048]{2,1,0:T(8,128)S(1)} %bitcast.120), channel_id=1, source_target_pairs={{0,4},{4,8},{8,12},{12,0},{16,20},{20,24},{24,28},{28,16},{32,36},... | collective-permute-start | bytes 786440 | tf_op jit(solution)/shard_map/ppermute | solution.py:45
  197.1 41.5 %copy-start.2 = (s32[1,2048]{1,0:T(1,128)S(1)}, s32[1,2048]{1,0:T(1,128)}, u32[]{:S(2)}) copy-start(s32[1,2048]{1,0:T(1,128)} %param.9) | copy-start | bytes 24580
  197.1 12.5 %collective-permute-start.4 = (f32[2,16,2048]{2,1,0:T(8,128)S(1)}, f32[2,16,2048]{2,1,0:T(8,128)S(1)}, u32[]{:S(2)}, u32[]{:S(2)}) collective-permute-start(f32[2,16,2048]{2,1,0:T(8,128)S(1)} %bitcast.121), channel_id=1, source_target_pairs={{0,8},{4,12},{8,0},{12,4},{16,24},{20,28},{24,16},{28,20},{32,40},... | collective-permute-start | bytes 786440 | tf_op jit(solution)/shard_map/ppermute | solution.py:45
  201.5 10.2 %collective-permute-start.5 = (f32[2,16,2048]{2,1,0:T(8,128)S(1)}, f32[2,16,2048]{2,1,0:T(8,128)S(1)}, u32[]{:S(2)}, u32[]{:S(2)}) collective-permute-start(f32[2,16,2048]{2,1,0:T(8,128)S(1)} %bitcast.122), channel_id=1, source_target_pairs={{0,12},{4,0},{8,4},{12,8},{16,28},{20,16},{24,20},{28,24},{32,44},... | collective-permute-start | bytes 786440 | tf_op jit(solution)/shard_map/ppermute | solution.py:45
  212.2 9.7 %collective-permute-start.6 = (f32[2,4,2048]{2,1,0:T(4,128)S(1)}, f32[2,4,2048]{2,1,0:T(4,128)S(1)}, u32[]{:S(2)}, u32[]{:S(2)}) collective-permute-start(f32[2,4,2048]{2,1,0:T(4,128)S(1)} %bitcast.124), channel_id=1, source_target_pairs={{0,16},{4,20},{8,24},{12,28},{16,32},{20,36},{24,40},{28,44},{32,4... | collective-permute-start | bytes 196616 | tf_op jit(solution)/shard_map/ppermute | solution.py:45
  215.1 7.7 %collective-permute-start.7 = (f32[2,4,2048]{2,1,0:T(4,128)S(1)}, f32[2,4,2048]{2,1,0:T(4,128)S(1)}, u32[]{:S(2)}, u32[]{:S(2)}) collective-permute-start(f32[2,4,2048]{2,1,0:T(4,128)S(1)} %bitcast.125), channel_id=1, source_target_pairs={{0,32},{4,36},{8,40},{12,44},{16,48},{20,52},{24,56},{28,60},{32,0... | collective-permute-start | bytes 196616 | tf_op jit(solution)/shard_map/ppermute | solution.py:45
  218.0 6.6 %collective-permute-start.8 = (f32[2,4,2048]{2,1,0:T(4,128)S(1)}, f32[2,4,2048]{2,1,0:T(4,128)S(1)}, u32[]{:S(2)}, u32[]{:S(2)}) collective-permute-start(f32[2,4,2048]{2,1,0:T(4,128)S(1)} %bitcast.126), channel_id=1, source_target_pairs={{0,48},{4,52},{8,56},{12,60},{16,0},{20,4},{24,8},{28,12},{32,16},... | collective-permute-start | bytes 196616 | tf_op jit(solution)/shard_map/ppermute | solution.py:45
  224.7 15.8 %collective-permute-start.10 = (f32[2,1,2048]{2,1,0:T(1,128)S(1)}, f32[2,1,2048]{2,1,0:T(1,128)S(1)}, u32[]{:S(2)}, u32[]{:S(2)}) collective-permute-start(f32[2,1,2048]{2,1,0:T(1,128)S(1)} %get-tuple-element.34), channel_id=1, source_target_pairs={{0,128},{4,132},{8,136},{12,140},{16,144},{20,148},{24,152},{28,15... | collective-permute-start | bytes 49160 | tf_op jit(solution)/shard_map/ppermute | solution.py:45
  228.8 11.7 %collective-permute-start.11 = (f32[2,1,2048]{2,1,0:T(1,128)S(1)}, f32[2,1,2048]{2,1,0:T(1,128)S(1)}, u32[]{:S(2)}, u32[]{:S(2)}) collective-permute-start(f32[2,1,2048]{2,1,0:T(1,128)S(1)} %get-tuple-element.33), channel_id=1, source_target_pairs={{0,192},{4,196},{8,200},{12,204},{16,208},{20,212},{24,216},{28,22... | collective-permute-start | bytes 49160 | tf_op jit(solution)/shard_map/ppermute | solution.py:45
  234.3 9.6 %collective-permute-start.9 = (f32[2,1,2048]{2,1,0:T(1,128)S(1)}, f32[2,1,2048]{2,1,0:T(1,128)S(1)}, u32[]{:S(2)}, u32[]{:S(2)}) collective-permute-start(f32[2,1,2048]{2,1,0:T(1,128)S(1)} %get-tuple-element.32), channel_id=1, source_target_pairs={{0,64},{4,68},{8,72},{12,76},{16,80},{20,84},{24,88},{28,92},{32,9... | collective-permute-start | bytes 49160 | tf_op jit(solution)/shard_map/ppermute | solution.py:45
  238.6 7.3 %collective-permute-start.13 = (s32[2048]{0:T(1024)S(1)}, s32[2048]{0:T(1024)S(1)}, u32[]{:S(2)}, u32[]{:S(2)}) collective-permute-start(s32[2048]{0:T(1024)S(1)} %bitcast.135), channel_id=1, source_target_pairs={{0,256},{256,0},{1,257},{257,1},{2,258},{258,2},{3,259},{259,3},{4... | collective-permute-start | bytes 24584 | tf_op jit(solution)/shard_map/ppermute | solution.py:25
  243.9 3.1 collective-permute-start.12
  248.0 6.6 %collective-permute-start.14 = (f32[3,128]{1,0:T(4,128)S(1)}, f32[3,128]{1,0:T(4,128)S(1)}, u32[]{:S(2)}, u32[]{:S(2)}) collective-permute-start(f32[3,128]{1,0:T(4,128)S(1)} %fusion), channel_id=1, source_target_pairs={{0,1},{1,0},{2,3},{3,2},{4,5},{5,4},{6,7},{7,6},{8,9},{9,8},{10,11... | collective-permute-start | bytes 4616 | tf_op jit(solution)/shard_map/ppermute | solution.py:25
  254.6 7.0 %collective-permute-start.15 = (f32[3,128]{1,0:T(4,128)S(1)}, f32[3,128]{1,0:T(4,128)S(1)}, u32[]{:S(2)}, u32[]{:S(2)}) collective-permute-start(f32[3,128]{1,0:T(4,128)S(1)} %add.358), channel_id=1, source_target_pairs={{0,2},{1,3},{2,0},{3,1},{4,6},{5,7},{6,4},{7,5},{8,10},{9,11},{10,... | collective-permute-start | bytes 4616 | tf_op jit(solution)/shard_map/ppermute | solution.py:25
  261.6 5.5 %collective-permute-start.16 = (f32[3,128]{1,0:T(4,128)S(1)}, f32[3,128]{1,0:T(4,128)S(1)}, u32[]{:S(2)}, u32[]{:S(2)}) collective-permute-start(f32[3,128]{1,0:T(4,128)S(1)} %add.359), channel_id=1, source_target_pairs={{0,4},{4,0},{8,12},{12,8},{16,20},{20,16},{24,28},{28,24},{32,36},... | collective-permute-start | bytes 4616 | tf_op jit(solution)/shard_map/ppermute | solution.py:25
  267.1 7.0 %collective-permute-start.17 = (f32[3,128]{1,0:T(4,128)S(1)}, f32[3,128]{1,0:T(4,128)S(1)}, u32[]{:S(2)}, u32[]{:S(2)}) collective-permute-start(f32[3,128]{1,0:T(4,128)S(1)} %add.360), channel_id=1, source_target_pairs={{0,8},{4,12},{8,0},{12,4},{16,24},{20,28},{24,16},{28,20},{32,40},... | collective-permute-start | bytes 4616 | tf_op jit(solution)/shard_map/ppermute | solution.py:25
  274.0 5.5 %collective-permute-start.18 = (f32[3,128]{1,0:T(4,128)S(1)}, f32[3,128]{1,0:T(4,128)S(1)}, u32[]{:S(2)}, u32[]{:S(2)}) collective-permute-start(f32[3,128]{1,0:T(4,128)S(1)} %add.361), channel_id=1, source_target_pairs={{0,16},{4,20},{8,24},{12,28},{16,0},{20,4},{24,8},{28,12},{32,48},... | collective-permute-start | bytes 4616 | tf_op jit(solution)/shard_map/ppermute | solution.py:25
  279.5 6.4 %collective-permute-start.19 = (f32[3,128]{1,0:T(4,128)S(1)}, f32[3,128]{1,0:T(4,128)S(1)}, u32[]{:S(2)}, u32[]{:S(2)}) collective-permute-start(f32[3,128]{1,0:T(4,128)S(1)} %add.362), channel_id=1, source_target_pairs={{0,32},{4,36},{8,40},{12,44},{16,48},{20,52},{24,56},{28,60},{32,0... | collective-permute-start | bytes 4616 | tf_op jit(solution)/shard_map/ppermute | solution.py:25
  285.9 9.4 %collective-permute-start.20 = (f32[3,128]{1,0:T(4,128)S(1)}, f32[3,128]{1,0:T(4,128)S(1)}, u32[]{:S(2)}, u32[]{:S(2)}) collective-permute-start(f32[3,128]{1,0:T(4,128)S(1)} %add.363), channel_id=1, source_target_pairs={{0,64},{4,68},{8,72},{12,76},{16,80},{20,84},{24,88},{28,92},{32,9... | collective-permute-start | bytes 4616 | tf_op jit(solution)/shard_map/ppermute | solution.py:25
  295.3 14.2 %collective-permute-start.21 = (f32[3,128]{1,0:T(4,128)S(1)}, f32[3,128]{1,0:T(4,128)S(1)}, u32[]{:S(2)}, u32[]{:S(2)}) collective-permute-start(f32[3,128]{1,0:T(4,128)S(1)} %add.364), channel_id=1, source_target_pairs={{0,128},{4,132},{8,136},{12,140},{16,144},{20,148},{24,152},{28,15... | collective-permute-start | bytes 4616 | tf_op jit(solution)/shard_map/ppermute | solution.py:25
  310.1 3.3 %copy-start.3 = (f32[1,128]{1,0:T(1,128)}, f32[1,128]{1,0:T(1,128)S(1)}, u32[]{:S(2)}) copy-start(f32[1,128]{1,0:T(1,128)S(1)} %get-tuple-element.37) | copy-start | bytes 1540

commit v5 on v4

--- a/solution.py
+++ b/solution.py
@@ -49,6 +49,15 @@
     for bit in range(lax.axis_size(axis).bit_length() - 1):
         x = x + partner(x, axis, bit)
     return x
+
+
+def exchange_sum(x, axis):
+    n = lax.axis_size(axis)
+    got = lax.all_to_all(jnp.broadcast_to(x[None], (n,) + x.shape), axis, 0, 0, tiled=True)
+    total = got[0]
+    for i in range(1, n):
+        total = total + got[i]
+    return total
 
 
 def digit_sum(x, axis):
@@ -163,7 +172,7 @@
         arrived, rolled_refs, (((1,), (1,)), ((), ())), preferred_element_type=jnp.float32
     )
     partial_scores = partial_scores.reshape(slot_count, SHIFTS, class_count)
-    scores = digit_sum(partial_scores, "vol")
+    scores = exchange_sum(partial_scores, "vol")
     squares = scores * scores
     mean_square = jnp.mean(squares, axis=(1, 2), keepdims=True)
     weights = (squares / (mean_square + EPS_W)).astype(jnp.bfloat16)
@@ -200,7 +209,7 @@
     )
     stats = jnp.stack([first_block * first_block, second_block * second_block, first_block * second_block])
     shell_terms = jnp.dot(stats, block_hot, precision=lax.Precision.HIGHEST)
-    shell_sums = butterfly_sum(butterfly_sum(shell_terms, "vol"), "cls")
+    shell_sums = exchange_sum(exchange_sum(shell_terms, "vol"), "cls")
     shell_fsc = shell_sums[2] / (jnp.sqrt(shell_sums[0]) * jnp.sqrt(shell_sums[1]) + EPS_F)
     mean_sq = (jnp.sum(shell_sums[0]) + jnp.sum(shell_sums[1]) + 2.0 * jnp.sum(shell_sums[2])) / (
         4.0 * n_vol * VOXS

time: 316 us -> 292 us (0.924)
  starting transfers between devices: 103 us -> 73.6 us
  blocking collectives: 0 us -> 7.66 us
  waiting for transfers between devices: 137 us -> 130 us
    ppermute x10 -> x2, starting transfers between devices: 40 us -> 3.84 us  [partner(): lax.ppermute(shard, axis, [(i, i ^ 1 << apart) for i in range(lax.axis_si...]
    ppermute x10 -> x2, waiting for transfers between devices: 26.3 us -> 1.13 us  [partner(): lax.ppermute(shard, axis, [(i, i ^ 1 << apart) for i in range(lax.axis_si...]
    all_to_all x0 -> x2, waiting for transfers between devices: none -> 20.7 us  [exchange_sum(): lax.all_to_all(jnp.broadcast_to(x[None], (n,) + x.shape), axis, 0, 0, til...]
    all_to_all x0 -> x2, starting transfers between devices: none -> 17.6 us  [exchange_sum(): lax.all_to_all(jnp.broadcast_to(x[None], (n,) + x.shape), axis, 0, 0, til...]
    ppermute x12 -> x9, starting transfers between devices: 43.8 us -> 33.4 us  [shift_in_digit(): return lax.ppermute(x, axis, perm)]
    all_to_all x0 -> x1, blocking collectives: none -> 7.66 us  [exchange_sum(): lax.all_to_all(jnp.broadcast_to(x[None], (n,) + x.shape), axis, 0, 0, til...]
    another operation x0 -> x2, local copies, waits for them, and re-layouts: none -> 4.11 us
    ppermute x12 -> x9, waiting for transfers between devices: 16 us -> 13.2 us  [shift_in_digit(): return lax.ppermute(x, axis, perm)]
  transfers between devices with their start and end apart: 23 -> 14, of which waited for: 17 -> 11; matrix products, arithmetic and copies ran while one was open for 2% -> 3% of each run, Pallas kernels for 0% -> 0%
where the time goes in v5:
time: 292 us; the launch traced here: 290 us
  waiting for transfers between devices  130 us (45%)
  starting transfers between devices  73.6 us (25%)
  Pallas kernels  28.8 us (10%)
  local copies, waits for them, and re-layouts  27.2 us (9%)
  other arithmetic  13 us (4%)
  blocking collectives  7.66 us (3%)
  matrix products  6.58 us (2%)
  between operations  3.21 us (1%)
    all_to_all x1, waiting for transfers between devices, shards(): lax.all_to_all(outgoing, 'cls', split_axis=0, concat_axis=0, tiled=True)  95 us
    ppermute x9, starting transfers between devices, shift_in_digit(): return lax.ppermute(x, axis, perm)  33.4 us
    pallas_call x1, Pallas kernels, project(): pl.pallas_call(_project_kernel, out_shape=jax.ShapeDtypeStruct((q_count,...  28.8 us
    all_to_all x2, waiting for transfers between devices, exchange_sum(): lax.all_to_all(jnp.broadcast_to(x[None], (n,) + x.shape), axis, 0, 0, til...  20.7 us
    all_to_all x1, starting transfers between devices, shards(): lax.all_to_all(outgoing, 'cls', split_axis=0, concat_axis=0, tiled=True)  18.7 us
    all_to_all x2, starting transfers between devices, exchange_sum(): lax.all_to_all(jnp.broadcast_to(x[None], (n,) + x.shape), axis, 0, 0, til...  17.6 us
    ppermute x9, waiting for transfers between devices, shift_in_digit(): return lax.ppermute(x, axis, perm)  13.2 us
    all_to_all x1, blocking collectives, exchange_sum(): lax.all_to_all(jnp.broadcast_to(x[None], (n,) + x.shape), axis, 0, 0, til...  7.66 us
  transfers between devices with their start and end apart: 14, of which 11 were waited for; matrix products, arithmetic and copies ran while one was open for 3% of the time, Pallas kernels for 0%

profile of v5, /device:TPU:6, one launch (start us, length us, event | category | flops | bytes accessed | tf_op | source)
XLA Modules:
  0.0 290.2 jit_solution(13269988916057051407)
XLA Ops:
  0.6 0.8 fusion.18
  1.5 0.2 reduce_window_sum.11
  1.6 0.8 select_reduce_fusion.1
  2.5 0.7 add_add_fusion.1
  3.5 1.8 gather_fusion
  5.4 2.2 gather.7
  7.7 3.7 %select_select_fusion = bf16[64,4,4096]{2,1,0:T(4,128)(2,1)} fusion(bf16[64,4,4096]{2,1,0:T(4,128)(2,1)} %gather.7, pred[64,4]{1,0:T(8,128)(4,1)S(1)} %compare_and_fusion, pred[64,4]{1,0:T(8,128)(4,1)S(1)} %broadcast_in_dim.67), kind=kLoop, calls=%fused_computation.2 | loop fusion | flops 2097152 | bytes 4194816 | tf_op jit(solution)/shard_map/jit(_where)/select_n | solution.py:155
  11.5 18.7 %all-to-all-start = ((bf16[64,4,4096]{2,1,0:T(4,128)(2,1)}), bf16[64,4,4096]{2,1,0:T(4,128)(2,1)S(1)}, u32[]{:S(2)}, u32[]{:S(2)}) async-start(bf16[64,4,4096]{2,1,0:T(4,128)(2,1)} %select_select_fusion), calls=%async_computation | async-start | bytes 4194304 | tf_op jit(solution)/shard_map/all_to_all | solution.py:158
  30.3 0.1 fusion.74
  30.6 0.3 pad_maximum_fusion
  31.1 0.3 pad_maximum_fusion.1
  31.4 0.8 bitcast_dynamic-update-slice_fusion.3
  32.2 0.8 bitcast_dynamic-update-slice_fusion.2
  33.0 0.7 constant_dynamic-update-slice_fusion
  33.7 0.8 bitcast_dynamic-update-slice_fusion.1
  34.5 0.8 bitcast_dynamic-update-slice_fusion
  35.3 95.0 %all-to-all-done = bf16[64,4,4096]{2,1,0:T(4,128)(2,1)S(1)} async-done(((bf16[64,4,4096]{2,1,0:T(4,128)(2,1)}), bf16[64,4,4096]{2,1,0:T(4,128)(2,1)S(1)}, u32[]{:S(2)}, u32[]{:S(2)}) %all-to-all-start) | async-done | bytes 2097184 | tf_op jit(solution)/shard_map/all_to_all | solution.py:158
  130.3 2.1 reshape.211
  132.4 2.8 fusion.78
  135.2 0.9 broadcast_in_dim.74
  136.1 4.5 %all-to-all-start.1 = ((f32[4,256,5,32]{1,3,2,0:T(8,128)}), f32[4,256,5,32]{1,3,2,0:T(8,128)}, u32[]{:S(2)}, u32[]{:S(2)}) async-start(f32[4,256,5,32]{1,3,2,0:T(8,128)} %broadcast_in_dim.74), calls=%async_computation.1 | async-start | bytes 1310720 | tf_op jit(solution)/shard_map/all_to_all | solution.py:56
  140.6 1.9 reshape.187.idx_ref
  142.5 2.1 reshape.181
  144.6 5.9 %all-to-all-done.1 = f32[4,256,5,32]{1,3,2,0:T(8,128)} async-done(((f32[4,256,5,32]{1,3,2,0:T(8,128)}), f32[4,256,5,32]{1,3,2,0:T(8,128)}, u32[]{:S(2)}, u32[]{:S(2)}) %all-to-all-start.1) | async-done | bytes 655392 | tf_op jit(solution)/shard_map/all_to_all | solution.py:56
  150.4 1.2 fusion.72
  151.7 2.1 fusion.79
  153.8 1.0 slice_bitcast_fusion
  154.9 1.0 slice.433
  156.0 1.0 slice.423
  157.1 1.0 slice.426
  158.2 1.0 slice.430
  159.2 1.9 squeeze.262
  161.1 3.1 %fusion.5.val_ref = f32[1024,128]{1,0:T(8,128)} fusion(f32[1024,128]{1,0:T(8,128)} %squeeze.262, f32[1024,2]{1,0:T(8,128)S(1)} %bitcast.383, f32[1024,126]{1,0:T(8,128)} %bitcast.389, f32[1024,1]{1,0:T(8,128)S(1)} %bitcast.385, f32[1024,127]{1,0:T(8,128)} %bitcast.390, f32[1024,127]{1,0:T(8,128)S(1)} %bitcast.387, f32[1024,1]{1,0:T(8,128)} %bitcast.391, ...), kind=kLoop, calls=%fused_computation.14 | loop fusion | flops 1048576 | bytes 3145728 | tf_op jit(solution)/shard_map/add | solution.py:188
  164.2 28.8 %shard_map.68 = f32[128,16,128]{2,1,0:T(8,128)} custom-call(f32[1024,128]{1,0:T(8,128)} %fusion.5.val_ref, s32[1024,128]{1,0:T(8,128)} %reshape.187.idx_ref), custom_call_target="tpu_custom_call" | custom-call | flops 1073741824 | bytes 2097152 | tf_op jit(solution)/shard_map/pallas_call | solution.py:118
  193.1 1.6 reshape_reshape.3
  194.6 1.1 constant_dynamic-slice_fusion.10
  195.9 1.9 collective-permute-start
  197.9 3.9 %collective-permute-start.1 = (f32[2,16,2048]{2,1,0:T(8,128)S(1)}, f32[2,16,2048]{2,1,0:T(8,128)S(1)}, u32[]{:S(2)}, u32[]{:S(2)}) collective-permute-start(f32[2,16,2048]{2,1,0:T(8,128)S(1)} %bitcast.399), channel_id=1, source_target_pairs={{0,8},{4,12},{8,0},{12,4},{16,24},{20,28},{24,16},{28,20},{32,40},... | collective-permute-start | bytes 786440 | tf_op jit(solution)/shard_map/ppermute | solution.py:45
  201.8 2.2 collective-permute-start.2
  204.1 1.9 collective-permute-done
  206.0 4.1 %collective-permute-done.1 = f32[2,16,2048]{2,1,0:T(8,128)S(1)} collective-permute-done((f32[2,16,2048]{2,1,0:T(8,128)S(1)}, f32[2,16,2048]{2,1,0:T(8,128)S(1)}, u32[]{:S(2)}, u32[]{:S(2)}) %collective-permute-start.1) | collective-permute-done | bytes 262176 | tf_op jit(solution)/shard_map/ppermute | solution.py:45
  210.1 2.4 collective-permute-done.2
  212.7 0.3 constant_dynamic-slice_fusion.6
  213.0 3.8 %collective-permute-start.3 = (f32[2,4,2048]{2,1,0:T(4,128)S(1)}, f32[2,4,2048]{2,1,0:T(4,128)S(1)}, u32[]{:S(2)}, u32[]{:S(2)}) collective-permute-start(f32[2,4,2048]{2,1,0:T(4,128)S(1)} %bitcast.401), channel_id=1, source_target_pairs={{0,16},{4,20},{8,24},{12,28},{16,32},{20,36},{24,40},{28,44},{32,4... | collective-permute-start | bytes 196616 | tf_op jit(solution)/shard_map/ppermute | solution.py:45
  216.8 2.3 collective-permute-start.4
  219.1 3.9 %collective-permute-start.5 = (f32[2,4,2048]{2,1,0:T(4,128)S(1)}, f32[2,4,2048]{2,1,0:T(4,128)S(1)}, u32[]{:S(2)}, u32[]{:S(2)}) collective-permute-start(f32[2,4,2048]{2,1,0:T(4,128)S(1)} %bitcast.403), channel_id=1, source_target_pairs={{0,48},{4,52},{8,56},{12,60},{16,0},{20,4},{24,8},{28,12},{32,16},... | collective-permute-start | bytes 196616 | tf_op jit(solution)/shard_map/ppermute | solution.py:45
  223.1 1.5 collective-permute-done.4
  224.6 0.8 collective-permute-done.5
  225.5 4.1 %collective-permute-start.6 = (f32[2,1,2048]{2,1,0:T(1,128)S(1)}, f32[2,1,2048]{2,1,0:T(1,128)S(1)}, u32[]{:S(2)}, u32[]{:S(2)}) collective-permute-start(f32[2,1,2048]{2,1,0:T(1,128)S(1)} %get-tuple-element.32), channel_id=1, source_target_pairs={{0,64},{4,68},{8,72},{12,76},{16,80},{20,84},{24,88},{28,92},{32,9... | collective-permute-start | bytes 49160 | tf_op jit(solution)/shard_map/ppermute | solution.py:45
  229.6 6.3 %collective-permute-start.7 = (f32[2,1,2048]{2,1,0:T(1,128)S(1)}, f32[2,1,2048]{2,1,0:T(1,128)S(1)}, u32[]{:S(2)}, u32[]{:S(2)}) collective-permute-start(f32[2,1,2048]{2,1,0:T(1,128)S(1)} %get-tuple-element.34), channel_id=1, source_target_pairs={{0,128},{4,132},{8,136},{12,140},{16,144},{20,148},{24,152},{28,15... | collective-permute-start | bytes 49160 | tf_op jit(solution)/shard_map/ppermute | solution.py:45
  235.9 5.2 %collective-permute-start.8 = (f32[2,1,2048]{2,1,0:T(1,128)S(1)}, f32[2,1,2048]{2,1,0:T(1,128)S(1)}, u32[]{:S(2)}, u32[]{:S(2)}) collective-permute-start(f32[2,1,2048]{2,1,0:T(1,128)S(1)} %get-tuple-element.33), channel_id=1, source_target_pairs={{0,192},{4,196},{8,200},{12,204},{16,208},{20,212},{24,216},{28,22... | collective-permute-start | bytes 49160 | tf_op jit(solution)/shard_map/ppermute | solution.py:45
  241.1 1.9 collective-permute-start.10
  243.1 0.9 collective-permute-done.7
  244.0 1.6 collective-permute-done.8
  245.6 1.9 collective-permute-start.9
  247.6 1.1 collective-permute-done.9
  248.7 1.0 fusion
  249.7 7.7 %all_to_all.21 = f32[4,3,128]{2,1,0:T(4,128)S(1)} all-to-all(f32[4,3,128]{2,1,0:T(4,128)S(1)} %broadcast_in_dim.75), channel_id=1, replica_groups=mesh['half'=2,'cls'=64,'vol'=4] {'vol'}, dimensions={0} | all-to-all | bytes 12288 | tf_op jit(solution)/shard_map/all_to_all | solution.py:56
  257.4 0.7 broadcast_in_dim.77
  258.0 13.2 %all-to-all-start.3 = ((f32[64,3,128]{2,1,0:T(4,128)}), f32[64,3,128]{2,1,0:T(4,128)S(1)}, u32[]{:S(2)}, u32[]{:S(2)}) async-start(f32[64,3,128]{2,1,0:T(4,128)} %broadcast_in_dim.77), calls=%async_computation.3 | async-start | bytes 262144 | tf_op jit(solution)/shard_map/all_to_all | solution.py:56
  271.3 14.9 %all-to-all-done.3 = f32[64,3,128]{2,1,0:T(4,128)S(1)} async-done(((f32[64,3,128]{2,1,0:T(4,128)}), f32[64,3,128]{2,1,0:T(4,128)S(1)}, u32[]{:S(2)}, u32[]{:S(2)}) %all-to-all-start.3) | async-done | bytes 98336 | tf_op jit(solution)/shard_map/all_to_all | solution.py:56
  286.2 0.7 slice_reduce_fusion.2
  288.8 0.7 fusion.2
  289.6 0.6 multiply_divide_fusion
  (48 shorter events, 2.2 us)
Async XLA Ops:
  0.6 2.9 copy-start
  11.5 18.7 %copy-start.1 = (bf16[32,4096]{1,0:T(8,128)(2,1)S(1)}, bf16[32,4096]{1,0:T(8,128)(2,1)}, u32[]{:S(2)}) copy-start(bf16[32,4096]{1,0:T(8,128)(2,1)} %param.7) | copy-start | bytes 786436
  11.5 118.9 %all-to-all-start = ((bf16[64,4,4096]{2,1,0:T(4,128)(2,1)}), bf16[64,4,4096]{2,1,0:T(4,128)(2,1)S(1)}, u32[]{:S(2)}, u32[]{:S(2)}) async-start(bf16[64,4,4096]{2,1,0:T(4,128)(2,1)} %select_select_fusion), calls=%async_computation | async-start | bytes 4194304 | tf_op jit(solution)/shard_map/all_to_all | solution.py:158
  136.1 14.3 %all-to-all-start.1 = ((f32[4,256,5,32]{1,3,2,0:T(8,128)}), f32[4,256,5,32]{1,3,2,0:T(8,128)}, u32[]{:S(2)}, u32[]{:S(2)}) async-start(f32[4,256,5,32]{1,3,2,0:T(8,128)} %broadcast_in_dim.74), calls=%async_computation.1 | async-start | bytes 1310720 | tf_op jit(solution)/shard_map/all_to_all | solution.py:56
  195.9 10.2 %collective-permute-start = (f32[2,16,2048]{2,1,0:T(8,128)S(1)}, f32[2,16,2048]{2,1,0:T(8,128)S(1)}, u32[]{:S(2)}, u32[]{:S(2)}) collective-permute-start(f32[2,16,2048]{2,1,0:T(8,128)S(1)} %bitcast.398), channel_id=1, source_target_pairs={{0,4},{4,8},{8,12},{12,0},{16,20},{20,24},{24,28},{28,16},{32,36},... | collective-permute-start | bytes 786440 | tf_op jit(solution)/shard_map/ppermute | solution.py:45
  197.9 43.2 %copy-start.2 = (s32[1,2048]{1,0:T(1,128)S(1)}, s32[1,2048]{1,0:T(1,128)}, u32[]{:S(2)}) copy-start(s32[1,2048]{1,0:T(1,128)} %param.9) | copy-start | bytes 24580
  197.9 12.2 %collective-permute-start.1 = (f32[2,16,2048]{2,1,0:T(8,128)S(1)}, f32[2,16,2048]{2,1,0:T(8,128)S(1)}, u32[]{:S(2)}, u32[]{:S(2)}) collective-permute-start(f32[2,16,2048]{2,1,0:T(8,128)S(1)} %bitcast.399), channel_id=1, source_target_pairs={{0,8},{4,12},{8,0},{12,4},{16,24},{20,28},{24,16},{28,20},{32,40},... | collective-permute-start | bytes 786440 | tf_op jit(solution)/shard_map/ppermute | solution.py:45
  201.8 10.6 %collective-permute-start.2 = (f32[2,16,2048]{2,1,0:T(8,128)S(1)}, f32[2,16,2048]{2,1,0:T(8,128)S(1)}, u32[]{:S(2)}, u32[]{:S(2)}) collective-permute-start(f32[2,16,2048]{2,1,0:T(8,128)S(1)} %bitcast.400), channel_id=1, source_target_pairs={{0,12},{4,0},{8,4},{12,8},{16,28},{20,16},{24,20},{28,24},{32,44},... | collective-permute-start | bytes 786440 | tf_op jit(solution)/shard_map/ppermute | solution.py:45
  213.0 10.1 %collective-permute-start.3 = (f32[2,4,2048]{2,1,0:T(4,128)S(1)}, f32[2,4,2048]{2,1,0:T(4,128)S(1)}, u32[]{:S(2)}, u32[]{:S(2)}) collective-permute-start(f32[2,4,2048]{2,1,0:T(4,128)S(1)} %bitcast.401), channel_id=1, source_target_pairs={{0,16},{4,20},{8,24},{12,28},{16,32},{20,36},{24,40},{28,44},{32,4... | collective-permute-start | bytes 196616 | tf_op jit(solution)/shard_map/ppermute | solution.py:45
  216.8 7.8 %collective-permute-start.4 = (f32[2,4,2048]{2,1,0:T(4,128)S(1)}, f32[2,4,2048]{2,1,0:T(4,128)S(1)}, u32[]{:S(2)}, u32[]{:S(2)}) collective-permute-start(f32[2,4,2048]{2,1,0:T(4,128)S(1)} %bitcast.402), channel_id=1, source_target_pairs={{0,32},{4,36},{8,40},{12,44},{16,48},{20,52},{24,56},{28,60},{32,0... | collective-permute-start | bytes 196616 | tf_op jit(solution)/shard_map/ppermute | solution.py:45
  219.1 6.3 %collective-permute-start.5 = (f32[2,4,2048]{2,1,0:T(4,128)S(1)}, f32[2,4,2048]{2,1,0:T(4,128)S(1)}, u32[]{:S(2)}, u32[]{:S(2)}) collective-permute-start(f32[2,4,2048]{2,1,0:T(4,128)S(1)} %bitcast.403), channel_id=1, source_target_pairs={{0,48},{4,52},{8,56},{12,60},{16,0},{20,4},{24,8},{28,12},{32,16},... | collective-permute-start | bytes 196616 | tf_op jit(solution)/shard_map/ppermute | solution.py:45
  225.5 17.5 %collective-permute-start.6 = (f32[2,1,2048]{2,1,0:T(1,128)S(1)}, f32[2,1,2048]{2,1,0:T(1,128)S(1)}, u32[]{:S(2)}, u32[]{:S(2)}) collective-permute-start(f32[2,1,2048]{2,1,0:T(1,128)S(1)} %get-tuple-element.32), channel_id=1, source_target_pairs={{0,64},{4,68},{8,72},{12,76},{16,80},{20,84},{24,88},{28,92},{32,9... | collective-permute-start | bytes 49160 | tf_op jit(solution)/shard_map/ppermute | solution.py:45
  229.6 14.3 %collective-permute-start.7 = (f32[2,1,2048]{2,1,0:T(1,128)S(1)}, f32[2,1,2048]{2,1,0:T(1,128)S(1)}, u32[]{:S(2)}, u32[]{:S(2)}) collective-permute-start(f32[2,1,2048]{2,1,0:T(1,128)S(1)} %get-tuple-element.34), channel_id=1, source_target_pairs={{0,128},{4,132},{8,136},{12,140},{16,144},{20,148},{24,152},{28,15... | collective-permute-start | bytes 49160 | tf_op jit(solution)/shard_map/ppermute | solution.py:45
  235.9 9.6 %collective-permute-start.8 = (f32[2,1,2048]{2,1,0:T(1,128)S(1)}, f32[2,1,2048]{2,1,0:T(1,128)S(1)}, u32[]{:S(2)}, u32[]{:S(2)}) collective-permute-start(f32[2,1,2048]{2,1,0:T(1,128)S(1)} %get-tuple-element.33), channel_id=1, source_target_pairs={{0,192},{4,196},{8,200},{12,204},{16,208},{20,212},{24,216},{28,22... | collective-permute-start | bytes 49160 | tf_op jit(solution)/shard_map/ppermute | solution.py:45
  241.1 6.4 %collective-permute-start.10 = (s32[2048]{0:T(1024)S(1)}, s32[2048]{0:T(1024)S(1)}, u32[]{:S(2)}, u32[]{:S(2)}) collective-permute-start(s32[2048]{0:T(1024)S(1)} %bitcast.412), channel_id=1, source_target_pairs={{0,256},{256,0},{1,257},{257,1},{2,258},{258,2},{3,259},{259,3},{4... | collective-permute-start | bytes 24584 | tf_op jit(solution)/shard_map/ppermute | solution.py:25
  245.6 3.1 %collective-permute-start.9 = (f32[4096]{0:T(1024)S(1)}, f32[4096]{0:T(1024)S(1)}, u32[]{:S(2)}, u32[]{:S(2)}) collective-permute-start(f32[4096]{0:T(1024)S(1)} %bitcast.404), channel_id=1, source_target_pairs={{0,256},{256,0},{1,257},{257,1},{2,258},{258,2},{3,259},{259,3},{4... | collective-permute-start | bytes 49160 | tf_op jit(solution)/shard_map/ppermute | solution.py:25
  258.0 28.1 %all-to-all-start.3 = ((f32[64,3,128]{2,1,0:T(4,128)}), f32[64,3,128]{2,1,0:T(4,128)S(1)}, u32[]{:S(2)}, u32[]{:S(2)}) async-start(f32[64,3,128]{2,1,0:T(4,128)} %broadcast_in_dim.77), calls=%async_computation.3 | async-start | bytes 262144 | tf_op jit(solution)/shard_map/all_to_all | solution.py:56
  286.9 3.3 %copy-start.3 = (f32[1,128]{1,0:T(1,128)}, f32[1,128]{1,0:T(1,128)S(1)}, u32[]{:S(2)}) copy-start(f32[1,128]{1,0:T(1,128)S(1)} %get-tuple-element.37) | copy-start | bytes 1540

commit v6 on v5

--- a/solution.py
+++ b/solution.py
@@ -86,16 +86,20 @@
     return data[:, 0]
 
 
-def _project_kernel(val_ref, idx_ref, out_ref, vt_ref, it_ref):
-    n = val_ref.shape[0]
+def _project_kernel(w_ref, idx_ref, out_ref, wt_ref, it_ref):
+    n = idx_ref.shape[0]
     hi_count = out_ref.shape[1]
-    vt_ref[...] = val_ref[...].T
+    for shift_id in range(SHIFTS):
+        wt_ref[shift_id] = w_ref[shift_id].T
     it_ref[...] = idx_ref[...].T
     lo_iota = lax.broadcasted_iota(jnp.int32, (LO, n), 0)
     hi_iota = lax.broadcasted_iota(jnp.int32, (hi_count, n), 0)
 
     def body(q, carry):
-        v = vt_ref[pl.ds(q, 1), :]
+        v = wt_ref[0, pl.ds(lax.rem(q + SHIFTS // 2, IMG), 1), :]
+        for shift_id in range(1, SHIFTS):
+            row = lax.rem(q - (shift_id - SHIFTS // 2) + IMG, IMG)
+            v = v + wt_ref[shift_id, pl.ds(row, 1), :]
         idx = it_ref[pl.ds(q, 1), :]
         lo = jnp.bitwise_and(idx, LO - 1)
         hi = jnp.right_shift(idx, 7)
@@ -112,8 +116,8 @@
     lax.fori_loop(0, IMG, body, 0)
 
 
-def project(val, idx, bins):
-    n, q_count = val.shape
+def project(weighted, idx, bins):
+    n, q_count = idx.shape
     hi_count = bins // LO
     return pl.pallas_call(
         _project_kernel,
@@ -124,15 +128,15 @@
         ],
         out_specs=pl.BlockSpec(memory_space=pltpu.VMEM),
         scratch_shapes=[
-            pltpu.VMEM((q_count, n), jnp.float32),
+            pltpu.VMEM((SHIFTS, q_count, n), jnp.float32),
             pltpu.VMEM((q_count, n), jnp.int32),
         ],
         cost_estimate=pl.CostEstimate(
             flops=2 * q_count * 2 * hi_count * LO * n,
-            bytes_accessed=q_count * n * 8 + q_count * bins * 4,
+            bytes_accessed=q_count * n * (4 * SHIFTS + 4) + q_count * bins * 4,
             transcendentals=0,
         ),
-    )(val, idx)
+    )(weighted, idx)
 
 
 def shards(images, groups, references, interp_index, shell_index):
@@ -148,13 +152,9 @@
     order_in = jnp.sum(jnp.cumsum(matches, axis=0) * matches, axis=1) - 1
     slot_ids = owner_ids * capacity + order_in
     slot_hits = slot_ids[None, :] == jnp.arange(slot_count, dtype=jnp.int32)[:, None]
-    source_ids = jnp.sum(
-        jnp.where(slot_hits, jnp.arange(part_count, dtype=jnp.int32)[None, :], 0), axis=1
-    )
-    filled = jnp.any(slot_hits, axis=1)
-    outgoing = jnp.where(
-        filled[:, None], jnp.take(images, source_ids, axis=0), jnp.zeros((), jnp.bfloat16)
-    )
+    outgoing = jnp.dot(
+        slot_hits.astype(jnp.bfloat16), images, preferred_element_type=jnp.float32
+    ).astype(jnp.bfloat16)
     arrived = lax.all_to_all(outgoing, "cls", split_axis=0, concat_axis=0, tiled=True)
     quarter_rows = pix_quarter // IMG
     bins = VOXS // IMG
@@ -182,12 +182,8 @@
         (((0,), (0,)), ((), ())),
         preferred_element_type=jnp.float32,
     )
-    weighted = weighted.reshape(SHIFTS, class_count, quarter_rows, IMG)
-    aligned = jnp.roll(weighted[0], -(SHIFTS // 2), axis=2)
-    for shift_id in range(1, SHIFTS):
-        aligned = aligned + jnp.roll(weighted[shift_id], shift_id - SHIFTS // 2, axis=2)
     slab_part = project(
-        aligned.reshape(class_count * quarter_rows, IMG),
+        weighted.reshape(SHIFTS, class_count * quarter_rows, IMG),
         interp_index.reshape(class_count * quarter_rows, IMG),
         bins,
     )

time: 292 us -> 283 us (0.969)
  other arithmetic: 13 us -> 5.92 us
  local copies, waits for them, and re-layouts: 27.2 us -> 21.5 us
    gather x2 -> x0, local copies, waits for them, and re-layouts: 4.07 us -> none  [shards(): jnp.take(images, source_ids, axis=0)]
    slice x4 -> x0, local copies, waits for them, and re-layouts: 4.03 us -> none  [the longest x3 3.03 us: shards(): jnp.roll(weighted[shift_id], shift_id - SHIFTS // 2, axis=2)]
    reshape x0 -> x1, local copies, waits for them, and re-layouts: none -> 3.75 us  [shards(): weighted.reshape(SHIFTS, class_count * quarter_rows, IMG)]
    select_n x2 -> x0, other arithmetic: 3.74 us -> none  [the longest x1 3.73 us: shards(): jnp.where(filled[:, None], jnp.take(images, source_ids, axis=0), jnp.zero...]
    add x1 -> x0, other arithmetic: 3.08 us -> none  [shards(): aligned + jnp.roll(weighted[shift_id], shift_id - SHIFTS // 2, axis=2)]
where the time goes in v6:
time: 283 us; the launch traced here: 281 us
  waiting for transfers between devices  130 us (46%)
  starting transfers between devices  73.5 us (26%)
  Pallas kernels  30 us (11%)
  local copies, waits for them, and re-layouts  21.5 us (8%)
  matrix products  8.81 us (3%)
  blocking collectives  7.66 us (3%)
  other arithmetic  5.92 us (2%)
  between operations  3.16 us (1%)
    all_to_all x1, waiting for transfers between devices, shards(): lax.all_to_all(outgoing, 'cls', split_axis=0, concat_axis=0, tiled=True)  95 us
    ppermute x9, starting transfers between devices, shift_in_digit(): return lax.ppermute(x, axis, perm)  33.3 us
    pallas_call x1, Pallas kernels, project(): pl.pallas_call(_project_kernel, out_shape=jax.ShapeDtypeStruct((q_count,...  30 us
    all_to_all x2, waiting for transfers between devices, exchange_sum(): lax.all_to_all(jnp.broadcast_to(x[None], (n,) + x.shape), axis, 0, 0, til...  20.7 us
    all_to_all x1, starting transfers between devices, shards(): lax.all_to_all(outgoing, 'cls', split_axis=0, concat_axis=0, tiled=True)  18.7 us
    all_to_all x2, starting transfers between devices, exchange_sum(): lax.all_to_all(jnp.broadcast_to(x[None], (n,) + x.shape), axis, 0, 0, til...  17.6 us
    ppermute x9, waiting for transfers between devices, shift_in_digit(): return lax.ppermute(x, axis, perm)  13.3 us
    all_to_all x1, blocking collectives, exchange_sum(): lax.all_to_all(jnp.broadcast_to(x[None], (n,) + x.shape), axis, 0, 0, til...  7.66 us
  transfers between devices with their start and end apart: 14, of which 11 were waited for; matrix products, arithmetic and copies ran while one was open for 3% of the time, Pallas kernels for 0%

profile of v6, /device:TPU:6, one launch (start us, length us, event | category | flops | bytes accessed | tf_op | source)
XLA Modules:
  0.0 280.7 jit_solution(4302089268510540660)
XLA Ops:
  0.6 0.8 fusion.15
  1.5 0.2 reduce_window_sum.11
  1.6 0.8 select_reduce_fusion
  2.5 0.7 add_add_fusion.1
  3.1 0.7 convolution_convert_fusion
  3.9 2.2 all_to_all.15
  6.1 18.7 %all-to-all-start = ((bf16[64,4,4096]{2,1,0:T(4,128)(2,1)}), bf16[64,4,4096]{2,1,0:T(4,128)(2,1)S(1)}, u32[]{:S(2)}, u32[]{:S(2)}) async-start(bf16[64,4,4096]{2,1,0:T(4,128)(2,1)} %all_to_all.15), calls=%async_computation | async-start | bytes 4194304 | tf_op jit(solution)/shard_map/all_to_all | solution.py:158
  24.9 0.1 fusion.71
  25.0 0.1 fusion.72
  25.1 0.3 pad_maximum_fusion
  25.4 0.1 fusion.73
  25.6 0.1 fusion.74
  25.7 0.3 pad_maximum_fusion.1
  26.0 0.8 bitcast_dynamic-update-slice_fusion.3
  26.8 0.8 bitcast_dynamic-update-slice_fusion.2
  27.6 0.7 constant_dynamic-update-slice_fusion
  28.3 0.8 bitcast_dynamic-update-slice_fusion.1
  29.2 0.8 bitcast_dynamic-update-slice_fusion
  29.9 95.0 %all-to-all-done = bf16[64,4,4096]{2,1,0:T(4,128)(2,1)S(1)} async-done(((bf16[64,4,4096]{2,1,0:T(4,128)(2,1)}), bf16[64,4,4096]{2,1,0:T(4,128)(2,1)S(1)}, u32[]{:S(2)}, u32[]{:S(2)}) %all-to-all-start) | async-done | bytes 2097184 | tf_op jit(solution)/shard_map/all_to_all | solution.py:158
  124.9 2.0 reshape.156
  127.0 2.8 fusion.75
  129.8 0.9 broadcast_in_dim.10
  130.7 4.5 %all-to-all-start.1 = ((f32[4,256,5,32]{1,3,2,0:T(8,128)}), f32[4,256,5,32]{1,3,2,0:T(8,128)}, u32[]{:S(2)}, u32[]{:S(2)}) async-start(f32[4,256,5,32]{1,3,2,0:T(8,128)} %broadcast_in_dim.10), calls=%async_computation.1 | async-start | bytes 1310720 | tf_op jit(solution)/shard_map/all_to_all | solution.py:56
  135.1 2.0 reshape.140.idx_ref
  137.1 2.0 reshape.133
  139.1 5.9 %all-to-all-done.1 = f32[4,256,5,32]{1,3,2,0:T(8,128)} async-done(((f32[4,256,5,32]{1,3,2,0:T(8,128)}), f32[4,256,5,32]{1,3,2,0:T(8,128)}, u32[]{:S(2)}, u32[]{:S(2)}) %all-to-all-start.1) | async-done | bytes 655392 | tf_op jit(solution)/shard_map/all_to_all | solution.py:56
  145.0 1.2 fusion.69
  146.2 3.6 %fusion.76 = f32[160,4096]{1,0:T(8,128)} fusion(bf16[256,160]{0,1:T(8,128)(2,1)S(1)} %bitcast.360, bf16[256,4096]{1,0:T(8,128)(2,1)} %reshape.133), kind=kOutput, calls=%fused_computation.191 | convolution fusion | flops 335544320 | bytes 4800512 | tf_op jit(solution)/shard_map/dot_general | solution.py:179
  149.9 3.7 %reshape.139.w_ref = f32[5,1024,128]{2,1,0:T(8,128)} reshape(f32[160,4096]{1,0:T(8,128)} %fusion.76) | data formatting | bytes 5242880 | tf_op jit(solution)/shard_map/reshape | solution.py:186
  153.6 30.0 %shard_map.68 = f32[128,16,128]{2,1,0:T(8,128)} custom-call(f32[5,1024,128]{2,1,0:T(8,128)} %reshape.139.w_ref, s32[1024,128]{1,0:T(8,128)} %reshape.140.idx_ref), custom_call_target="tpu_custom_call" | custom-call | flops 1073741824 | bytes 4194304 | tf_op jit(solution)/shard_map/pallas_call | solution.py:122
  183.6 1.6 reshape_reshape.3
  185.2 1.1 constant_dynamic-slice_fusion.10
  186.3 0.1 copy.35
  186.4 1.9 collective-permute-start
  188.3 0.1 copy.34
  188.4 3.9 %collective-permute-start.1 = (f32[2,16,2048]{2,1,0:T(8,128)S(1)}, f32[2,16,2048]{2,1,0:T(8,128)S(1)}, u32[]{:S(2)}, u32[]{:S(2)}) collective-permute-start(f32[2,16,2048]{2,1,0:T(8,128)S(1)} %bitcast.362), channel_id=1, source_target_pairs={{0,8},{4,12},{8,0},{12,4},{16,24},{20,28},{24,16},{28,20},{32,40},... | collective-permute-start | bytes 786440 | tf_op jit(solution)/shard_map/ppermute | solution.py:45
  192.3 0.1 copy.33
  192.4 2.0 collective-permute-start.2
  194.5 2.1 collective-permute-done
  196.6 4.1 %collective-permute-done.1 = f32[2,16,2048]{2,1,0:T(8,128)S(1)} collective-permute-done((f32[2,16,2048]{2,1,0:T(8,128)S(1)}, f32[2,16,2048]{2,1,0:T(8,128)S(1)}, u32[]{:S(2)}, u32[]{:S(2)}) %collective-permute-start.1) | collective-permute-done | bytes 262176 | tf_op jit(solution)/shard_map/ppermute | solution.py:45
  200.7 2.4 collective-permute-done.2
  203.0 0.1 fusion.5
  203.2 0.3 constant_dynamic-slice_fusion.6
  203.5 3.8 %collective-permute-start.3 = (f32[2,4,2048]{2,1,0:T(4,128)S(1)}, f32[2,4,2048]{2,1,0:T(4,128)S(1)}, u32[]{:S(2)}, u32[]{:S(2)}) collective-permute-start(f32[2,4,2048]{2,1,0:T(4,128)S(1)} %bitcast.364), channel_id=1, source_target_pairs={{0,16},{4,20},{8,24},{12,28},{16,32},{20,36},{24,40},{28,44},{32,4... | collective-permute-start | bytes 196616 | tf_op jit(solution)/shard_map/ppermute | solution.py:45
  207.3 2.3 collective-permute-start.4
  209.7 3.9 %collective-permute-start.5 = (f32[2,4,2048]{2,1,0:T(4,128)S(1)}, f32[2,4,2048]{2,1,0:T(4,128)S(1)}, u32[]{:S(2)}, u32[]{:S(2)}) collective-permute-start(f32[2,4,2048]{2,1,0:T(4,128)S(1)} %bitcast.366), channel_id=1, source_target_pairs={{0,48},{4,52},{8,56},{12,60},{16,0},{20,4},{24,8},{28,12},{32,16},... | collective-permute-start | bytes 196616 | tf_op jit(solution)/shard_map/ppermute | solution.py:45
  213.7 1.5 collective-permute-done.4
  215.1 0.8 collective-permute-done.5
  216.1 4.1 %collective-permute-start.6 = (f32[2,1,2048]{2,1,0:T(1,128)S(1)}, f32[2,1,2048]{2,1,0:T(1,128)S(1)}, u32[]{:S(2)}, u32[]{:S(2)}) collective-permute-start(f32[2,1,2048]{2,1,0:T(1,128)S(1)} %get-tuple-element.27), channel_id=1, source_target_pairs={{0,64},{4,68},{8,72},{12,76},{16,80},{20,84},{24,88},{28,92},{32,9... | collective-permute-start | bytes 49160 | tf_op jit(solution)/shard_map/ppermute | solution.py:45
  220.2 6.3 %collective-permute-start.7 = (f32[2,1,2048]{2,1,0:T(1,128)S(1)}, f32[2,1,2048]{2,1,0:T(1,128)S(1)}, u32[]{:S(2)}, u32[]{:S(2)}) collective-permute-start(f32[2,1,2048]{2,1,0:T(1,128)S(1)} %get-tuple-element.29), channel_id=1, source_target_pairs={{0,128},{4,132},{8,136},{12,140},{16,144},{20,148},{24,152},{28,15... | collective-permute-start | bytes 49160 | tf_op jit(solution)/shard_map/ppermute | solution.py:45
  226.5 5.2 %collective-permute-start.8 = (f32[2,1,2048]{2,1,0:T(1,128)S(1)}, f32[2,1,2048]{2,1,0:T(1,128)S(1)}, u32[]{:S(2)}, u32[]{:S(2)}) collective-permute-start(f32[2,1,2048]{2,1,0:T(1,128)S(1)} %get-tuple-element.28), channel_id=1, source_target_pairs={{0,192},{4,196},{8,200},{12,204},{16,208},{20,212},{24,216},{28,22... | collective-permute-start | bytes 49160 | tf_op jit(solution)/shard_map/ppermute | solution.py:45
  231.7 1.9 collective-permute-start.10
  233.6 0.9 collective-permute-done.7
  234.5 1.6 collective-permute-done.8
  236.2 1.9 collective-permute-start.9
  238.1 1.1 collective-permute-done.9
  239.3 1.0 fusion
  240.3 7.7 %all_to_all.24 = f32[4,3,128]{2,1,0:T(4,128)S(1)} all-to-all(f32[4,3,128]{2,1,0:T(4,128)S(1)} %broadcast_in_dim.11), channel_id=1, replica_groups=mesh['half'=2,'cls'=64,'vol'=4] {'vol'}, dimensions={0} | all-to-all | bytes 12288 | tf_op jit(solution)/shard_map/all_to_all | solution.py:56
  247.9 0.7 broadcast_in_dim.13
  248.6 13.2 %all-to-all-start.3 = ((f32[64,3,128]{2,1,0:T(4,128)}), f32[64,3,128]{2,1,0:T(4,128)S(1)}, u32[]{:S(2)}, u32[]{:S(2)}) async-start(f32[64,3,128]{2,1,0:T(4,128)} %broadcast_in_dim.13), calls=%async_computation.3 | async-start | bytes 262144 | tf_op jit(solution)/shard_map/all_to_all | solution.py:56
  261.8 14.9 %all-to-all-done.3 = f32[64,3,128]{2,1,0:T(4,128)S(1)} async-done(((f32[64,3,128]{2,1,0:T(4,128)}), f32[64,3,128]{2,1,0:T(4,128)S(1)}, u32[]{:S(2)}, u32[]{:S(2)}) %all-to-all-start.3) | async-done | bytes 98336 | tf_op jit(solution)/shard_map/all_to_all | solution.py:56
  276.8 0.7 slice_reduce_fusion.2
  279.4 0.7 fusion.2
  280.1 0.6 multiply_divide_fusion
  (30 shorter events, 0.5 us)
Async XLA Ops:
  0.6 2.5 copy-start
  6.1 18.7 %copy-start.1 = (bf16[32,4096]{1,0:T(8,128)(2,1)S(1)}, bf16[32,4096]{1,0:T(8,128)(2,1)}, u32[]{:S(2)}) copy-start(bf16[32,4096]{1,0:T(8,128)(2,1)} %param.7) | copy-start | bytes 786436
  6.1 118.9 %all-to-all-start = ((bf16[64,4,4096]{2,1,0:T(4,128)(2,1)}), bf16[64,4,4096]{2,1,0:T(4,128)(2,1)S(1)}, u32[]{:S(2)}, u32[]{:S(2)}) async-start(bf16[64,4,4096]{2,1,0:T(4,128)(2,1)} %all_to_all.15), calls=%async_computation | async-start | bytes 4194304 | tf_op jit(solution)/shard_map/all_to_all | solution.py:158
  130.7 14.3 %all-to-all-start.1 = ((f32[4,256,5,32]{1,3,2,0:T(8,128)}), f32[4,256,5,32]{1,3,2,0:T(8,128)}, u32[]{:S(2)}, u32[]{:S(2)}) async-start(f32[4,256,5,32]{1,3,2,0:T(8,128)} %broadcast_in_dim.10), calls=%async_computation.1 | async-start | bytes 1310720 | tf_op jit(solution)/shard_map/all_to_all | solution.py:56
  186.4 10.2 %collective-permute-start = (f32[2,16,2048]{2,1,0:T(8,128)S(1)}, f32[2,16,2048]{2,1,0:T(8,128)S(1)}, u32[]{:S(2)}, u32[]{:S(2)}) collective-permute-start(f32[2,16,2048]{2,1,0:T(8,128)S(1)} %bitcast.361), channel_id=1, source_target_pairs={{0,4},{4,8},{8,12},{12,0},{16,20},{20,24},{24,28},{28,16},{32,36},... | collective-permute-start | bytes 786440 | tf_op jit(solution)/shard_map/ppermute | solution.py:45
  188.4 43.2 %copy-start.2 = (s32[1,2048]{1,0:T(1,128)S(1)}, s32[1,2048]{1,0:T(1,128)}, u32[]{:S(2)}) copy-start(s32[1,2048]{1,0:T(1,128)} %param.9) | copy-start | bytes 24580
  188.4 12.2 %collective-permute-start.1 = (f32[2,16,2048]{2,1,0:T(8,128)S(1)}, f32[2,16,2048]{2,1,0:T(8,128)S(1)}, u32[]{:S(2)}, u32[]{:S(2)}) collective-permute-start(f32[2,16,2048]{2,1,0:T(8,128)S(1)} %bitcast.362), channel_id=1, source_target_pairs={{0,8},{4,12},{8,0},{12,4},{16,24},{20,28},{24,16},{28,20},{32,40},... | collective-permute-start | bytes 786440 | tf_op jit(solution)/shard_map/ppermute | solution.py:45
  192.4 10.6 %collective-permute-start.2 = (f32[2,16,2048]{2,1,0:T(8,128)S(1)}, f32[2,16,2048]{2,1,0:T(8,128)S(1)}, u32[]{:S(2)}, u32[]{:S(2)}) collective-permute-start(f32[2,16,2048]{2,1,0:T(8,128)S(1)} %bitcast.363), channel_id=1, source_target_pairs={{0,12},{4,0},{8,4},{12,8},{16,28},{20,16},{24,20},{28,24},{32,44},... | collective-permute-start | bytes 786440 | tf_op jit(solution)/shard_map/ppermute | solution.py:45
  203.5 10.1 %collective-permute-start.3 = (f32[2,4,2048]{2,1,0:T(4,128)S(1)}, f32[2,4,2048]{2,1,0:T(4,128)S(1)}, u32[]{:S(2)}, u32[]{:S(2)}) collective-permute-start(f32[2,4,2048]{2,1,0:T(4,128)S(1)} %bitcast.364), channel_id=1, source_target_pairs={{0,16},{4,20},{8,24},{12,28},{16,32},{20,36},{24,40},{28,44},{32,4... | collective-permute-start | bytes 196616 | tf_op jit(solution)/shard_map/ppermute | solution.py:45
  207.3 7.8 %collective-permute-start.4 = (f32[2,4,2048]{2,1,0:T(4,128)S(1)}, f32[2,4,2048]{2,1,0:T(4,128)S(1)}, u32[]{:S(2)}, u32[]{:S(2)}) collective-permute-start(f32[2,4,2048]{2,1,0:T(4,128)S(1)} %bitcast.365), channel_id=1, source_target_pairs={{0,32},{4,36},{8,40},{12,44},{16,48},{20,52},{24,56},{28,60},{32,0... | collective-permute-start | bytes 196616 | tf_op jit(solution)/shard_map/ppermute | solution.py:45
  209.7 6.3 %collective-permute-start.5 = (f32[2,4,2048]{2,1,0:T(4,128)S(1)}, f32[2,4,2048]{2,1,0:T(4,128)S(1)}, u32[]{:S(2)}, u32[]{:S(2)}) collective-permute-start(f32[2,4,2048]{2,1,0:T(4,128)S(1)} %bitcast.366), channel_id=1, source_target_pairs={{0,48},{4,52},{8,56},{12,60},{16,0},{20,4},{24,8},{28,12},{32,16},... | collective-permute-start | bytes 196616 | tf_op jit(solution)/shard_map/ppermute | solution.py:45
  216.1 17.5 %collective-permute-start.6 = (f32[2,1,2048]{2,1,0:T(1,128)S(1)}, f32[2,1,2048]{2,1,0:T(1,128)S(1)}, u32[]{:S(2)}, u32[]{:S(2)}) collective-permute-start(f32[2,1,2048]{2,1,0:T(1,128)S(1)} %get-tuple-element.27), channel_id=1, source_target_pairs={{0,64},{4,68},{8,72},{12,76},{16,80},{20,84},{24,88},{28,92},{32,9... | collective-permute-start | bytes 49160 | tf_op jit(solution)/shard_map/ppermute | solution.py:45
  220.2 14.3 %collective-permute-start.7 = (f32[2,1,2048]{2,1,0:T(1,128)S(1)}, f32[2,1,2048]{2,1,0:T(1,128)S(1)}, u32[]{:S(2)}, u32[]{:S(2)}) collective-permute-start(f32[2,1,2048]{2,1,0:T(1,128)S(1)} %get-tuple-element.29), channel_id=1, source_target_pairs={{0,128},{4,132},{8,136},{12,140},{16,144},{20,148},{24,152},{28,15... | collective-permute-start | bytes 49160 | tf_op jit(solution)/shard_map/ppermute | solution.py:45
  226.5 9.6 %collective-permute-start.8 = (f32[2,1,2048]{2,1,0:T(1,128)S(1)}, f32[2,1,2048]{2,1,0:T(1,128)S(1)}, u32[]{:S(2)}, u32[]{:S(2)}) collective-permute-start(f32[2,1,2048]{2,1,0:T(1,128)S(1)} %get-tuple-element.28), channel_id=1, source_target_pairs={{0,192},{4,196},{8,200},{12,204},{16,208},{20,212},{24,216},{28,22... | collective-permute-start | bytes 49160 | tf_op jit(solution)/shard_map/ppermute | solution.py:45
  231.7 6.4 %collective-permute-start.10 = (s32[2048]{0:T(1024)S(1)}, s32[2048]{0:T(1024)S(1)}, u32[]{:S(2)}, u32[]{:S(2)}) collective-permute-start(s32[2048]{0:T(1024)S(1)} %bitcast.375), channel_id=1, source_target_pairs={{0,256},{256,0},{1,257},{257,1},{2,258},{258,2},{3,259},{259,3},{4... | collective-permute-start | bytes 24584 | tf_op jit(solution)/shard_map/ppermute | solution.py:25
  236.2 3.1 %collective-permute-start.9 = (f32[4096]{0:T(1024)S(1)}, f32[4096]{0:T(1024)S(1)}, u32[]{:S(2)}, u32[]{:S(2)}) collective-permute-start(f32[4096]{0:T(1024)S(1)} %bitcast.367), channel_id=1, source_target_pairs={{0,256},{256,0},{1,257},{257,1},{2,258},{258,2},{3,259},{259,3},{4... | collective-permute-start | bytes 49160 | tf_op jit(solution)/shard_map/ppermute | solution.py:25
  248.6 28.1 %all-to-all-start.3 = ((f32[64,3,128]{2,1,0:T(4,128)}), f32[64,3,128]{2,1,0:T(4,128)S(1)}, u32[]{:S(2)}, u32[]{:S(2)}) async-start(f32[64,3,128]{2,1,0:T(4,128)} %broadcast_in_dim.13), calls=%async_computation.3 | async-start | bytes 262144 | tf_op jit(solution)/shard_map/all_to_all | solution.py:56
  277.4 3.3 %copy-start.3 = (f32[1,128]{1,0:T(1,128)}, f32[1,128]{1,0:T(1,128)S(1)}, u32[]{:S(2)}) copy-start(f32[1,128]{1,0:T(1,128)S(1)} %get-tuple-element.32) | copy-start | bytes 1540

commit v7 on v6

--- a/solution.py
+++ b/solution.py
@@ -113,7 +113,7 @@
         out_ref[q] = o[:hi_count] + o[hi_count:]
         return carry
 
-    lax.fori_loop(0, IMG, body, 0)
+    lax.fori_loop(0, IMG, body, 0, unroll=16)
 
 
 def project(weighted, idx, bins):

time: 283 us -> 266 us (0.940)
  Pallas kernels: 30 us -> 13.6 us
    pallas_call x1, Pallas kernels: 30 us -> 13.6 us  [project(): pl.pallas_call(_project_kernel, out_shape=jax.ShapeDtypeStruct((q_count,...]
  transfers between devices with their start and end apart: 14 -> 14, of which waited for: 11 -> 11; matrix products, arithmetic and copies ran while one was open for 3% -> 4% of each run, Pallas kernels for 0% -> 0%
where the time goes in v7:
time: 266 us; the launch traced here: 264 us
  waiting for transfers between devices  130 us (49%)
  starting transfers between devices  73.6 us (28%)
  local copies, waits for them, and re-layouts  21.5 us (8%)
  Pallas kernels  13.6 us (5%)
  matrix products  8.81 us (3%)
  blocking collectives  7.66 us (3%)
  other arithmetic  5.92 us (2%)
  between operations  3.16 us (1%)
    all_to_all x1, waiting for transfers between devices, shards(): lax.all_to_all(outgoing, 'cls', split_axis=0, concat_axis=0, tiled=True)  95 us
    ppermute x9, starting transfers between devices, shift_in_digit(): return lax.ppermute(x, axis, perm)  33.2 us
    all_to_all x2, waiting for transfers between devices, exchange_sum(): lax.all_to_all(jnp.broadcast_to(x[None], (n,) + x.shape), axis, 0, 0, til...  20.7 us
    all_to_all x1, starting transfers between devices, shards(): lax.all_to_all(outgoing, 'cls', split_axis=0, concat_axis=0, tiled=True)  18.7 us
    all_to_all x2, starting transfers between devices, exchange_sum(): lax.all_to_all(jnp.broadcast_to(x[None], (n,) + x.shape), axis, 0, 0, til...  17.6 us
    pallas_call x1, Pallas kernels, project(): pl.pallas_call(_project_kernel, out_shape=jax.ShapeDtypeStruct((q_count,...  13.6 us
    ppermute x9, waiting for transfers between devices, shift_in_digit(): return lax.ppermute(x, axis, perm)  13.4 us
    all_to_all x1, blocking collectives, exchange_sum(): lax.all_to_all(jnp.broadcast_to(x[None], (n,) + x.shape), axis, 0, 0, til...  7.66 us
  transfers between devices with their start and end apart: 14, of which 11 were waited for; matrix products, arithmetic and copies ran while one was open for 4% of the time, Pallas kernels for 0%

profile of v7, /device:TPU:6, one launch (start us, length us, event | category | flops | bytes accessed | tf_op | source)
XLA Modules:
  0.0 264.3 jit_solution(7779308788270408381)
XLA Ops:
  0.6 0.8 fusion.15
  1.5 0.2 reduce_window_sum.11
  1.6 0.8 select_reduce_fusion
  2.5 0.7 add_add_fusion.1
  3.1 0.7 convolution_convert_fusion
  3.9 2.2 all_to_all.15
  6.1 18.7 %all-to-all-start = ((bf16[64,4,4096]{2,1,0:T(4,128)(2,1)}), bf16[64,4,4096]{2,1,0:T(4,128)(2,1)S(1)}, u32[]{:S(2)}, u32[]{:S(2)}) async-start(bf16[64,4,4096]{2,1,0:T(4,128)(2,1)} %all_to_all.15), calls=%async_computation | async-start | bytes 4194304 | tf_op jit(solution)/shard_map/all_to_all | solution.py:158
  24.9 0.1 fusion.71
  25.0 0.1 fusion.72
  25.1 0.3 pad_maximum_fusion
  25.4 0.1 fusion.73
  25.6 0.1 fusion.74
  25.7 0.3 pad_maximum_fusion.1
  26.0 0.8 bitcast_dynamic-update-slice_fusion.3
  26.8 0.8 bitcast_dynamic-update-slice_fusion.2
  27.6 0.7 constant_dynamic-update-slice_fusion
  28.3 0.8 bitcast_dynamic-update-slice_fusion.1
  29.2 0.8 bitcast_dynamic-update-slice_fusion
  29.9 95.0 %all-to-all-done = bf16[64,4,4096]{2,1,0:T(4,128)(2,1)S(1)} async-done(((bf16[64,4,4096]{2,1,0:T(4,128)(2,1)}), bf16[64,4,4096]{2,1,0:T(4,128)(2,1)S(1)}, u32[]{:S(2)}, u32[]{:S(2)}) %all-to-all-start) | async-done | bytes 2097184 | tf_op jit(solution)/shard_map/all_to_all | solution.py:158
  124.9 2.0 reshape.156
  127.0 2.8 %fusion.75 = f32[256,5,32]{0,2,1:T(8,128)S(1)} fusion(bf16[256,4096,1]{1,0,2:T(8,128)(2,1)} %reshape.156, bf16[5,32,4096]{2,1,0:T(8,128)(2,1)} %bitcast.2), kind=kOutput, calls=%fused_computation.190 | convolution fusion | flops 335544320 | bytes 3571712 | tf_op jit(solution)/shard_map/dot_general | solution.py:171
  129.8 0.9 broadcast_in_dim.10
  130.7 4.5 %all-to-all-start.1 = ((f32[4,256,5,32]{1,3,2,0:T(8,128)}), f32[4,256,5,32]{1,3,2,0:T(8,128)}, u32[]{:S(2)}, u32[]{:S(2)}) async-start(f32[4,256,5,32]{1,3,2,0:T(8,128)} %broadcast_in_dim.10), calls=%async_computation.1 | async-start | bytes 1310720 | tf_op jit(solution)/shard_map/all_to_all | solution.py:56
  135.1 2.0 reshape.140.idx_ref
  137.1 2.0 reshape.133
  139.1 5.9 %all-to-all-done.1 = f32[4,256,5,32]{1,3,2,0:T(8,128)} async-done(((f32[4,256,5,32]{1,3,2,0:T(8,128)}), f32[4,256,5,32]{1,3,2,0:T(8,128)}, u32[]{:S(2)}, u32[]{:S(2)}) %all-to-all-start.1) | async-done | bytes 655392 | tf_op jit(solution)/shard_map/all_to_all | solution.py:56
  145.0 1.2 fusion.69
  146.2 3.6 %fusion.76 = f32[160,4096]{1,0:T(8,128)} fusion(bf16[256,160]{0,1:T(8,128)(2,1)S(1)} %bitcast.360, bf16[256,4096]{1,0:T(8,128)(2,1)} %reshape.133), kind=kOutput, calls=%fused_computation.191 | convolution fusion | flops 335544320 | bytes 4800512 | tf_op jit(solution)/shard_map/dot_general | solution.py:179
  149.9 3.7 %reshape.139.w_ref = f32[5,1024,128]{2,1,0:T(8,128)} reshape(f32[160,4096]{1,0:T(8,128)} %fusion.76) | data formatting | bytes 5242880 | tf_op jit(solution)/shard_map/reshape | solution.py:186
  153.6 13.6 %shard_map.68 = f32[128,16,128]{2,1,0:T(8,128)} custom-call(f32[5,1024,128]{2,1,0:T(8,128)} %reshape.139.w_ref, s32[1024,128]{1,0:T(8,128)} %reshape.140.idx_ref), custom_call_target="tpu_custom_call" | custom-call | flops 1073741824 | bytes 4194304 | tf_op jit(solution)/shard_map/pallas_call | solution.py:122
  167.2 1.6 reshape_reshape.3
  168.7 1.1 constant_dynamic-slice_fusion.10
  169.9 0.1 copy.35
  170.0 1.9 collective-permute-start
  171.9 0.1 copy.34
  172.0 3.9 %collective-permute-start.1 = (f32[2,16,2048]{2,1,0:T(8,128)S(1)}, f32[2,16,2048]{2,1,0:T(8,128)S(1)}, u32[]{:S(2)}, u32[]{:S(2)}) collective-permute-start(f32[2,16,2048]{2,1,0:T(8,128)S(1)} %bitcast.362), channel_id=1, source_target_pairs={{0,8},{4,12},{8,0},{12,4},{16,24},{20,28},{24,16},{28,20},{32,40},... | collective-permute-start | bytes 786440 | tf_op jit(solution)/shard_map/ppermute | solution.py:45
  175.9 0.1 copy.33
  175.9 2.0 collective-permute-start.2
  178.0 2.1 collective-permute-done
  180.1 4.1 %collective-permute-done.1 = f32[2,16,2048]{2,1,0:T(8,128)S(1)} collective-permute-done((f32[2,16,2048]{2,1,0:T(8,128)S(1)}, f32[2,16,2048]{2,1,0:T(8,128)S(1)}, u32[]{:S(2)}, u32[]{:S(2)}) %collective-permute-start.1) | collective-permute-done | bytes 262176 | tf_op jit(solution)/shard_map/ppermute | solution.py:45
  184.2 2.4 collective-permute-done.2
  186.6 0.1 fusion.5
  186.8 0.3 constant_dynamic-slice_fusion.6
  187.1 3.8 %collective-permute-start.3 = (f32[2,4,2048]{2,1,0:T(4,128)S(1)}, f32[2,4,2048]{2,1,0:T(4,128)S(1)}, u32[]{:S(2)}, u32[]{:S(2)}) collective-permute-start(f32[2,4,2048]{2,1,0:T(4,128)S(1)} %bitcast.364), channel_id=1, source_target_pairs={{0,16},{4,20},{8,24},{12,28},{16,32},{20,36},{24,40},{28,44},{32,4... | collective-permute-start | bytes 196616 | tf_op jit(solution)/shard_map/ppermute | solution.py:45
  190.9 2.3 collective-permute-start.4
  193.2 3.9 %collective-permute-start.5 = (f32[2,4,2048]{2,1,0:T(4,128)S(1)}, f32[2,4,2048]{2,1,0:T(4,128)S(1)}, u32[]{:S(2)}, u32[]{:S(2)}) collective-permute-start(f32[2,4,2048]{2,1,0:T(4,128)S(1)} %bitcast.366), channel_id=1, source_target_pairs={{0,48},{4,52},{8,56},{12,60},{16,0},{20,4},{24,8},{28,12},{32,16},... | collective-permute-start | bytes 196616 | tf_op jit(solution)/shard_map/ppermute | solution.py:45
  197.2 1.4 collective-permute-done.4
  198.7 0.9 collective-permute-done.5
  199.6 4.1 %collective-permute-start.6 = (f32[2,1,2048]{2,1,0:T(1,128)S(1)}, f32[2,1,2048]{2,1,0:T(1,128)S(1)}, u32[]{:S(2)}, u32[]{:S(2)}) collective-permute-start(f32[2,1,2048]{2,1,0:T(1,128)S(1)} %get-tuple-element.27), channel_id=1, source_target_pairs={{0,64},{4,68},{8,72},{12,76},{16,80},{20,84},{24,88},{28,92},{32,9... | collective-permute-start | bytes 49160 | tf_op jit(solution)/shard_map/ppermute | solution.py:45
  203.7 6.3 %collective-permute-start.7 = (f32[2,1,2048]{2,1,0:T(1,128)S(1)}, f32[2,1,2048]{2,1,0:T(1,128)S(1)}, u32[]{:S(2)}, u32[]{:S(2)}) collective-permute-start(f32[2,1,2048]{2,1,0:T(1,128)S(1)} %get-tuple-element.29), channel_id=1, source_target_pairs={{0,128},{4,132},{8,136},{12,140},{16,144},{20,148},{24,152},{28,15... | collective-permute-start | bytes 49160 | tf_op jit(solution)/shard_map/ppermute | solution.py:45
  210.0 5.2 %collective-permute-start.8 = (f32[2,1,2048]{2,1,0:T(1,128)S(1)}, f32[2,1,2048]{2,1,0:T(1,128)S(1)}, u32[]{:S(2)}, u32[]{:S(2)}) collective-permute-start(f32[2,1,2048]{2,1,0:T(1,128)S(1)} %get-tuple-element.28), channel_id=1, source_target_pairs={{0,192},{4,196},{8,200},{12,204},{16,208},{20,212},{24,216},{28,22... | collective-permute-start | bytes 49160 | tf_op jit(solution)/shard_map/ppermute | solution.py:45
  215.2 1.9 collective-permute-start.10
  217.2 0.9 collective-permute-done.7
  218.1 1.6 collective-permute-done.8
  219.7 2.1 collective-permute-start.9
  221.8 0.9 collective-permute-done.9
  222.8 1.0 fusion
  223.8 7.7 %all_to_all.24 = f32[4,3,128]{2,1,0:T(4,128)S(1)} all-to-all(f32[4,3,128]{2,1,0:T(4,128)S(1)} %broadcast_in_dim.11), channel_id=1, replica_groups=mesh['half'=2,'cls'=64,'vol'=4] {'vol'}, dimensions={0} | all-to-all | bytes 12288 | tf_op jit(solution)/shard_map/all_to_all | solution.py:56
  231.5 0.7 broadcast_in_dim.13
  232.2 13.2 %all-to-all-start.3 = ((f32[64,3,128]{2,1,0:T(4,128)}), f32[64,3,128]{2,1,0:T(4,128)S(1)}, u32[]{:S(2)}, u32[]{:S(2)}) async-start(f32[64,3,128]{2,1,0:T(4,128)} %broadcast_in_dim.13), calls=%async_computation.3 | async-start | bytes 262144 | tf_op jit(solution)/shard_map/all_to_all | solution.py:56
  245.4 14.9 %all-to-all-done.3 = f32[64,3,128]{2,1,0:T(4,128)S(1)} async-done(((f32[64,3,128]{2,1,0:T(4,128)}), f32[64,3,128]{2,1,0:T(4,128)S(1)}, u32[]{:S(2)}, u32[]{:S(2)}) %all-to-all-start.3) | async-done | bytes 98336 | tf_op jit(solution)/shard_map/all_to_all | solution.py:56
  260.3 0.7 slice_reduce_fusion.2
  263.0 0.7 fusion.2
  263.7 0.6 multiply_divide_fusion
  (30 shorter events, 0.5 us)
Async XLA Ops:
  0.6 2.5 copy-start
  6.1 18.7 %copy-start.1 = (bf16[32,4096]{1,0:T(8,128)(2,1)S(1)}, bf16[32,4096]{1,0:T(8,128)(2,1)}, u32[]{:S(2)}) copy-start(bf16[32,4096]{1,0:T(8,128)(2,1)} %param.7) | copy-start | bytes 786436
  6.1 118.9 %all-to-all-start = ((bf16[64,4,4096]{2,1,0:T(4,128)(2,1)}), bf16[64,4,4096]{2,1,0:T(4,128)(2,1)S(1)}, u32[]{:S(2)}, u32[]{:S(2)}) async-start(bf16[64,4,4096]{2,1,0:T(4,128)(2,1)} %all_to_all.15), calls=%async_computation | async-start | bytes 4194304 | tf_op jit(solution)/shard_map/all_to_all | solution.py:158
  130.7 14.3 %all-to-all-start.1 = ((f32[4,256,5,32]{1,3,2,0:T(8,128)}), f32[4,256,5,32]{1,3,2,0:T(8,128)}, u32[]{:S(2)}, u32[]{:S(2)}) async-start(f32[4,256,5,32]{1,3,2,0:T(8,128)} %broadcast_in_dim.10), calls=%async_computation.1 | async-start | bytes 1310720 | tf_op jit(solution)/shard_map/all_to_all | solution.py:56
  170.0 10.2 %collective-permute-start = (f32[2,16,2048]{2,1,0:T(8,128)S(1)}, f32[2,16,2048]{2,1,0:T(8,128)S(1)}, u32[]{:S(2)}, u32[]{:S(2)}) collective-permute-start(f32[2,16,2048]{2,1,0:T(8,128)S(1)} %bitcast.361), channel_id=1, source_target_pairs={{0,4},{4,8},{8,12},{12,0},{16,20},{20,24},{24,28},{28,16},{32,36},... | collective-permute-start | bytes 786440 | tf_op jit(solution)/shard_map/ppermute | solution.py:45
  172.0 43.2 %copy-start.2 = (s32[1,2048]{1,0:T(1,128)S(1)}, s32[1,2048]{1,0:T(1,128)}, u32[]{:S(2)}) copy-start(s32[1,2048]{1,0:T(1,128)} %param.9) | copy-start | bytes 24580
  172.0 12.2 %collective-permute-start.1 = (f32[2,16,2048]{2,1,0:T(8,128)S(1)}, f32[2,16,2048]{2,1,0:T(8,128)S(1)}, u32[]{:S(2)}, u32[]{:S(2)}) collective-permute-start(f32[2,16,2048]{2,1,0:T(8,128)S(1)} %bitcast.362), channel_id=1, source_target_pairs={{0,8},{4,12},{8,0},{12,4},{16,24},{20,28},{24,16},{28,20},{32,40},... | collective-permute-start | bytes 786440 | tf_op jit(solution)/shard_map/ppermute | solution.py:45
  175.9 10.6 %collective-permute-start.2 = (f32[2,16,2048]{2,1,0:T(8,128)S(1)}, f32[2,16,2048]{2,1,0:T(8,128)S(1)}, u32[]{:S(2)}, u32[]{:S(2)}) collective-permute-start(f32[2,16,2048]{2,1,0:T(8,128)S(1)} %bitcast.363), channel_id=1, source_target_pairs={{0,12},{4,0},{8,4},{12,8},{16,28},{20,16},{24,20},{28,24},{32,44},... | collective-permute-start | bytes 786440 | tf_op jit(solution)/shard_map/ppermute | solution.py:45
  187.1 10.1 %collective-permute-start.3 = (f32[2,4,2048]{2,1,0:T(4,128)S(1)}, f32[2,4,2048]{2,1,0:T(4,128)S(1)}, u32[]{:S(2)}, u32[]{:S(2)}) collective-permute-start(f32[2,4,2048]{2,1,0:T(4,128)S(1)} %bitcast.364), channel_id=1, source_target_pairs={{0,16},{4,20},{8,24},{12,28},{16,32},{20,36},{24,40},{28,44},{32,4... | collective-permute-start | bytes 196616 | tf_op jit(solution)/shard_map/ppermute | solution.py:45
  190.9 7.8 %collective-permute-start.4 = (f32[2,4,2048]{2,1,0:T(4,128)S(1)}, f32[2,4,2048]{2,1,0:T(4,128)S(1)}, u32[]{:S(2)}, u32[]{:S(2)}) collective-permute-start(f32[2,4,2048]{2,1,0:T(4,128)S(1)} %bitcast.365), channel_id=1, source_target_pairs={{0,32},{4,36},{8,40},{12,44},{16,48},{20,52},{24,56},{28,60},{32,0... | collective-permute-start | bytes 196616 | tf_op jit(solution)/shard_map/ppermute | solution.py:45
  193.2 6.3 %collective-permute-start.5 = (f32[2,4,2048]{2,1,0:T(4,128)S(1)}, f32[2,4,2048]{2,1,0:T(4,128)S(1)}, u32[]{:S(2)}, u32[]{:S(2)}) collective-permute-start(f32[2,4,2048]{2,1,0:T(4,128)S(1)} %bitcast.366), channel_id=1, source_target_pairs={{0,48},{4,52},{8,56},{12,60},{16,0},{20,4},{24,8},{28,12},{32,16},... | collective-permute-start | bytes 196616 | tf_op jit(solution)/shard_map/ppermute | solution.py:45
  199.6 17.5 %collective-permute-start.6 = (f32[2,1,2048]{2,1,0:T(1,128)S(1)}, f32[2,1,2048]{2,1,0:T(1,128)S(1)}, u32[]{:S(2)}, u32[]{:S(2)}) collective-permute-start(f32[2,1,2048]{2,1,0:T(1,128)S(1)} %get-tuple-element.27), channel_id=1, source_target_pairs={{0,64},{4,68},{8,72},{12,76},{16,80},{20,84},{24,88},{28,92},{32,9... | collective-permute-start | bytes 49160 | tf_op jit(solution)/shard_map/ppermute | solution.py:45
  203.7 14.3 %collective-permute-start.7 = (f32[2,1,2048]{2,1,0:T(1,128)S(1)}, f32[2,1,2048]{2,1,0:T(1,128)S(1)}, u32[]{:S(2)}, u32[]{:S(2)}) collective-permute-start(f32[2,1,2048]{2,1,0:T(1,128)S(1)} %get-tuple-element.29), channel_id=1, source_target_pairs={{0,128},{4,132},{8,136},{12,140},{16,144},{20,148},{24,152},{28,15... | collective-permute-start | bytes 49160 | tf_op jit(solution)/shard_map/ppermute | solution.py:45
  210.0 9.6 %collective-permute-start.8 = (f32[2,1,2048]{2,1,0:T(1,128)S(1)}, f32[2,1,2048]{2,1,0:T(1,128)S(1)}, u32[]{:S(2)}, u32[]{:S(2)}) collective-permute-start(f32[2,1,2048]{2,1,0:T(1,128)S(1)} %get-tuple-element.28), channel_id=1, source_target_pairs={{0,192},{4,196},{8,200},{12,204},{16,208},{20,212},{24,216},{28,22... | collective-permute-start | bytes 49160 | tf_op jit(solution)/shard_map/ppermute | solution.py:45
  215.2 6.6 %collective-permute-start.10 = (s32[2048]{0:T(1024)S(1)}, s32[2048]{0:T(1024)S(1)}, u32[]{:S(2)}, u32[]{:S(2)}) collective-permute-start(s32[2048]{0:T(1024)S(1)} %bitcast.375), channel_id=1, source_target_pairs={{0,256},{256,0},{1,257},{257,1},{2,258},{258,2},{3,259},{259,3},{4... | collective-permute-start | bytes 24584 | tf_op jit(solution)/shard_map/ppermute | solution.py:25
  219.7 3.1 %collective-permute-start.9 = (f32[4096]{0:T(1024)S(1)}, f32[4096]{0:T(1024)S(1)}, u32[]{:S(2)}, u32[]{:S(2)}) collective-permute-start(f32[4096]{0:T(1024)S(1)} %bitcast.367), channel_id=1, source_target_pairs={{0,256},{256,0},{1,257},{257,1},{2,258},{258,2},{3,259},{259,3},{4... | collective-permute-start | bytes 49160 | tf_op jit(solution)/shard_map/ppermute | solution.py:25
  232.2 28.1 %all-to-all-start.3 = ((f32[64,3,128]{2,1,0:T(4,128)}), f32[64,3,128]{2,1,0:T(4,128)S(1)}, u32[]{:S(2)}, u32[]{:S(2)}) async-start(f32[64,3,128]{2,1,0:T(4,128)} %broadcast_in_dim.13), calls=%async_computation.3 | async-start | bytes 262144 | tf_op jit(solution)/shard_map/all_to_all | solution.py:56
  261.0 3.3 %copy-start.3 = (f32[1,128]{1,0:T(1,128)}, f32[1,128]{1,0:T(1,128)S(1)}, u32[]{:S(2)}) copy-start(f32[1,128]{1,0:T(1,128)S(1)} %get-tuple-element.32) | copy-start | bytes 1540

commit v8 on v7

--- a/solution.py
+++ b/solution.py
@@ -19,6 +19,8 @@
 EPS_F = 1e-06
 
 LO = 128
+CLS = ("z", "x")
+X_CHIPS = 4
 
 
 def partner(shard, axis, apart):
@@ -72,18 +74,24 @@
     return x
 
 
-def reduce_scatter(x, axis):
-    me = lax.axis_index(axis)
+def reduce_scatter(x, inner, outer):
+    me = lax.axis_index(inner)
+    n_inner = lax.axis_size(inner)
+    n_outer = lax.axis_size(outer)
     data = x
-    for stride, radix in digits_of(lax.axis_size(axis)):
+    for stride, radix in digits_of(n_inner):
         d = (me // stride) % radix
         data = data.reshape(data.shape[0], data.shape[1] // radix, radix, data.shape[2])
         total = lax.dynamic_index_in_dim(data, d, axis=2, keepdims=False)
         for s in range(1, radix):
             send = lax.dynamic_index_in_dim(data, (d + s) % radix, axis=2, keepdims=False)
-            total = total + shift_in_digit(send, axis, stride, radix, s)
+            total = total + shift_in_digit(send, inner, stride, radix, s)
         data = total
-    return data[:, 0]
+    got = lax.all_to_all(jnp.swapaxes(data, 0, 1), outer, 0, 0, tiled=True)
+    total = got[0]
+    for i in range(1, n_outer):
+        total = total + got[i]
+    return total
 
 
 def _project_kernel(w_ref, idx_ref, out_ref, wt_ref, it_ref):
@@ -140,7 +148,7 @@
 
 
 def shards(images, groups, references, interp_index, shell_index):
-    n_cls = lax.axis_size("cls")
+    n_cls = lax.axis_size(CLS)
     n_vol = lax.axis_size("vol")
     n_half = lax.axis_size("half")
     part_count, pix_quarter = images.shape
@@ -155,7 +163,7 @@
     outgoing = jnp.dot(
         slot_hits.astype(jnp.bfloat16), images, preferred_element_type=jnp.float32
     ).astype(jnp.bfloat16)
-    arrived = lax.all_to_all(outgoing, "cls", split_axis=0, concat_axis=0, tiled=True)
+    arrived = lax.all_to_all(outgoing, CLS, split_axis=0, concat_axis=0, tiled=True)
     quarter_rows = pix_quarter // IMG
     bins = VOXS // IMG
     shaped_refs = references.reshape(class_count, quarter_rows, IMG)
@@ -189,7 +197,7 @@
     )
     piece_len = VOXS // (n_half * n_cls)
     slab_part = slab_part.reshape(n_half, n_cls, piece_len)
-    own_block = reduce_scatter(slab_part, "cls").reshape(-1)
+    own_block = reduce_scatter(slab_part, "x", "z").reshape(-1)
     half_id = lax.axis_index("half")
     other_block = partner(own_block, "half", 0)
     other_shell = partner(shell_index[0], "half", 0)
@@ -205,7 +213,7 @@
     )
     stats = jnp.stack([first_block * first_block, second_block * second_block, first_block * second_block])
     shell_terms = jnp.dot(stats, block_hot, precision=lax.Precision.HIGHEST)
-    shell_sums = exchange_sum(exchange_sum(shell_terms, "vol"), "cls")
+    shell_sums = exchange_sum(exchange_sum(shell_terms, "vol"), CLS)
     shell_fsc = shell_sums[2] / (jnp.sqrt(shell_sums[0]) * jnp.sqrt(shell_sums[1]) + EPS_F)
     mean_sq = (jnp.sum(shell_sums[0]) + jnp.sum(shell_sums[1]) + 2.0 * jnp.sum(shell_sums[2])) / (
         4.0 * n_vol * VOXS
@@ -221,17 +229,23 @@
 
 
 def solution(mesh):
+    n_cls = mesh.shape["cls"]
+    fine = jax.sharding.Mesh(
+        mesh.devices.reshape(mesh.shape["half"], n_cls // X_CHIPS, X_CHIPS, mesh.shape["vol"]),
+        ("half", "z", "x", "vol"),
+    )
+    rows = ("half", "z", "x")
     placed = (
-        P(("half", "cls"), "vol"),
-        P(("half", "cls"), None),
-        P("cls", "vol"),
-        P("cls", "vol"),
-        P("vol", ("half", "cls")),
+        P(rows, "vol"),
+        P(rows, None),
+        P(CLS, "vol"),
+        P(CLS, "vol"),
+        P("vol", rows),
     )
     return jax.shard_map(
         shards,
-        mesh=mesh,
+        mesh=fine,
         in_specs=placed,
-        out_specs=(P("vol", ("half", "cls")), P()),
+        out_specs=(P("vol", rows), P()),
         check_vma=False,
     )

time: 266 us -> 253 us (0.951)
  starting transfers between devices: 73.6 us -> 48.8 us
  waiting for transfers between devices: 130 us -> 141 us
    ppermute x9 -> x3, starting transfers between devices: 33.2 us -> 7.76 us  [shift_in_digit(): return lax.ppermute(x, axis, perm)]
    all_to_all x1 -> x2, waiting for transfers between devices: 95 us -> 111 us  [the longest x1 95 us: shards(): lax.all_to_all(outgoing, CLS, split_axis=0, concat_axis=0, tiled=True)]
    all_to_all x1 -> x2, starting transfers between devices: 18.7 us -> 23.9 us  [the longest x1 18.7 us: shards(): lax.all_to_all(outgoing, CLS, split_axis=0, concat_axis=0, tiled=True)]
    ppermute x9 -> x3, waiting for transfers between devices: 13.4 us -> 8.63 us  [shift_in_digit(): return lax.ppermute(x, axis, perm)]
    all_to_all x2, starting transfers between devices: 17.6 us -> 13.2 us  [exchange_sum(): lax.all_to_all(jnp.broadcast_to(x[None], (n,) + x.shape), axis, 0, 0, til...]
  transfers between devices with their start and end apart: 14 -> 9, of which waited for: 11 -> 8; matrix products, arithmetic and copies ran while one was open for 4% -> 4% of each run, Pallas kernels for 0% -> 0%
where the time goes in v8:
time: 253 us; the launch traced here: 251 us
  waiting for transfers between devices  141 us (56%)
  starting transfers between devices  48.8 us (19%)
  local copies, waits for them, and re-layouts  21.5 us (8%)
  Pallas kernels  13.6 us (5%)
  matrix products  8.78 us (3%)
  blocking collectives  7.66 us (3%)
  other arithmetic  6.86 us (3%)
  between operations  2.88 us (1%)
    all_to_all x1, waiting for transfers between devices, shards(): lax.all_to_all(outgoing, CLS, split_axis=0, concat_axis=0, tiled=True)  95 us
    all_to_all x2, waiting for transfers between devices, exchange_sum(): lax.all_to_all(jnp.broadcast_to(x[None], (n,) + x.shape), axis, 0, 0, til...  20.7 us
    all_to_all x1, starting transfers between devices, shards(): lax.all_to_all(outgoing, CLS, split_axis=0, concat_axis=0, tiled=True)  18.7 us
    all_to_all x1, waiting for transfers between devices, reduce_scatter(): got = lax.all_to_all(jnp.swapaxes(data, 0, 1), outer, 0, 0, tiled=True)  15.6 us
    pallas_call x1, Pallas kernels, project(): pl.pallas_call(_project_kernel, out_shape=jax.ShapeDtypeStruct((q_count,...  13.6 us
    all_to_all x2, starting transfers between devices, exchange_sum(): lax.all_to_all(jnp.broadcast_to(x[None], (n,) + x.shape), axis, 0, 0, til...  13.2 us
    ppermute x3, waiting for transfers between devices, shift_in_digit(): return lax.ppermute(x, axis, perm)  8.63 us
    ppermute x3, starting transfers between devices, shift_in_digit(): return lax.ppermute(x, axis, perm)  7.76 us
  transfers between devices with their start and end apart: 9, of which 8 were waited for; matrix products, arithmetic and copies ran while one was open for 4% of the time, Pallas kernels for 0%

profile of v8, /device:TPU:6, one launch (start us, length us, event | category | flops | bytes accessed | tf_op | source)
XLA Modules:
  0.0 251.1 jit_solution(15098963064721056815)
XLA Ops:
  0.6 0.0 copy-start
  0.6 0.8 fusion.14
  1.5 0.2 reduce_window_sum.11
  1.6 0.8 select_reduce_fusion
  2.5 0.7 add_add_fusion
  3.1 0.0 copy-done
  3.1 0.7 convolution_convert_fusion
  3.9 2.2 all_to_all.18
  6.1 18.7 %all-to-all-start = ((bf16[64,4,4096]{2,1,0:T(4,128)(2,1)}), bf16[64,4,4096]{2,1,0:T(4,128)(2,1)S(1)}, u32[]{:S(2)}, u32[]{:S(2)}) async-start(bf16[64,4,4096]{2,1,0:T(4,128)(2,1)} %all_to_all.18), calls=%async_computation | async-start | bytes 4194304 | tf_op jit(solution)/shard_map/all_to_all | solution.py:166
  24.8 0.0 copy-done.1
  24.9 0.1 fusion.71
  25.0 0.1 fusion.72
  25.2 0.3 pad_maximum_fusion
  25.5 0.1 fusion.73
  25.6 0.1 fusion.74
  25.7 0.3 pad_maximum_fusion.1
  26.0 0.8 bitcast_dynamic-update-slice_fusion.3
  26.8 0.8 bitcast_dynamic-update-slice_fusion.2
  27.6 0.7 constant_dynamic-update-slice_fusion
  28.3 0.8 bitcast_dynamic-update-slice_fusion.1
  29.1 0.8 bitcast_dynamic-update-slice_fusion
  29.9 95.0 %all-to-all-done = bf16[64,4,4096]{2,1,0:T(4,128)(2,1)S(1)} async-done(((bf16[64,4,4096]{2,1,0:T(4,128)(2,1)}), bf16[64,4,4096]{2,1,0:T(4,128)(2,1)S(1)}, u32[]{:S(2)}, u32[]{:S(2)}) %all-to-all-start) | async-done | bytes 2097184 | tf_op jit(solution)/shard_map/all_to_all | solution.py:166
  124.9 2.1 reshape.175
  127.0 2.8 %fusion.75 = f32[256,5,32]{0,2,1:T(8,128)S(1)} fusion(bf16[256,4096,1]{1,0,2:T(8,128)(2,1)} %reshape.175, bf16[5,32,4096]{2,1,0:T(8,128)(2,1)} %bitcast.2), kind=kOutput, calls=%fused_computation.193 | convolution fusion | flops 335544320 | bytes 3571712 | tf_op jit(solution)/shard_map/dot_general | solution.py:179
  129.8 0.9 broadcast_in_dim.10
  130.7 4.5 %all-to-all-start.1 = ((f32[4,256,5,32]{1,3,2,0:T(8,128)}), f32[4,256,5,32]{1,3,2,0:T(8,128)}, u32[]{:S(2)}, u32[]{:S(2)}) async-start(f32[4,256,5,32]{1,3,2,0:T(8,128)} %broadcast_in_dim.10), calls=%async_computation.1 | async-start | bytes 1310720 | tf_op jit(solution)/shard_map/all_to_all | solution.py:58
  135.2 1.9 reshape.149.idx_ref
  137.1 2.1 reshape.142
  139.2 5.8 %all-to-all-done.1 = f32[4,256,5,32]{1,3,2,0:T(8,128)} async-done(((f32[4,256,5,32]{1,3,2,0:T(8,128)}), f32[4,256,5,32]{1,3,2,0:T(8,128)}, u32[]{:S(2)}, u32[]{:S(2)}) %all-to-all-start.1) | async-done | bytes 655392 | tf_op jit(solution)/shard_map/all_to_all | solution.py:58
  145.0 1.2 fusion.69
  146.3 3.6 %fusion.76 = f32[160,4096]{1,0:T(8,128)} fusion(bf16[256,160]{0,1:T(8,128)(2,1)S(1)} %bitcast.351, bf16[256,4096]{1,0:T(8,128)(2,1)} %reshape.142), kind=kOutput, calls=%fused_computation.194 | convolution fusion | flops 335544320 | bytes 4800512 | tf_op jit(solution)/shard_map/dot_general | solution.py:187
  149.9 3.7 %reshape.148.w_ref = f32[5,1024,128]{2,1,0:T(8,128)} reshape(f32[160,4096]{1,0:T(8,128)} %fusion.76) | data formatting | bytes 5242880 | tf_op jit(solution)/shard_map/reshape | solution.py:194
  153.6 13.6 %shard_map.68 = f32[128,16,128]{2,1,0:T(8,128)} custom-call(f32[5,1024,128]{2,1,0:T(8,128)} %reshape.148.w_ref, s32[1024,128]{1,0:T(8,128)} %reshape.149.idx_ref), custom_call_target="tpu_custom_call" | custom-call | flops 1073741824 | bytes 4194304 | tf_op jit(solution)/shard_map/pallas_call | solution.py:130
  167.2 1.6 reshape_reshape.3
  168.8 1.1 constant_dynamic-slice_fusion.3
  169.9 0.0 copy-start.2
  169.9 0.2 copy.28
  170.1 1.9 collective-permute-start
  172.1 0.2 copy.27
  172.3 3.9 %collective-permute-start.1 = (f32[2,16,2048]{2,0,1:T(2,128)S(1)}, f32[2,16,2048]{2,0,1:T(2,128)S(1)}, u32[]{:S(2)}, u32[]{:S(2)}) collective-permute-start(f32[2,16,2048]{2,0,1:T(2,128)S(1)} %bitcast.353), channel_id=1, source_target_pairs={{0,8},{4,12},{8,0},{12,4},{1,9},{5,13},{9,1},{13,5},{2,10},{6,14},... | collective-permute-start | bytes 786440 | tf_op jit(solution)/shard_map/ppermute | solution.py:47
  176.2 0.2 copy.26
  176.4 2.0 collective-permute-start.2
  178.4 2.0 collective-permute-done
  180.3 4.1 %collective-permute-done.1 = f32[2,16,2048]{2,0,1:T(2,128)S(1)} collective-permute-done((f32[2,16,2048]{2,0,1:T(2,128)S(1)}, f32[2,16,2048]{2,0,1:T(2,128)S(1)}, u32[]{:S(2)}, u32[]{:S(2)}) %collective-permute-start.1) | collective-permute-done | bytes 262176 | tf_op jit(solution)/shard_map/ppermute | solution.py:47
  184.4 2.6 %collective-permute-done.2 = f32[2,16,2048]{2,0,1:T(2,128)S(1)} collective-permute-done((f32[2,16,2048]{2,0,1:T(2,128)S(1)}, f32[2,16,2048]{2,0,1:T(2,128)S(1)}, u32[]{:S(2)}, u32[]{:S(2)}) %collective-permute-start.2) | collective-permute-done | bytes 262176 | tf_op jit(solution)/shard_map/ppermute | solution.py:47
  187.0 1.1 fusion.6
  188.1 5.2 %all-to-all-start.2 = ((f32[16,2,2048]{2,1,0:T(2,128)}), f32[16,2,2048]{2,1,0:T(2,128)S(1)}, u32[]{:S(2)}, u32[]{:S(2)}) async-start(f32[16,2,2048]{2,1,0:T(2,128)} %fusion.6), calls=%async_computation.2 | async-start | bytes 524288 | tf_op jit(solution)/shard_map/all_to_all | solution.py:90
  193.3 0.0 copy-done.2
  193.3 1.9 collective-permute-start.4
  195.3 15.6 %all-to-all-done.2 = f32[16,2,2048]{2,1,0:T(2,128)S(1)} async-done(((f32[16,2,2048]{2,1,0:T(2,128)}), f32[16,2,2048]{2,1,0:T(2,128)S(1)}, u32[]{:S(2)}, u32[]{:S(2)}) %all-to-all-start.2) | async-done | bytes 262176 | tf_op jit(solution)/shard_map/all_to_all | solution.py:90
  210.9 0.1 fusion.15
  210.9 1.9 collective-permute-start.3
  212.9 0.0 collective-permute-done.4
  212.9 1.1 collective-permute-done.3
  214.1 1.0 fusion
  215.0 7.7 %all_to_all.29 = f32[4,3,128]{2,1,0:T(4,128)S(1)} all-to-all(f32[4,3,128]{2,1,0:T(4,128)S(1)} %broadcast_in_dim.11), channel_id=1, replica_groups=mesh['half'=2,'z'=16,'x'=4,'vol'=4] {'vol'}, dimensions={0} | all-to-all | bytes 12288 | tf_op jit(solution)/shard_map/all_to_all | solution.py:58
  222.7 0.7 broadcast_in_dim.13
  223.4 8.8 %all-to-all-start.4 = ((f32[64,3,128]{2,1,0:T(4,128)}), f32[64,3,128]{2,1,0:T(4,128)S(1)}, u32[]{:S(2)}, u32[]{:S(2)}) async-start(f32[64,3,128]{2,1,0:T(4,128)} %broadcast_in_dim.13), calls=%async_computation.4 | async-start | bytes 262144 | tf_op jit(solution)/shard_map/all_to_all | solution.py:58
  232.2 14.9 %all-to-all-done.4 = f32[64,3,128]{2,1,0:T(4,128)S(1)} async-done(((f32[64,3,128]{2,1,0:T(4,128)}), f32[64,3,128]{2,1,0:T(4,128)S(1)}, u32[]{:S(2)}, u32[]{:S(2)}) %all-to-all-start.4) | async-done | bytes 98336 | tf_op jit(solution)/shard_map/all_to_all | solution.py:58
  247.1 0.1 fusion.16
  247.1 0.7 slice_reduce_fusion.2
  249.8 0.7 fusion.2
  250.5 0.6 multiply_divide_fusion
  251.1 0.0 copy-done.3
  (14 shorter events, 0.2 us)
Async XLA Ops:
  0.6 2.5 %copy-start = (bf16[128,4096]{1,0:T(8,128)(2,1)S(1)}, bf16[128,4096]{1,0:T(8,128)(2,1)}, u32[]{:S(2)}) copy-start(bf16[128,4096]{1,0:T(8,128)(2,1)} %param.5) | copy-start | bytes 3145732
  6.1 18.7 %copy-start.1 = (bf16[32,4096]{1,0:T(8,128)(2,1)S(1)}, bf16[32,4096]{1,0:T(8,128)(2,1)}, u32[]{:S(2)}) copy-start(bf16[32,4096]{1,0:T(8,128)(2,1)} %param.7) | copy-start | bytes 786436
  6.1 118.9 %all-to-all-start = ((bf16[64,4,4096]{2,1,0:T(4,128)(2,1)}), bf16[64,4,4096]{2,1,0:T(4,128)(2,1)S(1)}, u32[]{:S(2)}, u32[]{:S(2)}) async-start(bf16[64,4,4096]{2,1,0:T(4,128)(2,1)} %all_to_all.18), calls=%async_computation | async-start | bytes 4194304 | tf_op jit(solution)/shard_map/all_to_all | solution.py:166
  130.7 14.3 %all-to-all-start.1 = ((f32[4,256,5,32]{1,3,2,0:T(8,128)}), f32[4,256,5,32]{1,3,2,0:T(8,128)}, u32[]{:S(2)}, u32[]{:S(2)}) async-start(f32[4,256,5,32]{1,3,2,0:T(8,128)} %broadcast_in_dim.10), calls=%async_computation.1 | async-start | bytes 1310720 | tf_op jit(solution)/shard_map/all_to_all | solution.py:58
  169.9 23.4 %copy-start.2 = (s32[1,2048]{1,0:T(1,128)S(1)}, s32[1,2048]{1,0:T(1,128)}, u32[]{:S(2)}) copy-start(s32[1,2048]{1,0:T(1,128)} %param.9) | copy-start | bytes 24580
  170.1 10.2 %collective-permute-start = (f32[2,16,2048]{2,0,1:T(2,128)S(1)}, f32[2,16,2048]{2,0,1:T(2,128)S(1)}, u32[]{:S(2)}, u32[]{:S(2)}) collective-permute-start(f32[2,16,2048]{2,0,1:T(2,128)S(1)} %bitcast.352), channel_id=1, source_target_pairs={{0,4},{4,8},{8,12},{12,0},{1,5},{5,9},{9,13},{13,1},{2,6},{6,10},{... | collective-permute-start | bytes 786440 | tf_op jit(solution)/shard_map/ppermute | solution.py:47
  172.3 12.1 %collective-permute-start.1 = (f32[2,16,2048]{2,0,1:T(2,128)S(1)}, f32[2,16,2048]{2,0,1:T(2,128)S(1)}, u32[]{:S(2)}, u32[]{:S(2)}) collective-permute-start(f32[2,16,2048]{2,0,1:T(2,128)S(1)} %bitcast.353), channel_id=1, source_target_pairs={{0,8},{4,12},{8,0},{12,4},{1,9},{5,13},{9,1},{13,5},{2,10},{6,14},... | collective-permute-start | bytes 786440 | tf_op jit(solution)/shard_map/ppermute | solution.py:47
  176.4 10.6 %collective-permute-start.2 = (f32[2,16,2048]{2,0,1:T(2,128)S(1)}, f32[2,16,2048]{2,0,1:T(2,128)S(1)}, u32[]{:S(2)}, u32[]{:S(2)}) collective-permute-start(f32[2,16,2048]{2,0,1:T(2,128)S(1)} %bitcast.354), channel_id=1, source_target_pairs={{0,12},{4,0},{8,4},{12,8},{1,13},{5,1},{9,5},{13,9},{2,14},{6,2},{... | collective-permute-start | bytes 786440 | tf_op jit(solution)/shard_map/ppermute | solution.py:47
  188.1 22.8 %all-to-all-start.2 = ((f32[16,2,2048]{2,1,0:T(2,128)}), f32[16,2,2048]{2,1,0:T(2,128)S(1)}, u32[]{:S(2)}, u32[]{:S(2)}) async-start(f32[16,2,2048]{2,1,0:T(2,128)} %fusion.6), calls=%async_computation.2 | async-start | bytes 524288 | tf_op jit(solution)/shard_map/all_to_all | solution.py:90
  193.3 19.6 %collective-permute-start.4 = (s32[2048]{0:T(1024)S(1)}, s32[2048]{0:T(1024)S(1)}, u32[]{:S(2)}, u32[]{:S(2)}) collective-permute-start(s32[2048]{0:T(1024)S(1)} %bitcast.363), channel_id=1, source_target_pairs={{0,256},{256,0},{1,257},{257,1},{2,258},{258,2},{3,259},{259,3},{4... | collective-permute-start | bytes 24584 | tf_op jit(solution)/shard_map/ppermute | solution.py:27
  210.9 3.1 %collective-permute-start.3 = (f32[4096]{0:T(1024)S(1)}, f32[4096]{0:T(1024)S(1)}, u32[]{:S(2)}, u32[]{:S(2)}) collective-permute-start(f32[4096]{0:T(1024)S(1)} %bitcast.355), channel_id=1, source_target_pairs={{0,256},{256,0},{1,257},{257,1},{2,258},{258,2},{3,259},{259,3},{4... | collective-permute-start | bytes 49160 | tf_op jit(solution)/shard_map/ppermute | solution.py:27
  223.4 23.7 %all-to-all-start.4 = ((f32[64,3,128]{2,1,0:T(4,128)}), f32[64,3,128]{2,1,0:T(4,128)S(1)}, u32[]{:S(2)}, u32[]{:S(2)}) async-start(f32[64,3,128]{2,1,0:T(4,128)} %broadcast_in_dim.13), calls=%async_computation.4 | async-start | bytes 262144 | tf_op jit(solution)/shard_map/all_to_all | solution.py:58
  247.8 3.3 %copy-start.3 = (f32[1,128]{1,0:T(1,128)}, f32[1,128]{1,0:T(1,128)S(1)}, u32[]{:S(2)}) copy-start(f32[1,128]{1,0:T(1,128)S(1)} %get-tuple-element.25) | copy-start | bytes 1540

commit v9 on v8

--- a/solution.py
+++ b/solution.py
@@ -74,24 +74,21 @@
     return x
 
 
+def exchange_rows(data, axis):
+    n = lax.axis_size(axis)
+    got = lax.all_to_all(jnp.moveaxis(data, 1, 0), axis, 0, 0, tiled=True)
+    total = got[0]
+    for i in range(1, n):
+        total = total + got[i]
+    return total
+
+
 def reduce_scatter(x, inner, outer):
-    me = lax.axis_index(inner)
     n_inner = lax.axis_size(inner)
     n_outer = lax.axis_size(outer)
-    data = x
-    for stride, radix in digits_of(n_inner):
-        d = (me // stride) % radix
-        data = data.reshape(data.shape[0], data.shape[1] // radix, radix, data.shape[2])
-        total = lax.dynamic_index_in_dim(data, d, axis=2, keepdims=False)
-        for s in range(1, radix):
-            send = lax.dynamic_index_in_dim(data, (d + s) % radix, axis=2, keepdims=False)
-            total = total + shift_in_digit(send, inner, stride, radix, s)
-        data = total
-    got = lax.all_to_all(jnp.swapaxes(data, 0, 1), outer, 0, 0, tiled=True)
-    total = got[0]
-    for i in range(1, n_outer):
-        total = total + got[i]
-    return total
+    a, _, length = x.shape
+    data = exchange_rows(jnp.swapaxes(x.reshape(a, n_outer, n_inner, length), 1, 2), inner)
+    return exchange_rows(data.reshape(a, n_outer, 1, length), outer)[:, 0]
 
 
 def _project_kernel(w_ref, idx_ref, out_ref, wt_ref, it_ref):
@@ -185,8 +182,8 @@
     mean_square = jnp.mean(squares, axis=(1, 2), keepdims=True)
     weights = (squares / (mean_square + EPS_W)).astype(jnp.bfloat16)
     weighted = lax.dot_general(
-        weights.reshape(slot_count, SHIFTS * class_count),
-        arrived,
+        weights,
+        arrived.reshape(slot_count, quarter_rows, IMG),
         (((0,), (0,)), ((), ())),
         preferred_element_type=jnp.float32,
     )

time: 253 us -> 247 us (0.976)
  blocking collectives: 7.66 us -> 22.4 us
  waiting for transfers between devices: 141 us -> 130 us
  starting transfers between devices: 48.8 us -> 40.8 us
    all_to_all x0 -> x1, blocking collectives: none -> 14.8 us  [exchange_rows(): got = lax.all_to_all(jnp.moveaxis(data, 1, 0), axis, 0, 0, tiled=True)]
    ppermute x3 -> x0, waiting for transfers between devices: 8.63 us -> none  [shift_in_digit(): return lax.ppermute(x, axis, perm)]
    ppermute x3 -> x0, starting transfers between devices: 7.76 us -> none  [shift_in_digit(): return lax.ppermute(x, axis, perm)]
    dot_general x0 -> x1, local copies, waits for them, and re-layouts: none -> 3 us  [shards(): lax.dot_general(weights, arrived.reshape(slot_count, quarter_rows, IMG),...]
  transfers between devices with their start and end apart: 9 -> 6, of which waited for: 8 -> 5; matrix products, arithmetic and copies ran while one was open for 4% -> 4% of each run, Pallas kernels for 0% -> 0%
where the time goes in v9:
time: 247 us; the launch traced here: 245 us
  waiting for transfers between devices  130 us (53%)
  starting transfers between devices  40.8 us (17%)
  blocking collectives  22.4 us (9%)
  local copies, waits for them, and re-layouts  21.6 us (9%)
  Pallas kernels  13.6 us (6%)
  matrix products  7.68 us (3%)
  other arithmetic  5.88 us (2%)
  between operations  2.81 us (1%)
    all_to_all x1, waiting for transfers between devices, shards(): lax.all_to_all(outgoing, CLS, split_axis=0, concat_axis=0, tiled=True)  95 us
    all_to_all x2, waiting for transfers between devices, exchange_sum(): lax.all_to_all(jnp.broadcast_to(x[None], (n,) + x.shape), axis, 0, 0, til...  19.6 us
    all_to_all x1, starting transfers between devices, shards(): lax.all_to_all(outgoing, CLS, split_axis=0, concat_axis=0, tiled=True)  18.7 us
    all_to_all x1, blocking collectives, exchange_rows(): got = lax.all_to_all(jnp.moveaxis(data, 1, 0), axis, 0, 0, tiled=True)  14.8 us
    all_to_all x1, waiting for transfers between devices, exchange_rows(): got = lax.all_to_all(jnp.moveaxis(data, 1, 0), axis, 0, 0, tiled=True)  14.6 us
    pallas_call x1, Pallas kernels, project(): pl.pallas_call(_project_kernel, out_shape=jax.ShapeDtypeStruct((q_count,...  13.6 us
    all_to_all x2, starting transfers between devices, exchange_sum(): lax.all_to_all(jnp.broadcast_to(x[None], (n,) + x.shape), axis, 0, 0, til...  13 us
    all_to_all x1, blocking collectives, exchange_sum(): lax.all_to_all(jnp.broadcast_to(x[None], (n,) + x.shape), axis, 0, 0, til...  7.66 us
  transfers between devices with their start and end apart: 6, of which 5 were waited for; matrix products, arithmetic and copies ran while one was open for 4% of the time, Pallas kernels for 0%

profile of v9, /device:TPU:6, one launch (start us, length us, event | category | flops | bytes accessed | tf_op | source)
XLA Modules:
  0.0 245.0 jit_solution(16826346283968701727)
XLA Ops:
  0.6 0.0 copy-start
  0.6 0.8 fusion.16
  1.5 0.2 reduce_window_sum.11
  1.6 0.8 select_reduce_fusion
  2.5 0.7 add_add_fusion
  3.1 0.0 copy-done
  3.1 0.7 convolution_convert_fusion
  3.9 2.2 all_to_all.21
  6.1 0.0 copy-start.1
  6.1 18.7 %all-to-all-start = ((bf16[64,4,4096]{2,1,0:T(4,128)(2,1)}), bf16[64,4,4096]{2,1,0:T(4,128)(2,1)S(1)}, u32[]{:S(2)}, u32[]{:S(2)}) async-start(bf16[64,4,4096]{2,1,0:T(4,128)(2,1)} %all_to_all.21), calls=%async_computation | async-start | bytes 4194304 | tf_op jit(solution)/shard_map/all_to_all | solution.py:163
  24.8 0.0 copy-done.1
  24.9 0.1 fusion.72
  25.0 0.1 fusion.73
  25.1 0.3 pad_maximum_fusion
  25.4 0.1 fusion.74
  25.6 0.1 fusion.75
  25.7 0.3 pad_maximum_fusion.1
  26.0 0.8 bitcast_dynamic-update-slice_fusion.3
  26.8 0.8 bitcast_dynamic-update-slice_fusion.2
  27.6 0.7 constant_dynamic-update-slice_fusion
  28.3 0.8 bitcast_dynamic-update-slice_fusion.1
  29.1 0.8 bitcast_dynamic-update-slice_fusion
  29.9 95.0 %all-to-all-done = bf16[64,4,4096]{2,1,0:T(4,128)(2,1)S(1)} async-done(((bf16[64,4,4096]{2,1,0:T(4,128)(2,1)}), bf16[64,4,4096]{2,1,0:T(4,128)(2,1)S(1)}, u32[]{:S(2)}, u32[]{:S(2)}) %all-to-all-start) | async-done | bytes 2097184 | tf_op jit(solution)/shard_map/all_to_all | solution.py:163
  124.9 2.1 reshape.255
  127.0 2.8 %fusion.76 = f32[256,5,32]{0,2,1:T(8,128)S(1)} fusion(bf16[256,4096,1]{1,0,2:T(8,128)(2,1)} %reshape.255, bf16[5,32,4096]{2,1,0:T(8,128)(2,1)} %bitcast.2), kind=kOutput, calls=%fused_computation.190 | convolution fusion | flops 335544320 | bytes 3571712 | tf_op jit(solution)/shard_map/dot_general | solution.py:176
  129.8 0.9 broadcast_in_dim.10
  130.7 4.5 %all-to-all-start.1 = ((f32[4,256,5,32]{1,3,2,0:T(8,128)}), f32[4,256,5,32]{1,3,2,0:T(8,128)}, u32[]{:S(2)}, u32[]{:S(2)}) async-start(f32[4,256,5,32]{1,3,2,0:T(8,128)} %broadcast_in_dim.10), calls=%async_computation.1 | async-start | bytes 1310720 | tf_op jit(solution)/shard_map/all_to_all | solution.py:58
  135.2 1.9 reshape.229.idx_ref
  137.1 3.2 %reshape.227 = bf16[256,32,128]{2,1,0:T(8,128)(2,1)} reshape(bf16[64,4,4096]{2,1,0:T(4,128)(2,1)S(1)} %all-to-all-done) | data formatting | bytes 4194304 | tf_op jit(solution)/shard_map/reshape | solution.py:186
  140.3 4.7 %all-to-all-done.1 = f32[4,256,5,32]{1,3,2,0:T(8,128)} async-done(((f32[4,256,5,32]{1,3,2,0:T(8,128)}), f32[4,256,5,32]{1,3,2,0:T(8,128)}, u32[]{:S(2)}, u32[]{:S(2)}) %all-to-all-start.1) | async-done | bytes 655392 | tf_op jit(solution)/shard_map/all_to_all | solution.py:58
  145.0 1.2 fusion.70
  146.2 2.5 %fusion = f32[5,32,32,128]{3,1,2,0:T(8,128)S(1)} fusion(bf16[256,32,128]{2,1,0:T(8,128)(2,1)} %reshape.227, f32[1,256,5,32]{1,3,2,0:T(8,128)S(1)} %get-tuple-element.10, f32[256]{0:T(256)S(1)} %multiply_add_fusion), kind=kOutput, calls=%fused_computation.1 | convolution fusion | flops 335626240 | bytes 4883456 | tf_op jit(solution)/shard_map/dot_general | solution.py:184
  148.7 3.0 %copy.11 = f32[5,32,32,128]{3,2,1,0:T(8,128)} copy(f32[5,32,32,128]{3,1,2,0:T(8,128)S(1)} %fusion) | data formatting | bytes 5242880 | tf_op jit(solution)/shard_map/dot_general | solution.py:184
  151.7 13.6 %shard_map.68 = f32[128,16,128]{2,1,0:T(8,128)} custom-call(f32[5,1024,128]{2,1,0:T(8,128)} %bitcast.339, s32[1024,128]{1,0:T(8,128)} %reshape.229.idx_ref), custom_call_target="tpu_custom_call" | custom-call | flops 1073741824 | bytes 4194304 | tf_op jit(solution)/shard_map/pallas_call | solution.py:127
  165.3 1.6 reshape_reshape.3
  166.9 0.6 copy.29
  167.5 0.0 copy-start.2
  167.5 14.8 %all_to_all.34 = f32[4,2,16,2048]{3,2,1,0:T(8,128)S(1)} all-to-all(f32[4,2,16,2048]{3,2,1,0:T(8,128)S(1)} %bitcast.340), channel_id=1, replica_groups=mesh['half'=2,'z'=16,'x'=4,'vol'=4] {'x'}, dimensions={0} | all-to-all | bytes 2097152 | tf_op jit(solution)/shard_map/all_to_all | solution.py:79
  182.3 0.1 fusion.7
  182.3 1.0 copy.13
  183.3 5.0 %all-to-all-start.3 = ((f32[16,2,1,2048]{3,2,1,0:T(1,128)}), f32[16,2,1,2048]{3,2,1,0:T(1,128)S(1)}, u32[]{:S(2)}, u32[]{:S(2)}) async-start(f32[16,2,1,2048]{3,2,1,0:T(1,128)} %copy.13), calls=%async_computation.3 | async-start | bytes 524288 | tf_op jit(solution)/shard_map/all_to_all | solution.py:79
  188.3 0.0 copy-done.2
  188.4 1.9 collective-permute-start.1
  190.3 14.6 %all-to-all-done.3 = f32[16,2,1,2048]{3,2,1,0:T(1,128)S(1)} async-done(((f32[16,2,1,2048]{3,2,1,0:T(1,128)}), f32[16,2,1,2048]{3,2,1,0:T(1,128)S(1)}, u32[]{:S(2)}, u32[]{:S(2)}) %all-to-all-start.3) | async-done | bytes 262176 | tf_op jit(solution)/shard_map/all_to_all | solution.py:79
  204.9 0.1 slice_add_fusion.6
  205.0 2.1 collective-permute-start
  207.1 0.0 collective-permute-done.1
  207.2 0.9 collective-permute-done
  208.1 1.0 fusion.3
  209.1 7.7 %all_to_all.35 = f32[4,3,128]{2,1,0:T(4,128)S(1)} all-to-all(f32[4,3,128]{2,1,0:T(4,128)S(1)} %broadcast_in_dim.11), channel_id=1, replica_groups=mesh['half'=2,'z'=16,'x'=4,'vol'=4] {'vol'}, dimensions={0} | all-to-all | bytes 12288 | tf_op jit(solution)/shard_map/all_to_all | solution.py:58
  216.8 0.7 broadcast_in_dim.13
  217.5 8.6 %all-to-all-start.5 = ((f32[64,3,128]{2,1,0:T(4,128)}), f32[64,3,128]{2,1,0:T(4,128)S(1)}, u32[]{:S(2)}, u32[]{:S(2)}) async-start(f32[64,3,128]{2,1,0:T(4,128)} %broadcast_in_dim.13), calls=%async_computation.5 | async-start | bytes 262144 | tf_op jit(solution)/shard_map/all_to_all | solution.py:58
  226.1 14.9 %all-to-all-done.5 = f32[64,3,128]{2,1,0:T(4,128)S(1)} async-done(((f32[64,3,128]{2,1,0:T(4,128)}), f32[64,3,128]{2,1,0:T(4,128)S(1)}, u32[]{:S(2)}, u32[]{:S(2)}) %all-to-all-start.5) | async-done | bytes 98336 | tf_op jit(solution)/shard_map/all_to_all | solution.py:58
  241.0 0.1 fusion.17
  241.1 0.7 slice_reduce_fusion.2
  241.7 0.0 copy-start.3
  243.7 0.7 fusion.5
  244.4 0.6 multiply_divide_fusion
  245.0 0.0 copy-done.3
  (10 shorter events, 0.1 us)
Async XLA Ops:
  0.6 2.5 %copy-start = (bf16[128,4096]{1,0:T(8,128)(2,1)S(1)}, bf16[128,4096]{1,0:T(8,128)(2,1)}, u32[]{:S(2)}) copy-start(bf16[128,4096]{1,0:T(8,128)(2,1)} %param.5) | copy-start | bytes 3145732
  6.1 18.7 %copy-start.1 = (bf16[32,4096]{1,0:T(8,128)(2,1)S(1)}, bf16[32,4096]{1,0:T(8,128)(2,1)}, u32[]{:S(2)}) copy-start(bf16[32,4096]{1,0:T(8,128)(2,1)} %param.7) | copy-start | bytes 786436
  6.1 118.9 %all-to-all-start = ((bf16[64,4,4096]{2,1,0:T(4,128)(2,1)}), bf16[64,4,4096]{2,1,0:T(4,128)(2,1)S(1)}, u32[]{:S(2)}, u32[]{:S(2)}) async-start(bf16[64,4,4096]{2,1,0:T(4,128)(2,1)} %all_to_all.21), calls=%async_computation | async-start | bytes 4194304 | tf_op jit(solution)/shard_map/all_to_all | solution.py:163
  130.7 14.3 %all-to-all-start.1 = ((f32[4,256,5,32]{1,3,2,0:T(8,128)}), f32[4,256,5,32]{1,3,2,0:T(8,128)}, u32[]{:S(2)}, u32[]{:S(2)}) async-start(f32[4,256,5,32]{1,3,2,0:T(8,128)} %broadcast_in_dim.10), calls=%async_computation.1 | async-start | bytes 1310720 | tf_op jit(solution)/shard_map/all_to_all | solution.py:58
  167.5 20.8 %copy-start.2 = (s32[1,2048]{1,0:T(1,128)S(1)}, s32[1,2048]{1,0:T(1,128)}, u32[]{:S(2)}) copy-start(s32[1,2048]{1,0:T(1,128)} %param.9) | copy-start | bytes 24580
  183.3 21.6 %all-to-all-start.3 = ((f32[16,2,1,2048]{3,2,1,0:T(1,128)}), f32[16,2,1,2048]{3,2,1,0:T(1,128)S(1)}, u32[]{:S(2)}, u32[]{:S(2)}) async-start(f32[16,2,1,2048]{3,2,1,0:T(1,128)} %copy.13), calls=%async_computation.3 | async-start | bytes 524288 | tf_op jit(solution)/shard_map/all_to_all | solution.py:79
  188.4 18.8 %collective-permute-start.1 = (s32[2048]{0:T(1024)S(1)}, s32[2048]{0:T(1024)S(1)}, u32[]{:S(2)}, u32[]{:S(2)}) collective-permute-start(s32[2048]{0:T(1024)S(1)} %bitcast.354), channel_id=1, source_target_pairs={{0,256},{256,0},{1,257},{257,1},{2,258},{258,2},{3,259},{259,3},{4... | collective-permute-start | bytes 24584 | tf_op jit(solution)/shard_map/ppermute | solution.py:27
  205.0 3.1 %collective-permute-start = (f32[4096]{0:T(1024)S(1)}, f32[4096]{0:T(1024)S(1)}, u32[]{:S(2)}, u32[]{:S(2)}) collective-permute-start(f32[4096]{0:T(1024)S(1)} %bitcast.346), channel_id=1, source_target_pairs={{0,256},{256,0},{1,257},{257,1},{2,258},{258,2},{3,259},{259,3},{4... | collective-permute-start | bytes 49160 | tf_op jit(solution)/shard_map/ppermute | solution.py:27
  217.5 23.5 %all-to-all-start.5 = ((f32[64,3,128]{2,1,0:T(4,128)}), f32[64,3,128]{2,1,0:T(4,128)S(1)}, u32[]{:S(2)}, u32[]{:S(2)}) async-start(f32[64,3,128]{2,1,0:T(4,128)} %broadcast_in_dim.13), calls=%async_computation.5 | async-start | bytes 262144 | tf_op jit(solution)/shard_map/all_to_all | solution.py:58
  241.7 3.3 %copy-start.3 = (f32[1,128]{1,0:T(1,128)}, f32[1,128]{1,0:T(1,128)S(1)}, u32[]{:S(2)}) copy-start(f32[1,128]{1,0:T(1,128)S(1)} %get-tuple-element.21) | copy-start | bytes 1540

commit v10 on v9

--- a/solution.py
+++ b/solution.py
@@ -157,24 +157,24 @@
     order_in = jnp.sum(jnp.cumsum(matches, axis=0) * matches, axis=1) - 1
     slot_ids = owner_ids * capacity + order_in
     slot_hits = slot_ids[None, :] == jnp.arange(slot_count, dtype=jnp.int32)[:, None]
-    outgoing = jnp.dot(
-        slot_hits.astype(jnp.bfloat16), images, preferred_element_type=jnp.float32
-    ).astype(jnp.bfloat16)
-    arrived = lax.all_to_all(outgoing, CLS, split_axis=0, concat_axis=0, tiled=True)
     quarter_rows = pix_quarter // IMG
     bins = VOXS // IMG
+    outgoing = lax.dot_general(
+        slot_hits.astype(jnp.bfloat16),
+        images.reshape(part_count, quarter_rows, IMG),
+        (((1,), (0,)), ((), ())),
+        preferred_element_type=jnp.float32,
+    ).astype(jnp.bfloat16)
+    arrived = lax.all_to_all(
+        outgoing.reshape(n_cls, capacity, quarter_rows, IMG), CLS, split_axis=0, concat_axis=0, tiled=True
+    ).reshape(slot_count, quarter_rows, IMG)
     shaped_refs = references.reshape(class_count, quarter_rows, IMG)
     rolled_refs = jnp.concatenate(
-        [
-            jnp.roll(shaped_refs, -(shift_id - SHIFTS // 2), axis=2).reshape(
-                class_count, pix_quarter
-            )
-            for shift_id in range(SHIFTS)
-        ],
+        [jnp.roll(shaped_refs, -(shift_id - SHIFTS // 2), axis=2) for shift_id in range(SHIFTS)],
         axis=0,
     )
     partial_scores = lax.dot_general(
-        arrived, rolled_refs, (((1,), (1,)), ((), ())), preferred_element_type=jnp.float32
+        arrived, rolled_refs, (((1, 2), (1, 2)), ((), ())), preferred_element_type=jnp.float32
     )
     partial_scores = partial_scores.reshape(slot_count, SHIFTS, class_count)
     scores = exchange_sum(partial_scores, "vol")
@@ -182,8 +182,8 @@
     mean_square = jnp.mean(squares, axis=(1, 2), keepdims=True)
     weights = (squares / (mean_square + EPS_W)).astype(jnp.bfloat16)
     weighted = lax.dot_general(
-        weights,
-        arrived.reshape(slot_count, quarter_rows, IMG),
+        weights.reshape(slot_count, SHIFTS * class_count),
+        arrived,
         (((0,), (0,)), ((), ())),
         preferred_element_type=jnp.float32,
     )

time: 247 us -> 245 us (level)
  local copies, waits for them, and re-layouts: 21.6 us -> 16.2 us
  waiting for transfers between devices: 130 us -> 134 us
  other arithmetic: 5.88 us -> 8.67 us
  matrix products: 7.68 us -> 4.95 us
    all_to_all x2, waiting for transfers between devices: 19.6 us -> 22.8 us  [exchange_sum(): lax.all_to_all(jnp.broadcast_to(x[None], (n,) + x.shape), axis, 0, 0, til...]
    dot_general x3, matrix products: 5.99 us -> 3.26 us  [the longest x1 2.05 us: shards(): lax.dot_general(arrived, rolled_refs, (((1, 2), (1, 2)), ((), ())), prefe...]
    unnamed x0 -> x3, other arithmetic: none -> 2.56 us
  transfers between devices with their start and end apart: 6 -> 6, of which waited for: 5 -> 5; matrix products, arithmetic and copies ran while one was open for 4% -> 3% of each run, Pallas kernels for 0% -> 0%
where the time goes in v10:
time: 245 us; the launch traced here: 243 us
  waiting for transfers between devices  134 us (55%)
  starting transfers between devices  41 us (17%)
  blocking collectives  22.4 us (9%)
  local copies, waits for them, and re-layouts  16.2 us (7%)
  Pallas kernels  13.6 us (6%)
  other arithmetic  8.67 us (4%)
  matrix products  4.95 us (2%)
  between operations  2.79 us (1%)
    all_to_all x1, waiting for transfers between devices, shards(): lax.all_to_all(outgoing.reshape(n_cls, capacity, quarter_rows, IMG), CLS,...  95.3 us
    all_to_all x2, waiting for transfers between devices, exchange_sum(): lax.all_to_all(jnp.broadcast_to(x[None], (n,) + x.shape), axis, 0, 0, til...  22.8 us
    all_to_all x1, starting transfers between devices, shards(): lax.all_to_all(outgoing.reshape(n_cls, capacity, quarter_rows, IMG), CLS,...  18.9 us
    all_to_all x1, blocking collectives, exchange_rows(): got = lax.all_to_all(jnp.moveaxis(data, 1, 0), axis, 0, 0, tiled=True)  14.8 us
    all_to_all x1, waiting for transfers between devices, exchange_rows(): got = lax.all_to_all(jnp.moveaxis(data, 1, 0), axis, 0, 0, tiled=True)  14.7 us
    pallas_call x1, Pallas kernels, project(): pl.pallas_call(_project_kernel, out_shape=jax.ShapeDtypeStruct((q_count,...  13.6 us
    all_to_all x2, starting transfers between devices, exchange_sum(): lax.all_to_all(jnp.broadcast_to(x[None], (n,) + x.shape), axis, 0, 0, til...  13 us
    all_to_all x1, blocking collectives, exchange_sum(): lax.all_to_all(jnp.broadcast_to(x[None], (n,) + x.shape), axis, 0, 0, til...  7.66 us
  transfers between devices with their start and end apart: 6, of which 5 were waited for; matrix products, arithmetic and copies ran while one was open for 3% of the time, Pallas kernels for 0%

profile of v10, /device:TPU:6, one launch (start us, length us, event | category | flops | bytes accessed | tf_op | source)
XLA Modules:
  0.0 243.3 jit_solution(14973276831724859745)
XLA Ops:
  0.6 0.0 copy-start
  0.6 0.8 fusion.21
  1.5 0.2 reduce_window_sum.11
  1.6 0.8 select_reduce_fusion
  2.5 0.7 add_add_fusion
  3.1 0.0 copy-done
  3.1 0.7 convolution_convert_fusion
  3.9 2.5 %copy.13 = bf16[64,4,32,128]{3,1,2,0:T(4,128)(2,1)} copy(bf16[64,4,32,128]{3,1,0,2:T(4,128)(2,1)S(1)} %bitcast.343) | data formatting | bytes 4194304 | tf_op jit(solution)/shard_map/reshape | solution.py:169
  6.3 0.0 copy-start.1
  6.3 18.9 %all-to-all-start = ((bf16[64,4,32,128]{3,1,2,0:T(4,128)(2,1)}), bf16[64,4,32,128]{3,1,2,0:T(4,128)(2,1)}, u32[]{:S(2)}, u32[]{:S(2)}) async-start(bf16[64,4,32,128]{3,1,2,0:T(4,128)(2,1)} %copy.13), calls=%async_computation | async-start | bytes 4194304 | tf_op jit(solution)/shard_map/all_to_all | solution.py:168
  25.2 0.0 copy-done.1
  25.3 0.1 fusion.77
  25.4 0.1 fusion.78
  25.6 0.8 maximum_dynamic-update-slice_fusion.3
  26.4 0.1 fusion.79
  26.6 0.1 fusion.80
  26.7 0.9 maximum_dynamic-update-slice_fusion.2
  27.6 0.7 constant_dynamic-update-slice_fusion
  28.3 0.9 maximum_dynamic-update-slice_fusion.1
  29.2 0.8 maximum_dynamic-update-slice_fusion
  30.0 95.3 %all-to-all-done = bf16[64,4,32,128]{3,1,2,0:T(4,128)(2,1)} async-done(((bf16[64,4,32,128]{3,1,2,0:T(4,128)(2,1)}), bf16[64,4,32,128]{3,1,2,0:T(4,128)(2,1)}, u32[]{:S(2)}, u32[]{:S(2)}) %all-to-all-start) | async-done | bytes 2097184 | tf_op jit(solution)/shard_map/all_to_all | solution.py:168
  125.3 2.7 %copy.14 = bf16[64,4,32,128]{3,1,0,2:T(4,128)(2,1)S(1)} copy(bf16[64,4,32,128]{3,1,2,0:T(4,128)(2,1)} %all-to-all-done) | data formatting | bytes 4194304 | tf_op jit(solution)/shard_map/all_to_all | solution.py:168
  128.0 2.1 fusion.3
  130.0 0.9 broadcast_in_dim.10
  130.9 4.5 %all-to-all-start.1 = ((f32[4,256,5,32]{1,3,2,0:T(8,128)}), f32[4,256,5,32]{1,3,2,0:T(8,128)}, u32[]{:S(2)}, u32[]{:S(2)}) async-start(f32[4,256,5,32]{1,3,2,0:T(8,128)} %broadcast_in_dim.10), calls=%async_computation.1 | async-start | bytes 1310720 | tf_op jit(solution)/shard_map/all_to_all | solution.py:58
  135.4 1.9 reshape.226.idx_ref
  137.3 7.9 %all-to-all-done.1 = f32[4,256,5,32]{1,3,2,0:T(8,128)} async-done(((f32[4,256,5,32]{1,3,2,0:T(8,128)}), f32[4,256,5,32]{1,3,2,0:T(8,128)}, u32[]{:S(2)}, u32[]{:S(2)}) %all-to-all-start.1) | async-done | bytes 655392 | tf_op jit(solution)/shard_map/all_to_all | solution.py:58
  145.3 1.2 fusion.75
  146.5 0.5 fusion.81
  147.0 3.0 %copy.16 = f32[160,32,128]{2,1,0:T(8,128)} copy(f32[160,32,128]{2,0,1:T(8,128)S(1)} %fusion.81) | data formatting | bytes 5242880 | tf_op jit(solution)/shard_map/dot_general | solution.py:184
  150.1 13.6 %shard_map.68 = f32[128,16,128]{2,1,0:T(8,128)} custom-call(f32[5,1024,128]{2,1,0:T(8,128)} %bitcast.340, s32[1024,128]{1,0:T(8,128)} %reshape.226.idx_ref), custom_call_target="tpu_custom_call" | custom-call | flops 1073741824 | bytes 4194304 | tf_op jit(solution)/shard_map/pallas_call | solution.py:127
  163.6 1.6 reshape_reshape.3
  165.2 0.6 copy.31
  165.8 14.8 %all_to_all.30 = f32[4,2,16,2048]{3,2,1,0:T(8,128)S(1)} all-to-all(f32[4,2,16,2048]{3,2,1,0:T(8,128)S(1)} %bitcast.344), channel_id=1, replica_groups=mesh['half'=2,'z'=16,'x'=4,'vol'=4] {'x'}, dimensions={0} | all-to-all | bytes 2097152 | tf_op jit(solution)/shard_map/all_to_all | solution.py:79
  180.6 0.0 copy-start.2
  180.6 0.1 fusion.11
  180.6 1.0 copy.18
  181.6 5.0 %all-to-all-start.3 = ((f32[16,2,1,2048]{3,2,1,0:T(1,128)}), f32[16,2,1,2048]{3,2,1,0:T(1,128)S(1)}, u32[]{:S(2)}, u32[]{:S(2)}) async-start(f32[16,2,1,2048]{3,2,1,0:T(1,128)} %copy.18), calls=%async_computation.3 | async-start | bytes 524288 | tf_op jit(solution)/shard_map/all_to_all | solution.py:79
  186.6 0.0 copy-done.2
  186.7 1.9 collective-permute-start.1
  188.6 14.7 %all-to-all-done.3 = f32[16,2,1,2048]{3,2,1,0:T(1,128)S(1)} async-done(((f32[16,2,1,2048]{3,2,1,0:T(1,128)}), f32[16,2,1,2048]{3,2,1,0:T(1,128)S(1)}, u32[]{:S(2)}, u32[]{:S(2)}) %all-to-all-start.3) | async-done | bytes 262176 | tf_op jit(solution)/shard_map/all_to_all | solution.py:79
  203.2 0.1 slice_add_fusion.6
  203.4 2.1 collective-permute-start
  205.5 0.0 collective-permute-done.1
  205.5 0.9 collective-permute-done
  206.5 1.0 fusion
  207.4 7.7 %all_to_all.31 = f32[4,3,128]{2,1,0:T(4,128)S(1)} all-to-all(f32[4,3,128]{2,1,0:T(4,128)S(1)} %broadcast_in_dim.11), channel_id=1, replica_groups=mesh['half'=2,'z'=16,'x'=4,'vol'=4] {'vol'}, dimensions={0} | all-to-all | bytes 12288 | tf_op jit(solution)/shard_map/all_to_all | solution.py:58
  215.1 0.7 broadcast_in_dim.13
  215.8 8.6 %all-to-all-start.5 = ((f32[64,3,128]{2,1,0:T(4,128)}), f32[64,3,128]{2,1,0:T(4,128)S(1)}, u32[]{:S(2)}, u32[]{:S(2)}) async-start(f32[64,3,128]{2,1,0:T(4,128)} %broadcast_in_dim.13), calls=%async_computation.5 | async-start | bytes 262144 | tf_op jit(solution)/shard_map/all_to_all | solution.py:58
  224.4 14.9 %all-to-all-done.5 = f32[64,3,128]{2,1,0:T(4,128)S(1)} async-done(((f32[64,3,128]{2,1,0:T(4,128)}), f32[64,3,128]{2,1,0:T(4,128)S(1)}, u32[]{:S(2)}, u32[]{:S(2)}) %all-to-all-start.5) | async-done | bytes 98336 | tf_op jit(solution)/shard_map/all_to_all | solution.py:58
  239.3 0.1 fusion.22
  239.4 0.6 slice_reduce_fusion.2
  240.0 0.0 copy-start.3
  241.9 0.7 fusion.9
  242.6 0.6 multiply_divide_fusion
  243.3 0.0 copy-done.3
  (11 shorter events, 0.2 us)
Async XLA Ops:
  0.6 2.5 %copy-start = (bf16[128,4096]{1,0:T(8,128)(2,1)S(1)}, bf16[128,4096]{1,0:T(8,128)(2,1)}, u32[]{:S(2)}) copy-start(bf16[128,4096]{1,0:T(8,128)(2,1)} %param.5) | copy-start | bytes 3145732
  6.3 18.9 %copy-start.1 = (bf16[32,4096]{1,0:T(8,128)(2,1)S(1)}, bf16[32,4096]{1,0:T(8,128)(2,1)}, u32[]{:S(2)}) copy-start(bf16[32,4096]{1,0:T(8,128)(2,1)} %param.7) | copy-start | bytes 786436
  6.3 119.0 %all-to-all-start = ((bf16[64,4,32,128]{3,1,2,0:T(4,128)(2,1)}), bf16[64,4,32,128]{3,1,2,0:T(4,128)(2,1)}, u32[]{:S(2)}, u32[]{:S(2)}) async-start(bf16[64,4,32,128]{3,1,2,0:T(4,128)(2,1)} %copy.13), calls=%async_computation | async-start | bytes 4194304 | tf_op jit(solution)/shard_map/all_to_all | solution.py:168
  130.9 14.3 %all-to-all-start.1 = ((f32[4,256,5,32]{1,3,2,0:T(8,128)}), f32[4,256,5,32]{1,3,2,0:T(8,128)}, u32[]{:S(2)}, u32[]{:S(2)}) async-start(f32[4,256,5,32]{1,3,2,0:T(8,128)} %broadcast_in_dim.10), calls=%async_computation.1 | async-start | bytes 1310720 | tf_op jit(solution)/shard_map/all_to_all | solution.py:58
  180.6 6.1 %copy-start.2 = (s32[1,2048]{1,0:T(1,128)S(1)}, s32[1,2048]{1,0:T(1,128)}, u32[]{:S(2)}) copy-start(s32[1,2048]{1,0:T(1,128)} %param.9) | copy-start | bytes 24580
  181.6 21.6 %all-to-all-start.3 = ((f32[16,2,1,2048]{3,2,1,0:T(1,128)}), f32[16,2,1,2048]{3,2,1,0:T(1,128)S(1)}, u32[]{:S(2)}, u32[]{:S(2)}) async-start(f32[16,2,1,2048]{3,2,1,0:T(1,128)} %copy.18), calls=%async_computation.3 | async-start | bytes 524288 | tf_op jit(solution)/shard_map/all_to_all | solution.py:79
  186.7 18.8 %collective-permute-start.1 = (s32[2048]{0:T(1024)S(1)}, s32[2048]{0:T(1024)S(1)}, u32[]{:S(2)}, u32[]{:S(2)}) collective-permute-start(s32[2048]{0:T(1024)S(1)} %bitcast.355), channel_id=1, source_target_pairs={{0,256},{256,0},{1,257},{257,1},{2,258},{258,2},{3,259},{259,3},{4... | collective-permute-start | bytes 24584 | tf_op jit(solution)/shard_map/ppermute | solution.py:27
  203.4 3.1 %collective-permute-start = (f32[4096]{0:T(1024)S(1)}, f32[4096]{0:T(1024)S(1)}, u32[]{:S(2)}, u32[]{:S(2)}) collective-permute-start(f32[4096]{0:T(1024)S(1)} %bitcast.347), channel_id=1, source_target_pairs={{0,256},{256,0},{1,257},{257,1},{2,258},{258,2},{3,259},{259,3},{4... | collective-permute-start | bytes 49160 | tf_op jit(solution)/shard_map/ppermute | solution.py:27
  215.8 23.5 %all-to-all-start.5 = ((f32[64,3,128]{2,1,0:T(4,128)}), f32[64,3,128]{2,1,0:T(4,128)S(1)}, u32[]{:S(2)}, u32[]{:S(2)}) async-start(f32[64,3,128]{2,1,0:T(4,128)} %broadcast_in_dim.13), calls=%async_computation.5 | async-start | bytes 262144 | tf_op jit(solution)/shard_map/all_to_all | solution.py:58
  240.0 3.3 %copy-start.3 = (f32[1,128]{1,0:T(1,128)}, f32[1,128]{1,0:T(1,128)S(1)}, u32[]{:S(2)}) copy-start(f32[1,128]{1,0:T(1,128)S(1)} %get-tuple-element.21) | copy-start | bytes 1540

commit v11 on v10

--- a/solution.py
+++ b/solution.py
@@ -84,11 +84,22 @@
 
 
 def reduce_scatter(x, inner, outer):
+    n_half = lax.axis_size("half")
     n_inner = lax.axis_size(inner)
     n_outer = lax.axis_size(outer)
-    a, _, length = x.shape
-    data = exchange_rows(jnp.swapaxes(x.reshape(a, n_outer, n_inner, length), 1, 2), inner)
-    return exchange_rows(data.reshape(a, n_outer, 1, length), outer)[:, 0]
+    length = x.shape[2]
+    data = x.reshape(n_half, n_outer, n_inner, length).transpose(0, 2, 1, 3)
+    got = lax.all_to_all(
+        data.reshape(n_half * n_inner, n_outer, length), ("half", inner), 0, 0, tiled=True
+    ).reshape(n_half, n_inner, n_outer, length)
+    part = got[:, 0]
+    for i in range(1, n_inner):
+        part = part + got[:, i]
+    got = lax.all_to_all(jnp.swapaxes(part, 0, 1), outer, 0, 0, tiled=True)
+    total = got[0]
+    for i in range(1, n_outer):
+        total = total + got[i]
+    return total
 
 
 def _project_kernel(w_ref, idx_ref, out_ref, wt_ref, it_ref):
@@ -194,31 +205,18 @@
     )
     piece_len = VOXS // (n_half * n_cls)
     slab_part = slab_part.reshape(n_half, n_cls, piece_len)
-    own_block = reduce_scatter(slab_part, "x", "z").reshape(-1)
-    half_id = lax.axis_index("half")
-    other_block = partner(own_block, "half", 0)
-    other_shell = partner(shell_index[0], "half", 0)
-    first_block = jnp.where(half_id == 0, own_block, other_block)
-    second_block = jnp.where(half_id == 0, other_block, own_block)
-    shell_block = jnp.where(
-        half_id == 0,
-        jnp.concatenate([shell_index[0], other_shell]),
-        jnp.concatenate([other_shell, shell_index[0]]),
-    )
-    block_hot = (shell_block[:, None] == jnp.arange(NSHELL, dtype=jnp.int32)[None, :]).astype(
+    maps = reduce_scatter(slab_part, "x", "z")
+    first = maps[0]
+    second = maps[1]
+    shell_hot = (shell_index[0][:, None] == jnp.arange(NSHELL, dtype=jnp.int32)[None, :]).astype(
         jnp.float32
     )
-    stats = jnp.stack([first_block * first_block, second_block * second_block, first_block * second_block])
-    shell_terms = jnp.dot(stats, block_hot, precision=lax.Precision.HIGHEST)
-    shell_sums = exchange_sum(exchange_sum(shell_terms, "vol"), CLS)
+    stats = jnp.stack([first * first, second * second, first * second])
+    shell_terms = jnp.dot(stats, shell_hot, precision=lax.Precision.HIGHEST)
+    shell_sums = exchange_sum(exchange_sum(shell_terms, ("half", "vol")), CLS)
     shell_fsc = shell_sums[2] / (jnp.sqrt(shell_sums[0]) * jnp.sqrt(shell_sums[1]) + EPS_F)
     mean_sq = (jnp.sum(shell_sums[0]) + jnp.sum(shell_sums[1]) + 2.0 * jnp.sum(shell_sums[2])) / (
         4.0 * n_vol * VOXS
-    )
-    first = lax.dynamic_index_in_dim(first_block.reshape(n_half, piece_len), half_id, keepdims=False)
-    second = lax.dynamic_index_in_dim(second_block.reshape(n_half, piece_len), half_id, keepdims=False)
-    shell_hot = (shell_index[0][:, None] == jnp.arange(NSHELL, dtype=jnp.int32)[None, :]).astype(
-        jnp.float32
     )
     filter_vox = jnp.dot(shell_hot, shell_fsc, precision=lax.Precision.HIGHEST)
     volume = filter_vox * (0.5 * (first + second)) / jnp.sqrt(mean_sq + EPS_F)

time: 245 us -> 245 us (level)
  blocking collectives: 22.4 us -> 47.2 us
  waiting for transfers between devices: 134 us -> 119 us
  starting transfers between devices: 41 us -> 32.1 us
    all_to_all x1 -> x2, blocking collectives: 14.8 us -> 39.6 us  [the longest x1 21.4 us: reduce_scatter(): got = lax.all_to_all(jnp.swapaxes(part, 0, 1), outer, 0, 0, tiled=True)]
    all_to_all x1 -> x0, waiting for transfers between devices: 14.7 us -> none  [exchange_rows(): got = lax.all_to_all(jnp.moveaxis(data, 1, 0), axis, 0, 0, tiled=True)]
    all_to_all x1 -> x0, starting transfers between devices: 5.03 us -> none  [exchange_rows(): got = lax.all_to_all(jnp.moveaxis(data, 1, 0), axis, 0, 0, tiled=True)]
    ppermute x2 -> x0, starting transfers between devices: 4.02 us -> none  [partner(): lax.ppermute(shard, axis, [(i, i ^ 1 << apart) for i in range(lax.axis_si...]
  transfers between devices with their start and end apart: 6 -> 3, of which waited for: 5 -> 3; matrix products, arithmetic and copies ran while one was open for 3% -> 3% of each run, Pallas kernels for 0% -> 0%
where the time goes in v11:
time: 245 us; the launch traced here: 244 us
  waiting for transfers between devices  119 us (49%)
  blocking collectives  47.2 us (19%)
  starting transfers between devices  32.1 us (13%)
  local copies, waits for them, and re-layouts  15.3 us (6%)
  Pallas kernels  13.6 us (6%)
  other arithmetic  9.18 us (4%)
  matrix products  4.55 us (2%)
  between operations  2.72 us (1%)
    all_to_all x1, waiting for transfers between devices, shards(): lax.all_to_all(outgoing.reshape(n_cls, capacity, quarter_rows, IMG), CLS,...  95.3 us
    all_to_all x2, waiting for transfers between devices, exchange_sum(): lax.all_to_all(jnp.broadcast_to(x[None], (n,) + x.shape), axis, 0, 0, til...  23.9 us
    all_to_all x1, blocking collectives, reduce_scatter(): got = lax.all_to_all(jnp.swapaxes(part, 0, 1), outer, 0, 0, tiled=True)  21.4 us
    all_to_all x1, starting transfers between devices, shards(): lax.all_to_all(outgoing.reshape(n_cls, capacity, quarter_rows, IMG), CLS,...  18.9 us
    all_to_all x1, blocking collectives, reduce_scatter(): lax.all_to_all(data.reshape(n_half * n_inner, n_outer, length), ('half',...  18.2 us
    pallas_call x1, Pallas kernels, project(): pl.pallas_call(_project_kernel, out_shape=jax.ShapeDtypeStruct((q_count,...  13.6 us
    all_to_all x2, starting transfers between devices, exchange_sum(): lax.all_to_all(jnp.broadcast_to(x[None], (n,) + x.shape), axis, 0, 0, til...  13.2 us
    all_to_all x1, blocking collectives, exchange_sum(): lax.all_to_all(jnp.broadcast_to(x[None], (n,) + x.shape), axis, 0, 0, til...  7.65 us
  transfers between devices with their start and end apart: 3, of which 3 were waited for; matrix products, arithmetic and copies ran while one was open for 3% of the time, Pallas kernels for 0%

profile of v11, /device:TPU:6, one launch (start us, length us, event | category | flops | bytes accessed | tf_op | source)
XLA Modules:
  0.0 243.9 jit_solution(12450616983505084099)
XLA Ops:
  0.6 0.0 copy-start
  0.6 0.8 fusion.16
  1.5 0.2 reduce_window_sum.11
  1.6 0.8 select_reduce_fusion
  2.5 0.7 add_add_fusion
  3.1 0.0 copy-done
  3.1 0.7 convolution_convert_fusion
  3.9 2.5 %copy.14 = bf16[64,4,32,128]{3,1,2,0:T(4,128)(2,1)} copy(bf16[64,4,32,128]{3,1,0,2:T(4,128)(2,1)S(1)} %bitcast.348) | data formatting | bytes 4194304 | tf_op jit(solution)/shard_map/reshape | solution.py:180
  6.3 0.0 copy-start.1
  6.3 18.9 %all-to-all-start = ((bf16[64,4,32,128]{3,1,2,0:T(4,128)(2,1)}), bf16[64,4,32,128]{3,1,2,0:T(4,128)(2,1)}, u32[]{:S(2)}, u32[]{:S(2)}) async-start(bf16[64,4,32,128]{3,1,2,0:T(4,128)(2,1)} %copy.14), calls=%async_computation | async-start | bytes 4194304 | tf_op jit(solution)/shard_map/all_to_all | solution.py:179
  25.2 0.0 copy-done.1
  25.3 0.1 fusion.76
  25.4 0.1 fusion.77
  25.6 0.8 maximum_dynamic-update-slice_fusion.3
  26.4 0.1 fusion.78
  26.6 0.1 fusion.79
  26.7 0.8 maximum_dynamic-update-slice_fusion.2
  27.6 0.7 constant_dynamic-update-slice_fusion
  28.3 0.9 maximum_dynamic-update-slice_fusion.1
  29.1 0.9 maximum_dynamic-update-slice_fusion
  30.0 95.3 %all-to-all-done = bf16[64,4,32,128]{3,1,2,0:T(4,128)(2,1)} async-done(((bf16[64,4,32,128]{3,1,2,0:T(4,128)(2,1)}), bf16[64,4,32,128]{3,1,2,0:T(4,128)(2,1)}, u32[]{:S(2)}, u32[]{:S(2)}) %all-to-all-start) | async-done | bytes 2097184 | tf_op jit(solution)/shard_map/all_to_all | solution.py:179
  125.3 2.7 %copy.15 = bf16[64,4,32,128]{3,1,0,2:T(4,128)(2,1)S(1)} copy(bf16[64,4,32,128]{3,1,2,0:T(4,128)(2,1)} %all-to-all-done) | data formatting | bytes 4194304 | tf_op jit(solution)/shard_map/all_to_all | solution.py:179
  128.0 2.1 fusion.2
  130.0 0.9 broadcast_in_dim.10
  131.0 4.5 %all-to-all-start.1 = ((f32[4,256,5,32]{1,3,2,0:T(8,128)}), f32[4,256,5,32]{1,3,2,0:T(8,128)}, u32[]{:S(2)}, u32[]{:S(2)}) async-start(f32[4,256,5,32]{1,3,2,0:T(8,128)} %broadcast_in_dim.10), calls=%async_computation.1 | async-start | bytes 1310720 | tf_op jit(solution)/shard_map/all_to_all | solution.py:58
  135.4 1.9 reshape.94.idx_ref
  137.4 7.9 %all-to-all-done.1 = f32[4,256,5,32]{1,3,2,0:T(8,128)} async-done(((f32[4,256,5,32]{1,3,2,0:T(8,128)}), f32[4,256,5,32]{1,3,2,0:T(8,128)}, u32[]{:S(2)}, u32[]{:S(2)}) %all-to-all-start.1) | async-done | bytes 655392 | tf_op jit(solution)/shard_map/all_to_all | solution.py:58
  145.3 1.2 fusion.73
  146.5 0.5 fusion.80
  147.0 3.0 %copy.17 = f32[160,32,128]{2,1,0:T(8,128)} copy(f32[160,32,128]{2,0,1:T(8,128)S(1)} %fusion.80) | data formatting | bytes 5242880 | tf_op jit(solution)/shard_map/dot_general | solution.py:195
  150.1 13.6 %shard_map.68 = f32[128,16,128]{2,1,0:T(8,128)} custom-call(f32[5,1024,128]{2,1,0:T(8,128)} %bitcast.345, s32[1024,128]{1,0:T(8,128)} %reshape.94.idx_ref), custom_call_target="tpu_custom_call" | custom-call | flops 1073741824 | bytes 4194304 | tf_op jit(solution)/shard_map/pallas_call | solution.py:138
  163.7 1.6 reshape_reshape.3
  165.2 0.6 copy.18
  165.8 18.2 %all_to_all.30 = f32[8,16,2048]{2,1,0:T(8,128)S(1)} all-to-all(f32[8,16,2048]{2,1,0:T(8,128)S(1)} %bitcast.350), channel_id=1, replica_groups=mesh['half'=2,'z'=16,'x'=4,'vol'=4] {'half','x'}, dimensions={0} | all-to-all | bytes 2097152 | tf_op jit(solution)/shard_map/all_to_all | solution.py:92
  184.0 0.1 fusion.75
  184.1 0.0 copy-start.3
  184.1 0.6 fusion.11
  184.7 21.4 %all_to_all.31 = f32[16,2,2048]{2,1,0:T(2,128)S(1)} all-to-all(f32[16,2,2048]{2,1,0:T(2,128)S(1)} %fusion.11), channel_id=1, replica_groups=mesh['half'=2,'z'=16,'x'=4,'vol'=4] {'z'}, dimensions={0} | all-to-all | bytes 524288 | tf_op jit(solution)/shard_map/all_to_all | solution.py:98
  206.2 0.1 slice_add_fusion.3
  206.3 0.0 copy-done.3
  206.3 0.6 fusion.8
  206.9 7.6 %all_to_all.32 = f32[8,3,128]{2,1,0:T(4,128)S(1)} all-to-all(f32[8,3,128]{2,1,0:T(4,128)S(1)} %broadcast_in_dim.11), channel_id=1, replica_groups=mesh['half'=2,'z'=16,'x'=4,'vol'=4] {'half','vol'}, dimensions={0} | all-to-all | bytes 24576 | tf_op jit(solution)/shard_map/all_to_all | solution.py:58
  214.5 0.7 broadcast_in_dim.13
  215.2 8.7 %all-to-all-start.5 = ((f32[64,3,128]{2,1,0:T(4,128)}), f32[64,3,128]{2,1,0:T(4,128)S(1)}, u32[]{:S(2)}, u32[]{:S(2)}) async-start(f32[64,3,128]{2,1,0:T(4,128)} %broadcast_in_dim.13), calls=%async_computation.5 | async-start | bytes 262144 | tf_op jit(solution)/shard_map/all_to_all | solution.py:58
  223.9 16.0 %all-to-all-done.5 = f32[64,3,128]{2,1,0:T(4,128)S(1)} async-done(((f32[64,3,128]{2,1,0:T(4,128)}), f32[64,3,128]{2,1,0:T(4,128)S(1)}, u32[]{:S(2)}, u32[]{:S(2)}) %all-to-all-start.5) | async-done | bytes 98336 | tf_op jit(solution)/shard_map/all_to_all | solution.py:58
  239.9 0.1 fusion.22
  240.0 0.6 slice_reduce_fusion.2
  240.7 0.0 copy-start.2
  242.5 0.7 fusion.7
  243.3 0.6 multiply_divide_fusion
  243.9 0.0 copy-done.2
  (7 shorter events, 0.1 us)
Async XLA Ops:
  0.6 2.5 %copy-start = (bf16[128,4096]{1,0:T(8,128)(2,1)S(1)}, bf16[128,4096]{1,0:T(8,128)(2,1)}, u32[]{:S(2)}) copy-start(bf16[128,4096]{1,0:T(8,128)(2,1)} %param.5) | copy-start | bytes 3145732
  6.3 18.9 %copy-start.1 = (bf16[32,4096]{1,0:T(8,128)(2,1)S(1)}, bf16[32,4096]{1,0:T(8,128)(2,1)}, u32[]{:S(2)}) copy-start(bf16[32,4096]{1,0:T(8,128)(2,1)} %param.7) | copy-start | bytes 786436
  6.3 119.0 %all-to-all-start = ((bf16[64,4,32,128]{3,1,2,0:T(4,128)(2,1)}), bf16[64,4,32,128]{3,1,2,0:T(4,128)(2,1)}, u32[]{:S(2)}, u32[]{:S(2)}) async-start(bf16[64,4,32,128]{3,1,2,0:T(4,128)(2,1)} %copy.14), calls=%async_computation | async-start | bytes 4194304 | tf_op jit(solution)/shard_map/all_to_all | solution.py:179
  131.0 14.3 %all-to-all-start.1 = ((f32[4,256,5,32]{1,3,2,0:T(8,128)}), f32[4,256,5,32]{1,3,2,0:T(8,128)}, u32[]{:S(2)}, u32[]{:S(2)}) async-start(f32[4,256,5,32]{1,3,2,0:T(8,128)} %broadcast_in_dim.10), calls=%async_computation.1 | async-start | bytes 1310720 | tf_op jit(solution)/shard_map/all_to_all | solution.py:58
  184.1 22.1 %copy-start.3 = (s32[1,2048]{1,0:T(1,128)S(1)}, s32[1,2048]{1,0:T(1,128)}, u32[]{:S(2)}) copy-start(s32[1,2048]{1,0:T(1,128)} %param.9) | copy-start | bytes 24580
  215.2 24.8 %all-to-all-start.5 = ((f32[64,3,128]{2,1,0:T(4,128)}), f32[64,3,128]{2,1,0:T(4,128)S(1)}, u32[]{:S(2)}, u32[]{:S(2)}) async-start(f32[64,3,128]{2,1,0:T(4,128)} %broadcast_in_dim.13), calls=%async_computation.5 | async-start | bytes 262144 | tf_op jit(solution)/shard_map/all_to_all | solution.py:58
  240.7 3.2 %copy-start.2 = (f32[1,128]{1,0:T(1,128)}, f32[1,128]{1,0:T(1,128)S(1)}, u32[]{:S(2)}) copy-start(f32[1,128]{1,0:T(1,128)S(1)} %get-tuple-element.22) | copy-start | bytes 1540

commit v12 on v10

--- a/solution.py
+++ b/solution.py
@@ -160,14 +160,15 @@
     quarter_rows = pix_quarter // IMG
     bins = VOXS // IMG
     outgoing = lax.dot_general(
-        slot_hits.astype(jnp.bfloat16),
+        slot_hits.astype(jnp.bfloat16).reshape(n_cls, capacity, part_count),
         images.reshape(part_count, quarter_rows, IMG),
-        (((1,), (0,)), ((), ())),
+        (((2,), (0,)), ((), ())),
         preferred_element_type=jnp.float32,
     ).astype(jnp.bfloat16)
     arrived = lax.all_to_all(
-        outgoing.reshape(n_cls, capacity, quarter_rows, IMG), CLS, split_axis=0, concat_axis=0, tiled=True
-    ).reshape(slot_count, quarter_rows, IMG)
+        jnp.swapaxes(outgoing, 1, 2), CLS, split_axis=0, concat_axis=0, tiled=True
+    )
+    arrived = jnp.swapaxes(arrived, 1, 2).reshape(slot_count, quarter_rows, IMG)
     shaped_refs = references.reshape(class_count, quarter_rows, IMG)
     rolled_refs = jnp.concatenate(
         [jnp.roll(shaped_refs, -(shift_id - SHIFTS // 2), axis=2) for shift_id in range(SHIFTS)],

time: 245 us -> 243 us (level)
  local copies, waits for them, and re-layouts: 16.2 us -> 13.7 us
    convert_element_type x0 -> x1, local copies, waits for them, and re-layouts: none -> 2.68 us  [shards(): outgoing = lax.dot_general(slot_hits.astype(jnp.bfloat16).reshape(n_cls,...]
    all_to_all x1 -> x0, local copies, waits for them, and re-layouts: 2.67 us -> none  [shards(): lax.all_to_all(outgoing.reshape(n_cls, capacity, quarter_rows, IMG), CLS,...]
    reshape x1 -> x0, local copies, waits for them, and re-layouts: 2.47 us -> none  [shards(): outgoing.reshape(n_cls, capacity, quarter_rows, IMG)]
where the time goes in v12:
time: 243 us; the launch traced here: 241 us
  waiting for transfers between devices  134 us (55%)
  starting transfers between devices  40.6 us (17%)
  blocking collectives  22.4 us (9%)
  local copies, waits for them, and re-layouts  13.7 us (6%)
  Pallas kernels  13.6 us (6%)
  other arithmetic  8.69 us (4%)
  matrix products  5.71 us (2%)
  between operations  2.78 us (1%)
    all_to_all x1, waiting for transfers between devices, shards(): lax.all_to_all(jnp.swapaxes(outgoing, 1, 2), CLS, split_axis=0, concat_ax...  95.4 us
    all_to_all x2, waiting for transfers between devices, exchange_sum(): lax.all_to_all(jnp.broadcast_to(x[None], (n,) + x.shape), axis, 0, 0, til...  22.8 us
    all_to_all x1, starting transfers between devices, shards(): lax.all_to_all(jnp.swapaxes(outgoing, 1, 2), CLS, split_axis=0, concat_ax...  18.7 us
    all_to_all x1, blocking collectives, exchange_rows(): got = lax.all_to_all(jnp.moveaxis(data, 1, 0), axis, 0, 0, tiled=True)  14.8 us
    all_to_all x1, waiting for transfers between devices, exchange_rows(): got = lax.all_to_all(jnp.moveaxis(data, 1, 0), axis, 0, 0, tiled=True)  14.6 us
    pallas_call x1, Pallas kernels, project(): pl.pallas_call(_project_kernel, out_shape=jax.ShapeDtypeStruct((q_count,...  13.6 us
    all_to_all x2, starting transfers between devices, exchange_sum(): lax.all_to_all(jnp.broadcast_to(x[None], (n,) + x.shape), axis, 0, 0, til...  13 us
    all_to_all x1, blocking collectives, exchange_sum(): lax.all_to_all(jnp.broadcast_to(x[None], (n,) + x.shape), axis, 0, 0, til...  7.66 us
  transfers between devices with their start and end apart: 6, of which 5 were waited for; matrix products, arithmetic and copies ran while one was open for 3% of the time, Pallas kernels for 0%

profile of v12, /device:TPU:6, one launch (start us, length us, event | category | flops | bytes accessed | tf_op | source)
XLA Modules:
  0.0 241.4 jit_solution(4320991556372409686)
XLA Ops:
  0.6 0.0 copy-start
  0.7 0.8 fusion.27
  1.5 0.2 reduce_window_sum.11
  1.7 0.8 select_reduce_fusion
  2.5 0.7 add_add_fusion
  3.2 0.0 copy-done
  3.2 0.7 convert_bitcast_fusion
  3.9 2.7 %copy.16 = bf16[64,32,4,128]{3,1,2,0:T(8,128)(2,1)} copy(bf16[64,32,4,128]{3,0,1,2:T(8,128)(2,1)S(1)} %convert_bitcast_fusion) | data formatting | bytes 4194304 | tf_op jit(solution)/shard_map/convert_element_type | solution.py:167
  6.6 0.0 copy-start.1
  6.6 18.7 %all-to-all-start = ((bf16[64,32,4,128]{3,1,2,0:T(8,128)(2,1)}), bf16[64,32,4,128]{3,1,2,0:T(8,128)(2,1)S(1)}, u32[]{:S(2)}, u32[]{:S(2)}) async-start(bf16[64,32,4,128]{3,1,2,0:T(8,128)(2,1)} %copy.16), calls=%async_computation | async-start | bytes 4194304 | tf_op jit(solution)/shard_map/all_to_all | solution.py:168
  25.3 0.0 copy-done.1
  25.4 0.1 fusion.83
  25.5 0.1 fusion.84
  25.7 0.9 maximum_dynamic-update-slice_fusion.3
  26.5 0.1 fusion.85
  26.7 0.1 fusion.86
  26.8 0.8 maximum_dynamic-update-slice_fusion.2
  27.7 0.7 constant_dynamic-update-slice_fusion
  28.4 0.9 maximum_dynamic-update-slice_fusion.1
  29.3 0.8 maximum_dynamic-update-slice_fusion
  30.1 95.4 %all-to-all-done = bf16[64,32,4,128]{3,1,2,0:T(8,128)(2,1)S(1)} async-done(((bf16[64,32,4,128]{3,1,2,0:T(8,128)(2,1)}), bf16[64,32,4,128]{3,1,2,0:T(8,128)(2,1)S(1)}, u32[]{:S(2)}, u32[]{:S(2)}) %all-to-all-start) | async-done | bytes 2097184 | tf_op jit(solution)/shard_map/all_to_all | solution.py:168
  125.5 2.3 fusion.7
  127.8 0.9 broadcast_in_dim.10
  128.7 4.5 %all-to-all-start.1 = ((f32[4,256,5,32]{1,3,2,0:T(8,128)}), f32[4,256,5,32]{1,3,2,0:T(8,128)}, u32[]{:S(2)}, u32[]{:S(2)}) async-start(f32[4,256,5,32]{1,3,2,0:T(8,128)} %broadcast_in_dim.10), calls=%async_computation.1 | async-start | bytes 1310720 | tf_op jit(solution)/shard_map/all_to_all | solution.py:58
  133.2 1.9 reshape.240.idx_ref
  135.1 7.9 %all-to-all-done.1 = f32[4,256,5,32]{1,3,2,0:T(8,128)} async-done(((f32[4,256,5,32]{1,3,2,0:T(8,128)}), f32[4,256,5,32]{1,3,2,0:T(8,128)}, u32[]{:S(2)}, u32[]{:S(2)}) %all-to-all-start.1) | async-done | bytes 655392 | tf_op jit(solution)/shard_map/all_to_all | solution.py:58
  143.0 1.2 fusion.81
  144.3 0.9 fusion.3
  145.2 3.0 %copy.20 = f32[160,32,128]{2,1,0:T(8,128)} copy(f32[160,32,128]{2,0,1:T(8,128)S(1)} %fusion.3) | data formatting | bytes 5242880 | tf_op jit(solution)/shard_map/dot_general | solution.py:185
  148.2 13.6 %shard_map.68 = f32[128,16,128]{2,1,0:T(8,128)} custom-call(f32[5,1024,128]{2,1,0:T(8,128)} %bitcast.349, s32[1024,128]{1,0:T(8,128)} %reshape.240.idx_ref), custom_call_target="tpu_custom_call" | custom-call | flops 1073741824 | bytes 4194304 | tf_op jit(solution)/shard_map/pallas_call | solution.py:127
  161.8 1.6 reshape_reshape.3
  163.4 0.6 copy.44
  164.0 14.8 %all_to_all.30 = f32[4,2,16,2048]{3,2,1,0:T(8,128)S(1)} all-to-all(f32[4,2,16,2048]{3,2,1,0:T(8,128)S(1)} %bitcast.352), channel_id=1, replica_groups=mesh['half'=2,'z'=16,'x'=4,'vol'=4] {'x'}, dimensions={0} | all-to-all | bytes 2097152 | tf_op jit(solution)/shard_map/all_to_all | solution.py:79
  178.8 0.0 copy-start.2
  178.8 0.1 fusion.16
  178.8 1.0 copy.22
  179.8 5.0 %all-to-all-start.3 = ((f32[16,2,1,2048]{3,2,1,0:T(1,128)}), f32[16,2,1,2048]{3,2,1,0:T(1,128)S(1)}, u32[]{:S(2)}, u32[]{:S(2)}) async-start(f32[16,2,1,2048]{3,2,1,0:T(1,128)} %copy.22), calls=%async_computation.3 | async-start | bytes 524288 | tf_op jit(solution)/shard_map/all_to_all | solution.py:79
  184.8 0.0 copy-done.2
  184.8 1.9 collective-permute-start.1
  186.8 14.6 %all-to-all-done.3 = f32[16,2,1,2048]{3,2,1,0:T(1,128)S(1)} async-done(((f32[16,2,1,2048]{3,2,1,0:T(1,128)}), f32[16,2,1,2048]{3,2,1,0:T(1,128)S(1)}, u32[]{:S(2)}, u32[]{:S(2)}) %all-to-all-start.3) | async-done | bytes 262176 | tf_op jit(solution)/shard_map/all_to_all | solution.py:79
  201.4 0.1 slice_add_fusion.6
  201.5 1.9 collective-permute-start
  203.4 0.0 collective-permute-done.1
  203.5 1.1 collective-permute-done
  204.6 1.0 fusion.2
  205.6 7.7 %all_to_all.31 = f32[4,3,128]{2,1,0:T(4,128)S(1)} all-to-all(f32[4,3,128]{2,1,0:T(4,128)S(1)} %broadcast_in_dim.11), channel_id=1, replica_groups=mesh['half'=2,'z'=16,'x'=4,'vol'=4] {'vol'}, dimensions={0} | all-to-all | bytes 12288 | tf_op jit(solution)/shard_map/all_to_all | solution.py:58
  213.3 0.7 broadcast_in_dim.13
  213.9 8.6 %all-to-all-start.5 = ((f32[64,3,128]{2,1,0:T(4,128)}), f32[64,3,128]{2,1,0:T(4,128)S(1)}, u32[]{:S(2)}, u32[]{:S(2)}) async-start(f32[64,3,128]{2,1,0:T(4,128)} %broadcast_in_dim.13), calls=%async_computation.5 | async-start | bytes 262144 | tf_op jit(solution)/shard_map/all_to_all | solution.py:58
  222.6 14.9 %all-to-all-done.5 = f32[64,3,128]{2,1,0:T(4,128)S(1)} async-done(((f32[64,3,128]{2,1,0:T(4,128)}), f32[64,3,128]{2,1,0:T(4,128)S(1)}, u32[]{:S(2)}, u32[]{:S(2)}) %all-to-all-start.5) | async-done | bytes 98336 | tf_op jit(solution)/shard_map/all_to_all | solution.py:58
  237.5 0.1 fusion.28
  237.5 0.6 slice_reduce_fusion.2
  238.2 0.0 copy-start.3
  240.1 0.7 fusion.14
  240.8 0.6 multiply_divide_fusion
  241.4 0.0 copy-done.3
  (12 shorter events, 0.2 us)
Async XLA Ops:
  0.6 2.5 %copy-start = (bf16[128,4096]{1,0:T(8,128)(2,1)S(1)}, bf16[128,4096]{1,0:T(8,128)(2,1)}, u32[]{:S(2)}) copy-start(bf16[128,4096]{1,0:T(8,128)(2,1)} %param.5) | copy-start | bytes 3145732
  6.6 18.7 %copy-start.1 = (bf16[32,4096]{1,0:T(8,128)(2,1)S(1)}, bf16[32,4096]{1,0:T(8,128)(2,1)}, u32[]{:S(2)}) copy-start(bf16[32,4096]{1,0:T(8,128)(2,1)} %param.7) | copy-start | bytes 786436
  6.6 118.9 %all-to-all-start = ((bf16[64,32,4,128]{3,1,2,0:T(8,128)(2,1)}), bf16[64,32,4,128]{3,1,2,0:T(8,128)(2,1)S(1)}, u32[]{:S(2)}, u32[]{:S(2)}) async-start(bf16[64,32,4,128]{3,1,2,0:T(8,128)(2,1)} %copy.16), calls=%async_computation | async-start | bytes 4194304 | tf_op jit(solution)/shard_map/all_to_all | solution.py:168
  128.7 14.3 %all-to-all-start.1 = ((f32[4,256,5,32]{1,3,2,0:T(8,128)}), f32[4,256,5,32]{1,3,2,0:T(8,128)}, u32[]{:S(2)}, u32[]{:S(2)}) async-start(f32[4,256,5,32]{1,3,2,0:T(8,128)} %broadcast_in_dim.10), calls=%async_computation.1 | async-start | bytes 1310720 | tf_op jit(solution)/shard_map/all_to_all | solution.py:58
  178.8 6.1 %copy-start.2 = (s32[1,2048]{1,0:T(1,128)S(1)}, s32[1,2048]{1,0:T(1,128)}, u32[]{:S(2)}) copy-start(s32[1,2048]{1,0:T(1,128)} %param.9) | copy-start | bytes 24580
  179.8 21.6 %all-to-all-start.3 = ((f32[16,2,1,2048]{3,2,1,0:T(1,128)}), f32[16,2,1,2048]{3,2,1,0:T(1,128)S(1)}, u32[]{:S(2)}, u32[]{:S(2)}) async-start(f32[16,2,1,2048]{3,2,1,0:T(1,128)} %copy.22), calls=%async_computation.3 | async-start | bytes 524288 | tf_op jit(solution)/shard_map/all_to_all | solution.py:79
  184.8 18.6 %collective-permute-start.1 = (s32[2048]{0:T(1024)S(1)}, s32[2048]{0:T(1024)S(1)}, u32[]{:S(2)}, u32[]{:S(2)}) collective-permute-start(s32[2048]{0:T(1024)S(1)} %bitcast.363), channel_id=1, source_target_pairs={{0,256},{256,0},{1,257},{257,1},{2,258},{258,2},{3,259},{259,3},{4... | collective-permute-start | bytes 24584 | tf_op jit(solution)/shard_map/ppermute | solution.py:27
  201.5 3.1 %collective-permute-start = (f32[4096]{0:T(1024)S(1)}, f32[4096]{0:T(1024)S(1)}, u32[]{:S(2)}, u32[]{:S(2)}) collective-permute-start(f32[4096]{0:T(1024)S(1)} %bitcast.355), channel_id=1, source_target_pairs={{0,256},{256,0},{1,257},{257,1},{2,258},{258,2},{3,259},{259,3},{4... | collective-permute-start | bytes 49160 | tf_op jit(solution)/shard_map/ppermute | solution.py:27
  213.9 23.5 %all-to-all-start.5 = ((f32[64,3,128]{2,1,0:T(4,128)}), f32[64,3,128]{2,1,0:T(4,128)S(1)}, u32[]{:S(2)}, u32[]{:S(2)}) async-start(f32[64,3,128]{2,1,0:T(4,128)} %broadcast_in_dim.13), calls=%async_computation.5 | async-start | bytes 262144 | tf_op jit(solution)/shard_map/all_to_all | solution.py:58
  238.2 3.3 %copy-start.3 = (f32[1,128]{1,0:T(1,128)}, f32[1,128]{1,0:T(1,128)S(1)}, u32[]{:S(2)}) copy-start(f32[1,128]{1,0:T(1,128)S(1)} %get-tuple-element.21) | copy-start | bytes 1540

commit v13 on v12

--- a/solution.py
+++ b/solution.py
@@ -118,7 +118,7 @@
         out_ref[q] = o[:hi_count] + o[hi_count:]
         return carry
 
-    lax.fori_loop(0, IMG, body, 0, unroll=16)
+    lax.fori_loop(0, IMG, body, 0, unroll=32)
 
 
 def project(weighted, idx, bins):

time: 243 us -> 243 us (level)
  no operation moved by 1% of the time
where the time goes in v13:
time: 243 us; the launch traced here: 241 us
  waiting for transfers between devices  134 us (55%)
  starting transfers between devices  40.5 us (17%)
  blocking collectives  22.5 us (9%)
  local copies, waits for them, and re-layouts  13.7 us (6%)
  Pallas kernels  13 us (5%)
  other arithmetic  8.69 us (4%)
  matrix products  5.71 us (2%)
  between operations  2.78 us (1%)
    all_to_all x1, waiting for transfers between devices, shards(): lax.all_to_all(jnp.swapaxes(outgoing, 1, 2), CLS, split_axis=0, concat_ax...  95.4 us
    all_to_all x2, waiting for transfers between devices, exchange_sum(): lax.all_to_all(jnp.broadcast_to(x[None], (n,) + x.shape), axis, 0, 0, til...  22.9 us
    all_to_all x1, starting transfers between devices, shards(): lax.all_to_all(jnp.swapaxes(outgoing, 1, 2), CLS, split_axis=0, concat_ax...  18.7 us
    all_to_all x1, waiting for transfers between devices, exchange_rows(): got = lax.all_to_all(jnp.moveaxis(data, 1, 0), axis, 0, 0, tiled=True)  14.9 us
    all_to_all x1, blocking collectives, exchange_rows(): got = lax.all_to_all(jnp.moveaxis(data, 1, 0), axis, 0, 0, tiled=True)  14.8 us
    pallas_call x1, Pallas kernels, project(): pl.pallas_call(_project_kernel, out_shape=jax.ShapeDtypeStruct((q_count,...  13 us
    all_to_all x2, starting transfers between devices, exchange_sum(): lax.all_to_all(jnp.broadcast_to(x[None], (n,) + x.shape), axis, 0, 0, til...  12.9 us
    all_to_all x1, blocking collectives, exchange_sum(): lax.all_to_all(jnp.broadcast_to(x[None], (n,) + x.shape), axis, 0, 0, til...  7.66 us
  transfers between devices with their start and end apart: 6, of which 5 were waited for; matrix products, arithmetic and copies ran while one was open for 3% of the time, Pallas kernels for 0%

profile of v13, /device:TPU:6, one launch (start us, length us, event | category | flops | bytes accessed | tf_op | source)
XLA Modules:
  0.0 241.1 jit_solution(1108957080211750302)
XLA Ops:
  0.6 0.0 copy-start
  0.7 0.8 fusion.27
  1.5 0.2 reduce_window_sum.11
  1.7 0.8 select_reduce_fusion
  2.5 0.7 add_add_fusion
  3.2 0.0 copy-done
  3.2 0.7 convert_bitcast_fusion
  3.9 2.7 %copy.16 = bf16[64,32,4,128]{3,1,2,0:T(8,128)(2,1)} copy(bf16[64,32,4,128]{3,0,1,2:T(8,128)(2,1)S(1)} %convert_bitcast_fusion) | data formatting | bytes 4194304 | tf_op jit(solution)/shard_map/convert_element_type | solution.py:167
  6.6 0.0 copy-start.1
  6.6 18.7 %all-to-all-start = ((bf16[64,32,4,128]{3,1,2,0:T(8,128)(2,1)}), bf16[64,32,4,128]{3,1,2,0:T(8,128)(2,1)S(1)}, u32[]{:S(2)}, u32[]{:S(2)}) async-start(bf16[64,32,4,128]{3,1,2,0:T(8,128)(2,1)} %copy.16), calls=%async_computation | async-start | bytes 4194304 | tf_op jit(solution)/shard_map/all_to_all | solution.py:168
  25.3 0.0 copy-done.1
  25.4 0.1 fusion.83
  25.5 0.1 fusion.84
  25.7 0.9 maximum_dynamic-update-slice_fusion.3
  26.5 0.1 fusion.85
  26.7 0.1 fusion.86
  26.8 0.8 maximum_dynamic-update-slice_fusion.2
  27.7 0.7 constant_dynamic-update-slice_fusion
  28.4 0.9 maximum_dynamic-update-slice_fusion.1
  29.3 0.8 maximum_dynamic-update-slice_fusion
  30.1 95.4 %all-to-all-done = bf16[64,32,4,128]{3,1,2,0:T(8,128)(2,1)S(1)} async-done(((bf16[64,32,4,128]{3,1,2,0:T(8,128)(2,1)}), bf16[64,32,4,128]{3,1,2,0:T(8,128)(2,1)S(1)}, u32[]{:S(2)}, u32[]{:S(2)}) %all-to-all-start) | async-done | bytes 2097184 | tf_op jit(solution)/shard_map/all_to_all | solution.py:168
  125.5 2.3 fusion.7
  127.8 0.9 broadcast_in_dim.10
  128.7 4.5 %all-to-all-start.1 = ((f32[4,256,5,32]{1,3,2,0:T(8,128)}), f32[4,256,5,32]{1,3,2,0:T(8,128)}, u32[]{:S(2)}, u32[]{:S(2)}) async-start(f32[4,256,5,32]{1,3,2,0:T(8,128)} %broadcast_in_dim.10), calls=%async_computation.1 | async-start | bytes 1310720 | tf_op jit(solution)/shard_map/all_to_all | solution.py:58
  133.2 1.9 reshape.240.idx_ref
  135.1 8.0 %all-to-all-done.1 = f32[4,256,5,32]{1,3,2,0:T(8,128)} async-done(((f32[4,256,5,32]{1,3,2,0:T(8,128)}), f32[4,256,5,32]{1,3,2,0:T(8,128)}, u32[]{:S(2)}, u32[]{:S(2)}) %all-to-all-start.1) | async-done | bytes 655392 | tf_op jit(solution)/shard_map/all_to_all | solution.py:58
  143.1 1.2 fusion.81
  144.4 0.9 fusion.3
  145.3 3.0 %copy.20 = f32[160,32,128]{2,1,0:T(8,128)} copy(f32[160,32,128]{2,0,1:T(8,128)S(1)} %fusion.3) | data formatting | bytes 5242880 | tf_op jit(solution)/shard_map/dot_general | solution.py:185
  148.3 13.0 %shard_map.68 = f32[128,16,128]{2,1,0:T(8,128)} custom-call(f32[5,1024,128]{2,1,0:T(8,128)} %bitcast.349, s32[1024,128]{1,0:T(8,128)} %reshape.240.idx_ref), custom_call_target="tpu_custom_call" | custom-call | flops 1073741824 | bytes 4194304 | tf_op jit(solution)/shard_map/pallas_call | solution.py:127
  161.3 1.6 reshape_reshape.3
  162.9 0.6 copy.44
  163.5 14.8 %all_to_all.30 = f32[4,2,16,2048]{3,2,1,0:T(8,128)S(1)} all-to-all(f32[4,2,16,2048]{3,2,1,0:T(8,128)S(1)} %bitcast.352), channel_id=1, replica_groups=mesh['half'=2,'z'=16,'x'=4,'vol'=4] {'x'}, dimensions={0} | all-to-all | bytes 2097152 | tf_op jit(solution)/shard_map/all_to_all | solution.py:79
  178.3 0.0 copy-start.2
  178.3 0.1 fusion.16
  178.4 1.0 copy.22
  179.3 5.0 %all-to-all-start.3 = ((f32[16,2,1,2048]{3,2,1,0:T(1,128)}), f32[16,2,1,2048]{3,2,1,0:T(1,128)S(1)}, u32[]{:S(2)}, u32[]{:S(2)}) async-start(f32[16,2,1,2048]{3,2,1,0:T(1,128)} %copy.22), calls=%async_computation.3 | async-start | bytes 524288 | tf_op jit(solution)/shard_map/all_to_all | solution.py:79
  184.4 0.0 copy-done.2
  184.4 1.9 collective-permute-start.1
  186.3 14.9 %all-to-all-done.3 = f32[16,2,1,2048]{3,2,1,0:T(1,128)S(1)} async-done(((f32[16,2,1,2048]{3,2,1,0:T(1,128)}), f32[16,2,1,2048]{3,2,1,0:T(1,128)S(1)}, u32[]{:S(2)}, u32[]{:S(2)}) %all-to-all-start.3) | async-done | bytes 262176 | tf_op jit(solution)/shard_map/all_to_all | solution.py:79
  201.2 0.1 slice_add_fusion.6
  201.3 1.9 collective-permute-start
  203.2 0.0 collective-permute-done.1
  203.3 1.1 collective-permute-done
  204.4 1.0 fusion.2
  205.4 7.7 %all_to_all.31 = f32[4,3,128]{2,1,0:T(4,128)S(1)} all-to-all(f32[4,3,128]{2,1,0:T(4,128)S(1)} %broadcast_in_dim.11), channel_id=1, replica_groups=mesh['half'=2,'z'=16,'x'=4,'vol'=4] {'vol'}, dimensions={0} | all-to-all | bytes 12288 | tf_op jit(solution)/shard_map/all_to_all | solution.py:58
  213.1 0.7 broadcast_in_dim.13
  213.7 8.4 %all-to-all-start.5 = ((f32[64,3,128]{2,1,0:T(4,128)}), f32[64,3,128]{2,1,0:T(4,128)S(1)}, u32[]{:S(2)}, u32[]{:S(2)}) async-start(f32[64,3,128]{2,1,0:T(4,128)} %broadcast_in_dim.13), calls=%async_computation.5 | async-start | bytes 262144 | tf_op jit(solution)/shard_map/all_to_all | solution.py:58
  222.2 14.9 %all-to-all-done.5 = f32[64,3,128]{2,1,0:T(4,128)S(1)} async-done(((f32[64,3,128]{2,1,0:T(4,128)}), f32[64,3,128]{2,1,0:T(4,128)S(1)}, u32[]{:S(2)}, u32[]{:S(2)}) %all-to-all-start.5) | async-done | bytes 98336 | tf_op jit(solution)/shard_map/all_to_all | solution.py:58
  237.1 0.1 fusion.28
  237.2 0.6 slice_reduce_fusion.2
  237.8 0.0 copy-start.3
  239.7 0.7 fusion.14
  240.4 0.6 multiply_divide_fusion
  241.1 0.0 copy-done.3
  (12 shorter events, 0.2 us)
Async XLA Ops:
  0.6 2.5 %copy-start = (bf16[128,4096]{1,0:T(8,128)(2,1)S(1)}, bf16[128,4096]{1,0:T(8,128)(2,1)}, u32[]{:S(2)}) copy-start(bf16[128,4096]{1,0:T(8,128)(2,1)} %param.5) | copy-start | bytes 3145732
  6.6 18.7 %copy-start.1 = (bf16[32,4096]{1,0:T(8,128)(2,1)S(1)}, bf16[32,4096]{1,0:T(8,128)(2,1)}, u32[]{:S(2)}) copy-start(bf16[32,4096]{1,0:T(8,128)(2,1)} %param.7) | copy-start | bytes 786436
  6.6 118.9 %all-to-all-start = ((bf16[64,32,4,128]{3,1,2,0:T(8,128)(2,1)}), bf16[64,32,4,128]{3,1,2,0:T(8,128)(2,1)S(1)}, u32[]{:S(2)}, u32[]{:S(2)}) async-start(bf16[64,32,4,128]{3,1,2,0:T(8,128)(2,1)} %copy.16), calls=%async_computation | async-start | bytes 4194304 | tf_op jit(solution)/shard_map/all_to_all | solution.py:168
  128.7 14.4 %all-to-all-start.1 = ((f32[4,256,5,32]{1,3,2,0:T(8,128)}), f32[4,256,5,32]{1,3,2,0:T(8,128)}, u32[]{:S(2)}, u32[]{:S(2)}) async-start(f32[4,256,5,32]{1,3,2,0:T(8,128)} %broadcast_in_dim.10), calls=%async_computation.1 | async-start | bytes 1310720 | tf_op jit(solution)/shard_map/all_to_all | solution.py:58
  178.3 6.1 %copy-start.2 = (s32[1,2048]{1,0:T(1,128)S(1)}, s32[1,2048]{1,0:T(1,128)}, u32[]{:S(2)}) copy-start(s32[1,2048]{1,0:T(1,128)} %param.9) | copy-start | bytes 24580
  179.3 21.9 %all-to-all-start.3 = ((f32[16,2,1,2048]{3,2,1,0:T(1,128)}), f32[16,2,1,2048]{3,2,1,0:T(1,128)S(1)}, u32[]{:S(2)}, u32[]{:S(2)}) async-start(f32[16,2,1,2048]{3,2,1,0:T(1,128)} %copy.22), calls=%async_computation.3 | async-start | bytes 524288 | tf_op jit(solution)/shard_map/all_to_all | solution.py:79
  184.4 18.8 %collective-permute-start.1 = (s32[2048]{0:T(1024)S(1)}, s32[2048]{0:T(1024)S(1)}, u32[]{:S(2)}, u32[]{:S(2)}) collective-permute-start(s32[2048]{0:T(1024)S(1)} %bitcast.363), channel_id=1, source_target_pairs={{0,256},{256,0},{1,257},{257,1},{2,258},{258,2},{3,259},{259,3},{4... | collective-permute-start | bytes 24584 | tf_op jit(solution)/shard_map/ppermute | solution.py:27
  201.3 3.1 %collective-permute-start = (f32[4096]{0:T(1024)S(1)}, f32[4096]{0:T(1024)S(1)}, u32[]{:S(2)}, u32[]{:S(2)}) collective-permute-start(f32[4096]{0:T(1024)S(1)} %bitcast.355), channel_id=1, source_target_pairs={{0,256},{256,0},{1,257},{257,1},{2,258},{258,2},{3,259},{259,3},{4... | collective-permute-start | bytes 49160 | tf_op jit(solution)/shard_map/ppermute | solution.py:27
  213.7 23.4 %all-to-all-start.5 = ((f32[64,3,128]{2,1,0:T(4,128)}), f32[64,3,128]{2,1,0:T(4,128)S(1)}, u32[]{:S(2)}, u32[]{:S(2)}) async-start(f32[64,3,128]{2,1,0:T(4,128)} %broadcast_in_dim.13), calls=%async_computation.5 | async-start | bytes 262144 | tf_op jit(solution)/shard_map/all_to_all | solution.py:58
  237.8 3.3 %copy-start.3 = (f32[1,128]{1,0:T(1,128)}, f32[1,128]{1,0:T(1,128)S(1)}, u32[]{:S(2)}) copy-start(f32[1,128]{1,0:T(1,128)S(1)} %get-tuple-element.21) | copy-start | bytes 1540

commit v14 on v13

--- a/solution.py
+++ b/solution.py
@@ -118,7 +118,7 @@
         out_ref[q] = o[:hi_count] + o[hi_count:]
         return carry
 
-    lax.fori_loop(0, IMG, body, 0, unroll=32)
+    lax.fori_loop(0, IMG, body, 0, unroll=64)
 
 
 def project(weighted, idx, bins):

time: 243 us -> 242 us (level)
  no operation moved by 1% of the time
where the time goes in v14:
time: 242 us; the launch traced here: 241 us
  waiting for transfers between devices  134 us (55%)
  starting transfers between devices  40.5 us (17%)
  blocking collectives  22.5 us (9%)
  local copies, waits for them, and re-layouts  13.7 us (6%)
  Pallas kernels  12.7 us (5%)
  other arithmetic  8.69 us (4%)
  matrix products  5.71 us (2%)
  between operations  2.78 us (1%)
    all_to_all x1, waiting for transfers between devices, shards(): lax.all_to_all(jnp.swapaxes(outgoing, 1, 2), CLS, split_axis=0, concat_ax...  95.4 us
    all_to_all x2, waiting for transfers between devices, exchange_sum(): lax.all_to_all(jnp.broadcast_to(x[None], (n,) + x.shape), axis, 0, 0, til...  22.9 us
    all_to_all x1, starting transfers between devices, shards(): lax.all_to_all(jnp.swapaxes(outgoing, 1, 2), CLS, split_axis=0, concat_ax...  18.7 us
    all_to_all x1, waiting for transfers between devices, exchange_rows(): got = lax.all_to_all(jnp.moveaxis(data, 1, 0), axis, 0, 0, tiled=True)  14.9 us
    all_to_all x1, blocking collectives, exchange_rows(): got = lax.all_to_all(jnp.moveaxis(data, 1, 0), axis, 0, 0, tiled=True)  14.8 us
    all_to_all x2, starting transfers between devices, exchange_sum(): lax.all_to_all(jnp.broadcast_to(x[None], (n,) + x.shape), axis, 0, 0, til...  12.9 us
    pallas_call x1, Pallas kernels, project(): pl.pallas_call(_project_kernel, out_shape=jax.ShapeDtypeStruct((q_count,...  12.7 us
    all_to_all x1, blocking collectives, exchange_sum(): lax.all_to_all(jnp.broadcast_to(x[None], (n,) + x.shape), axis, 0, 0, til...  7.66 us
  transfers between devices with their start and end apart: 6, of which 5 were waited for; matrix products, arithmetic and copies ran while one was open for 3% of the time, Pallas kernels for 0%

profile of v14, /device:TPU:6, one launch (start us, length us, event | category | flops | bytes accessed | tf_op | source)
XLA Modules:
  0.0 240.8 jit_solution(6661815700173056534)
XLA Ops:
  0.6 0.0 copy-start
  0.7 0.8 fusion.27
  1.5 0.2 reduce_window_sum.11
  1.7 0.8 select_reduce_fusion
  2.5 0.7 add_add_fusion
  3.2 0.0 copy-done
  3.2 0.7 convert_bitcast_fusion
  3.9 2.7 %copy.16 = bf16[64,32,4,128]{3,1,2,0:T(8,128)(2,1)} copy(bf16[64,32,4,128]{3,0,1,2:T(8,128)(2,1)S(1)} %convert_bitcast_fusion) | data formatting | bytes 4194304 | tf_op jit(solution)/shard_map/convert_element_type | solution.py:167
  6.6 0.0 copy-start.1
  6.6 18.7 %all-to-all-start = ((bf16[64,32,4,128]{3,1,2,0:T(8,128)(2,1)}), bf16[64,32,4,128]{3,1,2,0:T(8,128)(2,1)S(1)}, u32[]{:S(2)}, u32[]{:S(2)}) async-start(bf16[64,32,4,128]{3,1,2,0:T(8,128)(2,1)} %copy.16), calls=%async_computation | async-start | bytes 4194304 | tf_op jit(solution)/shard_map/all_to_all | solution.py:168
  25.3 0.0 copy-done.1
  25.4 0.1 fusion.83
  25.5 0.1 fusion.84
  25.7 0.9 maximum_dynamic-update-slice_fusion.3
  26.5 0.1 fusion.85
  26.7 0.1 fusion.86
  26.8 0.8 maximum_dynamic-update-slice_fusion.2
  27.7 0.7 constant_dynamic-update-slice_fusion
  28.4 0.9 maximum_dynamic-update-slice_fusion.1
  29.3 0.8 maximum_dynamic-update-slice_fusion
  30.1 95.4 %all-to-all-done = bf16[64,32,4,128]{3,1,2,0:T(8,128)(2,1)S(1)} async-done(((bf16[64,32,4,128]{3,1,2,0:T(8,128)(2,1)}), bf16[64,32,4,128]{3,1,2,0:T(8,128)(2,1)S(1)}, u32[]{:S(2)}, u32[]{:S(2)}) %all-to-all-start) | async-done | bytes 2097184 | tf_op jit(solution)/shard_map/all_to_all | solution.py:168
  125.5 2.3 fusion.7
  127.8 0.9 broadcast_in_dim.10
  128.7 4.5 %all-to-all-start.1 = ((f32[4,256,5,32]{1,3,2,0:T(8,128)}), f32[4,256,5,32]{1,3,2,0:T(8,128)}, u32[]{:S(2)}, u32[]{:S(2)}) async-start(f32[4,256,5,32]{1,3,2,0:T(8,128)} %broadcast_in_dim.10), calls=%async_computation.1 | async-start | bytes 1310720 | tf_op jit(solution)/shard_map/all_to_all | solution.py:58
  133.2 1.9 reshape.240.idx_ref
  135.1 8.0 %all-to-all-done.1 = f32[4,256,5,32]{1,3,2,0:T(8,128)} async-done(((f32[4,256,5,32]{1,3,2,0:T(8,128)}), f32[4,256,5,32]{1,3,2,0:T(8,128)}, u32[]{:S(2)}, u32[]{:S(2)}) %all-to-all-start.1) | async-done | bytes 655392 | tf_op jit(solution)/shard_map/all_to_all | solution.py:58
  143.1 1.2 fusion.81
  144.4 0.9 fusion.3
  145.3 3.0 %copy.20 = f32[160,32,128]{2,1,0:T(8,128)} copy(f32[160,32,128]{2,0,1:T(8,128)S(1)} %fusion.3) | data formatting | bytes 5242880 | tf_op jit(solution)/shard_map/dot_general | solution.py:185
  148.3 12.7 %shard_map.68 = f32[128,16,128]{2,1,0:T(8,128)} custom-call(f32[5,1024,128]{2,1,0:T(8,128)} %bitcast.349, s32[1024,128]{1,0:T(8,128)} %reshape.240.idx_ref), custom_call_target="tpu_custom_call" | custom-call | flops 1073741824 | bytes 4194304 | tf_op jit(solution)/shard_map/pallas_call | solution.py:127
  161.0 1.6 reshape_reshape.3
  162.6 0.6 copy.44
  163.2 14.8 %all_to_all.30 = f32[4,2,16,2048]{3,2,1,0:T(8,128)S(1)} all-to-all(f32[4,2,16,2048]{3,2,1,0:T(8,128)S(1)} %bitcast.352), channel_id=1, replica_groups=mesh['half'=2,'z'=16,'x'=4,'vol'=4] {'x'}, dimensions={0} | all-to-all | bytes 2097152 | tf_op jit(solution)/shard_map/all_to_all | solution.py:79
  178.0 0.0 copy-start.2
  178.0 0.1 fusion.16
  178.1 1.0 copy.22
  179.0 5.0 %all-to-all-start.3 = ((f32[16,2,1,2048]{3,2,1,0:T(1,128)}), f32[16,2,1,2048]{3,2,1,0:T(1,128)S(1)}, u32[]{:S(2)}, u32[]{:S(2)}) async-start(f32[16,2,1,2048]{3,2,1,0:T(1,128)} %copy.22), calls=%async_computation.3 | async-start | bytes 524288 | tf_op jit(solution)/shard_map/all_to_all | solution.py:79
  184.1 0.0 copy-done.2
  184.1 1.9 collective-permute-start.1
  186.0 14.9 %all-to-all-done.3 = f32[16,2,1,2048]{3,2,1,0:T(1,128)S(1)} async-done(((f32[16,2,1,2048]{3,2,1,0:T(1,128)}), f32[16,2,1,2048]{3,2,1,0:T(1,128)S(1)}, u32[]{:S(2)}, u32[]{:S(2)}) %all-to-all-start.3) | async-done | bytes 262176 | tf_op jit(solution)/shard_map/all_to_all | solution.py:79
  200.9 0.1 slice_add_fusion.6
  201.0 1.9 collective-permute-start
  202.9 0.0 collective-permute-done.1
  203.0 1.1 collective-permute-done
  204.1 1.0 fusion.2
  205.1 7.7 %all_to_all.31 = f32[4,3,128]{2,1,0:T(4,128)S(1)} all-to-all(f32[4,3,128]{2,1,0:T(4,128)S(1)} %broadcast_in_dim.11), channel_id=1, replica_groups=mesh['half'=2,'z'=16,'x'=4,'vol'=4] {'vol'}, dimensions={0} | all-to-all | bytes 12288 | tf_op jit(solution)/shard_map/all_to_all | solution.py:58
  212.8 0.7 broadcast_in_dim.13
  213.4 8.4 %all-to-all-start.5 = ((f32[64,3,128]{2,1,0:T(4,128)}), f32[64,3,128]{2,1,0:T(4,128)S(1)}, u32[]{:S(2)}, u32[]{:S(2)}) async-start(f32[64,3,128]{2,1,0:T(4,128)} %broadcast_in_dim.13), calls=%async_computation.5 | async-start | bytes 262144 | tf_op jit(solution)/shard_map/all_to_all | solution.py:58
  221.9 14.9 %all-to-all-done.5 = f32[64,3,128]{2,1,0:T(4,128)S(1)} async-done(((f32[64,3,128]{2,1,0:T(4,128)}), f32[64,3,128]{2,1,0:T(4,128)S(1)}, u32[]{:S(2)}, u32[]{:S(2)}) %all-to-all-start.5) | async-done | bytes 98336 | tf_op jit(solution)/shard_map/all_to_all | solution.py:58
  236.8 0.1 fusion.28
  236.9 0.6 slice_reduce_fusion.2
  237.5 0.0 copy-start.3
  239.4 0.7 fusion.14
  240.1 0.6 multiply_divide_fusion
  240.8 0.0 copy-done.3
  (12 shorter events, 0.2 us)
Async XLA Ops:
  0.6 2.5 %copy-start = (bf16[128,4096]{1,0:T(8,128)(2,1)S(1)}, bf16[128,4096]{1,0:T(8,128)(2,1)}, u32[]{:S(2)}) copy-start(bf16[128,4096]{1,0:T(8,128)(2,1)} %param.5) | copy-start | bytes 3145732
  6.6 18.7 %copy-start.1 = (bf16[32,4096]{1,0:T(8,128)(2,1)S(1)}, bf16[32,4096]{1,0:T(8,128)(2,1)}, u32[]{:S(2)}) copy-start(bf16[32,4096]{1,0:T(8,128)(2,1)} %param.7) | copy-start | bytes 786436
  6.6 118.9 %all-to-all-start = ((bf16[64,32,4,128]{3,1,2,0:T(8,128)(2,1)}), bf16[64,32,4,128]{3,1,2,0:T(8,128)(2,1)S(1)}, u32[]{:S(2)}, u32[]{:S(2)}) async-start(bf16[64,32,4,128]{3,1,2,0:T(8,128)(2,1)} %copy.16), calls=%async_computation | async-start | bytes 4194304 | tf_op jit(solution)/shard_map/all_to_all | solution.py:168
  128.7 14.4 %all-to-all-start.1 = ((f32[4,256,5,32]{1,3,2,0:T(8,128)}), f32[4,256,5,32]{1,3,2,0:T(8,128)}, u32[]{:S(2)}, u32[]{:S(2)}) async-start(f32[4,256,5,32]{1,3,2,0:T(8,128)} %broadcast_in_dim.10), calls=%async_computation.1 | async-start | bytes 1310720 | tf_op jit(solution)/shard_map/all_to_all | solution.py:58
  178.0 6.1 %copy-start.2 = (s32[1,2048]{1,0:T(1,128)S(1)}, s32[1,2048]{1,0:T(1,128)}, u32[]{:S(2)}) copy-start(s32[1,2048]{1,0:T(1,128)} %param.9) | copy-start | bytes 24580
  179.0 21.9 %all-to-all-start.3 = ((f32[16,2,1,2048]{3,2,1,0:T(1,128)}), f32[16,2,1,2048]{3,2,1,0:T(1,128)S(1)}, u32[]{:S(2)}, u32[]{:S(2)}) async-start(f32[16,2,1,2048]{3,2,1,0:T(1,128)} %copy.22), calls=%async_computation.3 | async-start | bytes 524288 | tf_op jit(solution)/shard_map/all_to_all | solution.py:79
  184.1 18.8 %collective-permute-start.1 = (s32[2048]{0:T(1024)S(1)}, s32[2048]{0:T(1024)S(1)}, u32[]{:S(2)}, u32[]{:S(2)}) collective-permute-start(s32[2048]{0:T(1024)S(1)} %bitcast.363), channel_id=1, source_target_pairs={{0,256},{256,0},{1,257},{257,1},{2,258},{258,2},{3,259},{259,3},{4... | collective-permute-start | bytes 24584 | tf_op jit(solution)/shard_map/ppermute | solution.py:27
  201.0 3.1 %collective-permute-start = (f32[4096]{0:T(1024)S(1)}, f32[4096]{0:T(1024)S(1)}, u32[]{:S(2)}, u32[]{:S(2)}) collective-permute-start(f32[4096]{0:T(1024)S(1)} %bitcast.355), channel_id=1, source_target_pairs={{0,256},{256,0},{1,257},{257,1},{2,258},{258,2},{3,259},{259,3},{4... | collective-permute-start | bytes 49160 | tf_op jit(solution)/shard_map/ppermute | solution.py:27
  213.4 23.4 %all-to-all-start.5 = ((f32[64,3,128]{2,1,0:T(4,128)}), f32[64,3,128]{2,1,0:T(4,128)S(1)}, u32[]{:S(2)}, u32[]{:S(2)}) async-start(f32[64,3,128]{2,1,0:T(4,128)} %broadcast_in_dim.13), calls=%async_computation.5 | async-start | bytes 262144 | tf_op jit(solution)/shard_map/all_to_all | solution.py:58
  237.5 3.3 %copy-start.3 = (f32[1,128]{1,0:T(1,128)}, f32[1,128]{1,0:T(1,128)S(1)}, u32[]{:S(2)}) copy-start(f32[1,128]{1,0:T(1,128)S(1)} %get-tuple-element.21) | copy-start | bytes 1540

commit v15 on v14

--- a/solution.py
+++ b/solution.py
@@ -211,7 +211,7 @@
     )
     stats = jnp.stack([first_block * first_block, second_block * second_block, first_block * second_block])
     shell_terms = jnp.dot(stats, block_hot, precision=lax.Precision.HIGHEST)
-    shell_sums = exchange_sum(exchange_sum(shell_terms, "vol"), CLS)
+    shell_sums = exchange_sum(exchange_sum(shell_terms, CLS), "vol")
     shell_fsc = shell_sums[2] / (jnp.sqrt(shell_sums[0]) * jnp.sqrt(shell_sums[1]) + EPS_F)
     mean_sq = (jnp.sum(shell_sums[0]) + jnp.sum(shell_sums[1]) + 2.0 * jnp.sum(shell_sums[2])) / (
         4.0 * n_vol * VOXS

time: 242 us -> 245 us (1.012)
  blocking collectives: 22.5 us -> 14.8 us
  waiting for transfers between devices: 134 us -> 141 us
  starting transfers between devices: 40.5 us -> 43.7 us
    all_to_all x1 -> x0, blocking collectives: 7.66 us -> none  [exchange_sum(): lax.all_to_all(jnp.broadcast_to(x[None], (n,) + x.shape), axis, 0, 0, til...]
    all_to_all x2 -> x3, waiting for transfers between devices: 22.9 us -> 29.3 us  [exchange_sum(): lax.all_to_all(jnp.broadcast_to(x[None], (n,) + x.shape), axis, 0, 0, til...]
    all_to_all x2 -> x3, starting transfers between devices: 12.9 us -> 16.1 us  [exchange_sum(): lax.all_to_all(jnp.broadcast_to(x[None], (n,) + x.shape), axis, 0, 0, til...]
  transfers between devices with their start and end apart: 6 -> 7, of which waited for: 5 -> 6; matrix products, arithmetic and copies ran while one was open for 3% -> 3% of each run, Pallas kernels for 0% -> 0%
where the time goes in v15:
time: 245 us; the launch traced here: 244 us
  waiting for transfers between devices  141 us (58%)
  starting transfers between devices  43.7 us (18%)
  blocking collectives  14.8 us (6%)
  local copies, waits for them, and re-layouts  14.3 us (6%)
  Pallas kernels  12.7 us (5%)
  other arithmetic  8.73 us (4%)
  matrix products  5.71 us (2%)
  between operations  2.81 us (1%)
    all_to_all x1, waiting for transfers between devices, shards(): lax.all_to_all(jnp.swapaxes(outgoing, 1, 2), CLS, split_axis=0, concat_ax...  95.4 us
    all_to_all x3, waiting for transfers between devices, exchange_sum(): lax.all_to_all(jnp.broadcast_to(x[None], (n,) + x.shape), axis, 0, 0, til...  29.3 us
    all_to_all x1, starting transfers between devices, shards(): lax.all_to_all(jnp.swapaxes(outgoing, 1, 2), CLS, split_axis=0, concat_ax...  18.7 us
    all_to_all x3, starting transfers between devices, exchange_sum(): lax.all_to_all(jnp.broadcast_to(x[None], (n,) + x.shape), axis, 0, 0, til...  16.1 us
    all_to_all x1, waiting for transfers between devices, exchange_rows(): got = lax.all_to_all(jnp.moveaxis(data, 1, 0), axis, 0, 0, tiled=True)  14.9 us
    all_to_all x1, blocking collectives, exchange_rows(): got = lax.all_to_all(jnp.moveaxis(data, 1, 0), axis, 0, 0, tiled=True)  14.8 us
    pallas_call x1, Pallas kernels, project(): pl.pallas_call(_project_kernel, out_shape=jax.ShapeDtypeStruct((q_count,...  12.7 us
    all_to_all x1, starting transfers between devices, exchange_rows(): got = lax.all_to_all(jnp.moveaxis(data, 1, 0), axis, 0, 0, tiled=True)  5.02 us
  transfers between devices with their start and end apart: 7, of which 6 were waited for; matrix products, arithmetic and copies ran while one was open for 3% of the time, Pallas kernels for 0%

profile of v15, /device:TPU:6, one launch (start us, length us, event | category | flops | bytes accessed | tf_op | source)
XLA Modules:
  0.0 243.5 jit_solution(1332720486231180576)
XLA Ops:
  0.6 0.0 copy-start
  0.7 0.8 fusion.27
  1.5 0.2 reduce_window_sum.11
  1.7 0.8 select_reduce_fusion
  2.5 0.7 add_add_fusion
  3.2 0.0 copy-done
  3.2 0.7 convert_bitcast_fusion
  3.9 2.7 %copy.16 = bf16[64,32,4,128]{3,1,2,0:T(8,128)(2,1)} copy(bf16[64,32,4,128]{3,0,1,2:T(8,128)(2,1)S(1)} %convert_bitcast_fusion) | data formatting | bytes 4194304 | tf_op jit(solution)/shard_map/convert_element_type | solution.py:167
  6.6 0.0 copy-start.1
  6.6 18.7 %all-to-all-start = ((bf16[64,32,4,128]{3,1,2,0:T(8,128)(2,1)}), bf16[64,32,4,128]{3,1,2,0:T(8,128)(2,1)S(1)}, u32[]{:S(2)}, u32[]{:S(2)}) async-start(bf16[64,32,4,128]{3,1,2,0:T(8,128)(2,1)} %copy.16), calls=%async_computation | async-start | bytes 4194304 | tf_op jit(solution)/shard_map/all_to_all | solution.py:168
  25.3 0.0 copy-done.1
  25.4 0.1 fusion.35
  25.5 0.1 fusion.36
  25.7 0.9 maximum_dynamic-update-slice_fusion.3
  26.5 0.1 fusion.37
  26.7 0.1 fusion.38
  26.8 0.8 maximum_dynamic-update-slice_fusion.2
  27.7 0.7 constant_dynamic-update-slice_fusion
  28.4 0.9 maximum_dynamic-update-slice_fusion.1
  29.3 0.8 maximum_dynamic-update-slice_fusion
  30.1 95.4 %all-to-all-done = bf16[64,32,4,128]{3,1,2,0:T(8,128)(2,1)S(1)} async-done(((bf16[64,32,4,128]{3,1,2,0:T(8,128)(2,1)}), bf16[64,32,4,128]{3,1,2,0:T(8,128)(2,1)S(1)}, u32[]{:S(2)}, u32[]{:S(2)}) %all-to-all-start) | async-done | bytes 2097184 | tf_op jit(solution)/shard_map/all_to_all | solution.py:168
  125.5 2.3 fusion.7
  127.8 0.9 broadcast_in_dim.10
  128.7 4.5 %all-to-all-start.1 = ((f32[4,256,5,32]{1,3,2,0:T(8,128)}), f32[4,256,5,32]{1,3,2,0:T(8,128)}, u32[]{:S(2)}, u32[]{:S(2)}) async-start(f32[4,256,5,32]{1,3,2,0:T(8,128)} %broadcast_in_dim.10), calls=%async_computation.1 | async-start | bytes 1310720 | tf_op jit(solution)/shard_map/all_to_all | solution.py:58
  133.2 1.9 reshape.244.idx_ref
  135.1 8.0 %all-to-all-done.1 = f32[4,256,5,32]{1,3,2,0:T(8,128)} async-done(((f32[4,256,5,32]{1,3,2,0:T(8,128)}), f32[4,256,5,32]{1,3,2,0:T(8,128)}, u32[]{:S(2)}, u32[]{:S(2)}) %all-to-all-start.1) | async-done | bytes 655392 | tf_op jit(solution)/shard_map/all_to_all | solution.py:58
  143.1 1.2 fusion.33
  144.4 0.9 fusion.3
  145.3 3.0 %copy.20 = f32[160,32,128]{2,1,0:T(8,128)} copy(f32[160,32,128]{2,0,1:T(8,128)S(1)} %fusion.3) | data formatting | bytes 5242880 | tf_op jit(solution)/shard_map/dot_general | solution.py:185
  148.3 12.7 %shard_map.68 = f32[128,16,128]{2,1,0:T(8,128)} custom-call(f32[5,1024,128]{2,1,0:T(8,128)} %bitcast.66, s32[1024,128]{1,0:T(8,128)} %reshape.244.idx_ref), custom_call_target="tpu_custom_call" | custom-call | flops 1073741824 | bytes 4194304 | tf_op jit(solution)/shard_map/pallas_call | solution.py:127
  161.0 1.6 reshape_reshape.3
  162.6 0.6 copy.44
  163.2 14.8 %all_to_all.30 = f32[4,2,16,2048]{3,2,1,0:T(8,128)S(1)} all-to-all(f32[4,2,16,2048]{3,2,1,0:T(8,128)S(1)} %bitcast.69), channel_id=1, replica_groups=mesh['half'=2,'z'=16,'x'=4,'vol'=4] {'x'}, dimensions={0} | all-to-all | bytes 2097152 | tf_op jit(solution)/shard_map/all_to_all | solution.py:79
  178.1 0.0 copy-start.2
  178.1 0.1 fusion.16
  178.1 1.0 copy.22
  179.1 5.0 %all-to-all-start.3 = ((f32[16,2,1,2048]{3,2,1,0:T(1,128)}), f32[16,2,1,2048]{3,2,1,0:T(1,128)S(1)}, u32[]{:S(2)}, u32[]{:S(2)}) async-start(f32[16,2,1,2048]{3,2,1,0:T(1,128)} %copy.22), calls=%async_computation.3 | async-start | bytes 524288 | tf_op jit(solution)/shard_map/all_to_all | solution.py:79
  184.1 0.0 copy-done.2
  184.1 1.9 collective-permute-start.1
  186.1 14.9 %all-to-all-done.3 = f32[16,2,1,2048]{3,2,1,0:T(1,128)S(1)} async-done(((f32[16,2,1,2048]{3,2,1,0:T(1,128)}), f32[16,2,1,2048]{3,2,1,0:T(1,128)S(1)}, u32[]{:S(2)}, u32[]{:S(2)}) %all-to-all-start.3) | async-done | bytes 262176 | tf_op jit(solution)/shard_map/all_to_all | solution.py:79
  200.9 0.1 slice_add_fusion.6
  201.1 1.9 collective-permute-start
  203.0 0.0 collective-permute-done.1
  203.0 1.1 collective-permute-done
  204.2 1.0 fusion.2
  205.1 0.7 broadcast_in_dim.11
  205.8 8.4 %all-to-all-start.4 = ((f32[64,3,128]{2,1,0:T(4,128)}), f32[64,3,128]{2,1,0:T(4,128)S(1)}, u32[]{:S(2)}, u32[]{:S(2)}) async-start(f32[64,3,128]{2,1,0:T(4,128)} %broadcast_in_dim.11), calls=%async_computation.4 | async-start | bytes 262144 | tf_op jit(solution)/shard_map/all_to_all | solution.py:58
  214.3 16.0 %all-to-all-done.4 = f32[64,3,128]{2,1,0:T(4,128)S(1)} async-done(((f32[64,3,128]{2,1,0:T(4,128)}), f32[64,3,128]{2,1,0:T(4,128)S(1)}, u32[]{:S(2)}, u32[]{:S(2)}) %all-to-all-start.4) | async-done | bytes 98336 | tf_op jit(solution)/shard_map/all_to_all | solution.py:58
  230.3 0.1 fusion.28
  230.4 0.6 broadcast_in_dim.13
  231.0 3.2 %all-to-all-start.5 = ((f32[4,3,128]{2,1,0:T(4,128)}), f32[4,3,128]{2,1,0:T(4,128)S(1)}, u32[]{:S(2)}, u32[]{:S(2)}) async-start(f32[4,3,128]{2,1,0:T(4,128)} %broadcast_in_dim.13), calls=%async_computation.5 | async-start | bytes 16384 | tf_op jit(solution)/shard_map/all_to_all | solution.py:58
  234.3 5.3 %all-to-all-done.5 = f32[4,3,128]{2,1,0:T(4,128)S(1)} async-done(((f32[4,3,128]{2,1,0:T(4,128)}), f32[4,3,128]{2,1,0:T(4,128)S(1)}, u32[]{:S(2)}, u32[]{:S(2)}) %all-to-all-start.5) | async-done | bytes 6176 | tf_op jit(solution)/shard_map/all_to_all | solution.py:58
  239.5 0.7 slice_reduce_fusion.2
  240.2 0.0 copy-start.3
  242.2 0.7 fusion.14
  242.9 0.6 multiply_divide_fusion
  243.5 0.0 copy-done.3
  (11 shorter events, 0.2 us)
Async XLA Ops:
  0.6 2.5 %copy-start = (bf16[128,4096]{1,0:T(8,128)(2,1)S(1)}, bf16[128,4096]{1,0:T(8,128)(2,1)}, u32[]{:S(2)}) copy-start(bf16[128,4096]{1,0:T(8,128)(2,1)} %param.5) | copy-start | bytes 3145732
  6.6 18.7 %copy-start.1 = (bf16[32,4096]{1,0:T(8,128)(2,1)S(1)}, bf16[32,4096]{1,0:T(8,128)(2,1)}, u32[]{:S(2)}) copy-start(bf16[32,4096]{1,0:T(8,128)(2,1)} %param.7) | copy-start | bytes 786436
  6.6 118.9 %all-to-all-start = ((bf16[64,32,4,128]{3,1,2,0:T(8,128)(2,1)}), bf16[64,32,4,128]{3,1,2,0:T(8,128)(2,1)S(1)}, u32[]{:S(2)}, u32[]{:S(2)}) async-start(bf16[64,32,4,128]{3,1,2,0:T(8,128)(2,1)} %copy.16), calls=%async_computation | async-start | bytes 4194304 | tf_op jit(solution)/shard_map/all_to_all | solution.py:168
  128.7 14.4 %all-to-all-start.1 = ((f32[4,256,5,32]{1,3,2,0:T(8,128)}), f32[4,256,5,32]{1,3,2,0:T(8,128)}, u32[]{:S(2)}, u32[]{:S(2)}) async-start(f32[4,256,5,32]{1,3,2,0:T(8,128)} %broadcast_in_dim.10), calls=%async_computation.1 | async-start | bytes 1310720 | tf_op jit(solution)/shard_map/all_to_all | solution.py:58
  178.1 6.1 %copy-start.2 = (s32[1,2048]{1,0:T(1,128)S(1)}, s32[1,2048]{1,0:T(1,128)}, u32[]{:S(2)}) copy-start(s32[1,2048]{1,0:T(1,128)} %param.9) | copy-start | bytes 24580
  179.1 21.9 %all-to-all-start.3 = ((f32[16,2,1,2048]{3,2,1,0:T(1,128)}), f32[16,2,1,2048]{3,2,1,0:T(1,128)S(1)}, u32[]{:S(2)}, u32[]{:S(2)}) async-start(f32[16,2,1,2048]{3,2,1,0:T(1,128)} %copy.22), calls=%async_computation.3 | async-start | bytes 524288 | tf_op jit(solution)/shard_map/all_to_all | solution.py:79
  184.1 18.8 %collective-permute-start.1 = (s32[2048]{0:T(1024)S(1)}, s32[2048]{0:T(1024)S(1)}, u32[]{:S(2)}, u32[]{:S(2)}) collective-permute-start(s32[2048]{0:T(1024)S(1)} %bitcast.80), channel_id=1, source_target_pairs={{0,256},{256,0},{1,257},{257,1},{2,258},{258,2},{3,259},{259,3},{4... | collective-permute-start | bytes 24584 | tf_op jit(solution)/shard_map/ppermute | solution.py:27
  201.1 3.1 %collective-permute-start = (f32[4096]{0:T(1024)S(1)}, f32[4096]{0:T(1024)S(1)}, u32[]{:S(2)}, u32[]{:S(2)}) collective-permute-start(f32[4096]{0:T(1024)S(1)} %bitcast.72), channel_id=1, source_target_pairs={{0,256},{256,0},{1,257},{257,1},{2,258},{258,2},{3,259},{259,3},{4... | collective-permute-start | bytes 49160 | tf_op jit(solution)/shard_map/ppermute | solution.py:27
  205.8 24.5 %all-to-all-start.4 = ((f32[64,3,128]{2,1,0:T(4,128)}), f32[64,3,128]{2,1,0:T(4,128)S(1)}, u32[]{:S(2)}, u32[]{:S(2)}) async-start(f32[64,3,128]{2,1,0:T(4,128)} %broadcast_in_dim.11), calls=%async_computation.4 | async-start | bytes 262144 | tf_op jit(solution)/shard_map/all_to_all | solution.py:58
  231.0 8.5 %all-to-all-start.5 = ((f32[4,3,128]{2,1,0:T(4,128)}), f32[4,3,128]{2,1,0:T(4,128)S(1)}, u32[]{:S(2)}, u32[]{:S(2)}) async-start(f32[4,3,128]{2,1,0:T(4,128)} %broadcast_in_dim.13), calls=%async_computation.5 | async-start | bytes 16384 | tf_op jit(solution)/shard_map/all_to_all | solution.py:58
  240.2 3.3 %copy-start.3 = (f32[1,1,128]{2,1,0:T(1,128)}, f32[1,1,128]{2,1,0:T(1,128)S(1)}, u32[]{:S(2)}) copy-start(f32[1,1,128]{2,1,0:T(1,128)S(1)} %get-tuple-element.21) | copy-start | bytes 1540

commit v16 on v14

--- a/solution.py
+++ b/solution.py
@@ -118,7 +118,7 @@
         out_ref[q] = o[:hi_count] + o[hi_count:]
         return carry
 
-    lax.fori_loop(0, IMG, body, 0, unroll=64)
+    lax.fori_loop(0, IMG, body, 0, unroll=IMG)
 
 
 def project(weighted, idx, bins):

time: 242 us -> 244 us (level)
  no operation moved by 1% of the time
where the time goes in v16:
time: 244 us; the launch traced here: 243 us
  waiting for transfers between devices  134 us (55%)
  starting transfers between devices  40.6 us (17%)
  blocking collectives  22.4 us (9%)
  Pallas kernels  14.6 us (6%)
  local copies, waits for them, and re-layouts  13.9 us (6%)
  other arithmetic  8.69 us (4%)
  matrix products  5.71 us (2%)
  between operations  2.78 us (1%)
    all_to_all x1, waiting for transfers between devices, shards(): lax.all_to_all(jnp.swapaxes(outgoing, 1, 2), CLS, split_axis=0, concat_ax...  95.4 us
    all_to_all x2, waiting for transfers between devices, exchange_sum(): lax.all_to_all(jnp.broadcast_to(x[None], (n,) + x.shape), axis, 0, 0, til...  22.8 us
    all_to_all x1, starting transfers between devices, shards(): lax.all_to_all(jnp.swapaxes(outgoing, 1, 2), CLS, split_axis=0, concat_ax...  18.7 us
    all_to_all x1, blocking collectives, exchange_rows(): got = lax.all_to_all(jnp.moveaxis(data, 1, 0), axis, 0, 0, tiled=True)  14.8 us
    all_to_all x1, waiting for transfers between devices, exchange_rows(): got = lax.all_to_all(jnp.moveaxis(data, 1, 0), axis, 0, 0, tiled=True)  14.6 us
    pallas_call x1, Pallas kernels, project(): pl.pallas_call(_project_kernel, out_shape=jax.ShapeDtypeStruct((q_count,...  14.6 us
    all_to_all x2, starting transfers between devices, exchange_sum(): lax.all_to_all(jnp.broadcast_to(x[None], (n,) + x.shape), axis, 0, 0, til...  13 us
    all_to_all x1, blocking collectives, exchange_sum(): lax.all_to_all(jnp.broadcast_to(x[None], (n,) + x.shape), axis, 0, 0, til...  7.66 us
  transfers between devices with their start and end apart: 6, of which 5 were waited for; matrix products, arithmetic and copies ran while one was open for 3% of the time, Pallas kernels for 0%

profile of v16, /device:TPU:6, one launch (start us, length us, event | category | flops | bytes accessed | tf_op | source)
XLA Modules:
  0.0 242.6 jit_solution(12094070217124379745)
XLA Ops:
  0.6 0.0 copy-start
  0.7 0.8 fusion.27
  1.5 0.2 reduce_window_sum.11
  1.7 0.8 select_reduce_fusion
  2.5 0.7 add_add_fusion
  3.2 0.0 copy-done
  3.2 0.7 convert_bitcast_fusion
  3.9 2.7 %copy.16 = bf16[64,32,4,128]{3,1,2,0:T(8,128)(2,1)} copy(bf16[64,32,4,128]{3,0,1,2:T(8,128)(2,1)S(1)} %convert_bitcast_fusion) | data formatting | bytes 4194304 | tf_op jit(solution)/shard_map/convert_element_type | solution.py:167
  6.6 0.0 copy-start.1
  6.6 18.7 %all-to-all-start = ((bf16[64,32,4,128]{3,1,2,0:T(8,128)(2,1)}), bf16[64,32,4,128]{3,1,2,0:T(8,128)(2,1)S(1)}, u32[]{:S(2)}, u32[]{:S(2)}) async-start(bf16[64,32,4,128]{3,1,2,0:T(8,128)(2,1)} %copy.16), calls=%async_computation | async-start | bytes 4194304 | tf_op jit(solution)/shard_map/all_to_all | solution.py:168
  25.3 0.0 copy-done.1
  25.4 0.1 fusion.83
  25.5 0.1 fusion.84
  25.7 0.9 maximum_dynamic-update-slice_fusion.3
  26.5 0.1 fusion.85
  26.7 0.1 fusion.86
  26.8 0.8 maximum_dynamic-update-slice_fusion.2
  27.7 0.7 constant_dynamic-update-slice_fusion
  28.4 0.9 maximum_dynamic-update-slice_fusion.1
  29.3 0.8 maximum_dynamic-update-slice_fusion
  30.1 95.4 %all-to-all-done = bf16[64,32,4,128]{3,1,2,0:T(8,128)(2,1)S(1)} async-done(((bf16[64,32,4,128]{3,1,2,0:T(8,128)(2,1)}), bf16[64,32,4,128]{3,1,2,0:T(8,128)(2,1)S(1)}, u32[]{:S(2)}, u32[]{:S(2)}) %all-to-all-start) | async-done | bytes 2097184 | tf_op jit(solution)/shard_map/all_to_all | solution.py:168
  125.5 2.3 fusion.7
  127.8 0.9 broadcast_in_dim.10
  128.7 4.5 %all-to-all-start.1 = ((f32[4,256,5,32]{1,3,2,0:T(8,128)}), f32[4,256,5,32]{1,3,2,0:T(8,128)}, u32[]{:S(2)}, u32[]{:S(2)}) async-start(f32[4,256,5,32]{1,3,2,0:T(8,128)} %broadcast_in_dim.10), calls=%async_computation.1 | async-start | bytes 1310720 | tf_op jit(solution)/shard_map/all_to_all | solution.py:58
  133.2 1.9 reshape.240.idx_ref
  135.1 7.9 %all-to-all-done.1 = f32[4,256,5,32]{1,3,2,0:T(8,128)} async-done(((f32[4,256,5,32]{1,3,2,0:T(8,128)}), f32[4,256,5,32]{1,3,2,0:T(8,128)}, u32[]{:S(2)}, u32[]{:S(2)}) %all-to-all-start.1) | async-done | bytes 655392 | tf_op jit(solution)/shard_map/all_to_all | solution.py:58
  143.0 1.2 fusion.81
  144.3 0.9 fusion.3
  145.2 3.0 %copy.20 = f32[160,32,128]{2,1,0:T(8,128)} copy(f32[160,32,128]{2,0,1:T(8,128)S(1)} %fusion.3) | data formatting | bytes 5242880 | tf_op jit(solution)/shard_map/dot_general | solution.py:185
  148.2 14.6 %shard_map.68 = f32[128,16,128]{2,1,0:T(8,128)} custom-call(f32[5,1024,128]{2,1,0:T(8,128)} %bitcast.349, s32[1024,128]{1,0:T(8,128)} %reshape.240.idx_ref), custom_call_target="tpu_custom_call" | custom-call | flops 1073741824 | bytes 4194304 | tf_op jit(solution)/shard_map/pallas_call | solution.py:127
  162.8 1.6 reshape_reshape.3
  164.4 0.8 copy.44
  165.2 14.8 %all_to_all.30 = f32[4,2,16,2048]{3,2,1,0:T(8,128)S(1)} all-to-all(f32[4,2,16,2048]{3,2,1,0:T(8,128)S(1)} %bitcast.352), channel_id=1, replica_groups=mesh['half'=2,'z'=16,'x'=4,'vol'=4] {'x'}, dimensions={0} | all-to-all | bytes 2097152 | tf_op jit(solution)/shard_map/all_to_all | solution.py:79
  180.0 0.0 copy-start.2
  180.0 0.1 fusion.16
  180.0 1.0 copy.22
  181.0 5.0 %all-to-all-start.3 = ((f32[16,2,1,2048]{3,2,1,0:T(1,128)}), f32[16,2,1,2048]{3,2,1,0:T(1,128)S(1)}, u32[]{:S(2)}, u32[]{:S(2)}) async-start(f32[16,2,1,2048]{3,2,1,0:T(1,128)} %copy.22), calls=%async_computation.3 | async-start | bytes 524288 | tf_op jit(solution)/shard_map/all_to_all | solution.py:79
  186.0 0.0 copy-done.2
  186.0 1.9 collective-permute-start.1
  188.0 14.6 %all-to-all-done.3 = f32[16,2,1,2048]{3,2,1,0:T(1,128)S(1)} async-done(((f32[16,2,1,2048]{3,2,1,0:T(1,128)}), f32[16,2,1,2048]{3,2,1,0:T(1,128)S(1)}, u32[]{:S(2)}, u32[]{:S(2)}) %all-to-all-start.3) | async-done | bytes 262176 | tf_op jit(solution)/shard_map/all_to_all | solution.py:79
  202.6 0.1 slice_add_fusion.6
  202.7 1.9 collective-permute-start
  204.6 0.0 collective-permute-done.1
  204.7 1.1 collective-permute-done
  205.8 1.0 fusion.2
  206.8 7.7 %all_to_all.31 = f32[4,3,128]{2,1,0:T(4,128)S(1)} all-to-all(f32[4,3,128]{2,1,0:T(4,128)S(1)} %broadcast_in_dim.11), channel_id=1, replica_groups=mesh['half'=2,'z'=16,'x'=4,'vol'=4] {'vol'}, dimensions={0} | all-to-all | bytes 12288 | tf_op jit(solution)/shard_map/all_to_all | solution.py:58
  214.5 0.7 broadcast_in_dim.13
  215.1 8.6 %all-to-all-start.5 = ((f32[64,3,128]{2,1,0:T(4,128)}), f32[64,3,128]{2,1,0:T(4,128)S(1)}, u32[]{:S(2)}, u32[]{:S(2)}) async-start(f32[64,3,128]{2,1,0:T(4,128)} %broadcast_in_dim.13), calls=%async_computation.5 | async-start | bytes 262144 | tf_op jit(solution)/shard_map/all_to_all | solution.py:58
  223.8 14.9 %all-to-all-done.5 = f32[64,3,128]{2,1,0:T(4,128)S(1)} async-done(((f32[64,3,128]{2,1,0:T(4,128)}), f32[64,3,128]{2,1,0:T(4,128)S(1)}, u32[]{:S(2)}, u32[]{:S(2)}) %all-to-all-start.5) | async-done | bytes 98336 | tf_op jit(solution)/shard_map/all_to_all | solution.py:58
  238.7 0.1 fusion.28
  238.7 0.6 slice_reduce_fusion.2
  239.4 0.0 copy-start.3
  241.3 0.7 fusion.14
  242.0 0.6 multiply_divide_fusion
  242.6 0.0 copy-done.3
  (12 shorter events, 0.2 us)
Async XLA Ops:
  0.6 2.5 %copy-start = (bf16[128,4096]{1,0:T(8,128)(2,1)S(1)}, bf16[128,4096]{1,0:T(8,128)(2,1)}, u32[]{:S(2)}) copy-start(bf16[128,4096]{1,0:T(8,128)(2,1)} %param.5) | copy-start | bytes 3145732
  6.6 18.7 %copy-start.1 = (bf16[32,4096]{1,0:T(8,128)(2,1)S(1)}, bf16[32,4096]{1,0:T(8,128)(2,1)}, u32[]{:S(2)}) copy-start(bf16[32,4096]{1,0:T(8,128)(2,1)} %param.7) | copy-start | bytes 786436
  6.6 118.9 %all-to-all-start = ((bf16[64,32,4,128]{3,1,2,0:T(8,128)(2,1)}), bf16[64,32,4,128]{3,1,2,0:T(8,128)(2,1)S(1)}, u32[]{:S(2)}, u32[]{:S(2)}) async-start(bf16[64,32,4,128]{3,1,2,0:T(8,128)(2,1)} %copy.16), calls=%async_computation | async-start | bytes 4194304 | tf_op jit(solution)/shard_map/all_to_all | solution.py:168
  128.7 14.3 %all-to-all-start.1 = ((f32[4,256,5,32]{1,3,2,0:T(8,128)}), f32[4,256,5,32]{1,3,2,0:T(8,128)}, u32[]{:S(2)}, u32[]{:S(2)}) async-start(f32[4,256,5,32]{1,3,2,0:T(8,128)} %broadcast_in_dim.10), calls=%async_computation.1 | async-start | bytes 1310720 | tf_op jit(solution)/shard_map/all_to_all | solution.py:58
  180.0 6.1 %copy-start.2 = (s32[1,2048]{1,0:T(1,128)S(1)}, s32[1,2048]{1,0:T(1,128)}, u32[]{:S(2)}) copy-start(s32[1,2048]{1,0:T(1,128)} %param.9) | copy-start | bytes 24580
  181.0 21.6 %all-to-all-start.3 = ((f32[16,2,1,2048]{3,2,1,0:T(1,128)}), f32[16,2,1,2048]{3,2,1,0:T(1,128)S(1)}, u32[]{:S(2)}, u32[]{:S(2)}) async-start(f32[16,2,1,2048]{3,2,1,0:T(1,128)} %copy.22), calls=%async_computation.3 | async-start | bytes 524288 | tf_op jit(solution)/shard_map/all_to_all | solution.py:79
  186.0 18.6 %collective-permute-start.1 = (s32[2048]{0:T(1024)S(1)}, s32[2048]{0:T(1024)S(1)}, u32[]{:S(2)}, u32[]{:S(2)}) collective-permute-start(s32[2048]{0:T(1024)S(1)} %bitcast.363), channel_id=1, source_target_pairs={{0,256},{256,0},{1,257},{257,1},{2,258},{258,2},{3,259},{259,3},{4... | collective-permute-start | bytes 24584 | tf_op jit(solution)/shard_map/ppermute | solution.py:27
  202.7 3.1 %collective-permute-start = (f32[4096]{0:T(1024)S(1)}, f32[4096]{0:T(1024)S(1)}, u32[]{:S(2)}, u32[]{:S(2)}) collective-permute-start(f32[4096]{0:T(1024)S(1)} %bitcast.355), channel_id=1, source_target_pairs={{0,256},{256,0},{1,257},{257,1},{2,258},{258,2},{3,259},{259,3},{4... | collective-permute-start | bytes 49160 | tf_op jit(solution)/shard_map/ppermute | solution.py:27
  215.1 23.5 %all-to-all-start.5 = ((f32[64,3,128]{2,1,0:T(4,128)}), f32[64,3,128]{2,1,0:T(4,128)S(1)}, u32[]{:S(2)}, u32[]{:S(2)}) async-start(f32[64,3,128]{2,1,0:T(4,128)} %broadcast_in_dim.13), calls=%async_computation.5 | async-start | bytes 262144 | tf_op jit(solution)/shard_map/all_to_all | solution.py:58
  239.4 3.3 %copy-start.3 = (f32[1,128]{1,0:T(1,128)}, f32[1,128]{1,0:T(1,128)S(1)}, u32[]{:S(2)}) copy-start(f32[1,128]{1,0:T(1,128)S(1)} %get-tuple-element.21) | copy-start | bytes 1540
